TPU v7x, 32 devices: a whole 2x2x4 slice. The times are simulated.
32 devices in a mesh: dom: 4 (over y, x), dev: 8 (over z, core).
Axes of the slice: x: 2, y: 2, z: 4, core: 2. Of those that a mesh axis runs over, the one named last changes fastest.
Arguments:
- feats: bfloat16 [65536, 256], P(('dom', 'dev')), may hold values from -6 to 6
- w_self: bfloat16 [256, 256], replicated, may hold values from -0.375 to 0.375
- w_neigh: bfloat16 [256, 256], replicated, may hold values from -0.375 to 0.375
- cotangent: bfloat16 [65536, 256], P(('dom', 'dev')), may hold values from -8 to 8
- hub_rows: int32 [1024], P(('dom', 'dev')), may hold values from 0 to 2047
- send_rows: int32 [32, 32, 16], P(('dom', 'dev')), may hold values from 0 to 2047
- send_count: int32 [32, 32], P(('dom', 'dev')), may hold values from 1 to 16, as said below
- tile_dst: int32 [10240], P(('dom', 'dev')), may hold values from 0 to 15
- tile_src: int32 [10240], P(('dom', 'dev')), may hold values from 0 to 21
- tile_count: int32 [32], P(('dom', 'dev')), may hold values from 80 to 320, as said below
- tile_val: bfloat16 [10240, 128, 128], P(('dom', 'dev')), may hold values from -0.125 to 0.125
Outputs:
- out: bfloat16 [65536, 256], P(('dom', 'dev'))
- grad_x: bfloat16 [65536, 256], P(('dom', 'dev'))
- grad_ws: float32 [256, 256], replicated
- grad_wn: float32 [256, 256], replicated
Inputs may be any that keep to these rules, and one draw needn't show every extreme that they name: `send_count`: in every draw some peer receives 16 live slots from every device. `tile_count`: each device's count is 320, 160 or 80; some device has 320.
All inputs are finite; a program needn't handle non-finite values.
Results may differ from a plain program's by a relative error of at most 0.0057.
Values may be sent and summed in bfloat16 or wider, within the bound.
No kernel may reach another device: no remote copies, remote signals or barrier semaphores. Data moves between devices by JAX's collectives and lax.ppermute only.
A program may use at most 256 MiB of HBM per device.

v0:
```python
import jax
import jax.numpy as jnp
from jax import lax
from jax.sharding import PartitionSpec as P


def tile_forward(tile_val, picked, valid):
    terms = jnp.einsum("tij,tjd->tid", tile_val, picked, preferred_element_type=jnp.float32)
    return jnp.where(valid[:, None, None], terms, jnp.float32(0.0))


def tile_backward(tile_val, spread, valid):
    terms = jnp.einsum("tij,tid->tjd", tile_val, spread, preferred_element_type=jnp.float32)
    return jnp.where(valid[:, None, None], terms, jnp.float32(0.0))


def one_hot_table(index, count, dtype):
    columns = lax.broadcasted_iota(jnp.int32, (index.shape[0], count), 1)
    return (columns == index[:, None]).astype(dtype)


def select_blocks(table, blocks):
    flat = blocks.reshape(blocks.shape[0], -1)
    chosen = jnp.dot(table, flat, preferred_element_type=jnp.float32)
    return chosen.astype(jnp.bfloat16).reshape((table.shape[0],) + blocks.shape[1:])


def add_blocks(table, terms):
    flat = terms.reshape(terms.shape[0], -1)
    contract_rows = (((0,), (0,)), ((), ()))
    summed = lax.dot_general(
        table,
        flat,
        contract_rows,
        precision=lax.Precision.HIGHEST,
        preferred_element_type=jnp.float32,
    )
    return summed


def body(
    feats,
    w_self,
    w_neigh,
    cotangent,
    hub_rows,
    send_rows,
    send_count,
    tile_dst,
    tile_src,
    tile_count,
    tile_val,
):
    edge = tile_val.shape[1]
    rows, width = feats.shape
    peers = send_rows.shape[1]
    slots = send_rows.shape[2]
    own_blocks = rows // edge
    hub_table = lax.all_gather(feats[hub_rows], "dev", axis=0, tiled=True)
    live = lax.broadcasted_iota(jnp.int32, (peers, slots), 1) < send_count[0][:, None]
    outgoing = jnp.where(live[:, :, None], feats[send_rows[0]], jnp.zeros((), jnp.bfloat16))
    incoming = lax.all_to_all(outgoing, ("dom", "dev"), split_axis=0, concat_axis=0, tiled=True)
    source = jnp.concatenate([feats, incoming.reshape(peers * slots, width), hub_table], axis=0)
    source_blocks = source.shape[0] // edge
    valid = lax.broadcasted_iota(jnp.int32, (tile_val.shape[0],), 0) < tile_count[0]
    src_table = one_hot_table(tile_src, source_blocks, jnp.bfloat16)
    dst_table = one_hot_table(tile_dst, own_blocks, jnp.bfloat16)
    dst_sums = one_hot_table(tile_dst, own_blocks, jnp.float32)
    src_sums = one_hot_table(tile_src, source_blocks, jnp.float32)
    picked = select_blocks(src_table, source.reshape(source_blocks, edge, width))
    terms = tile_forward(tile_val, picked, valid)
    agg = add_blocks(dst_sums, terms).reshape(rows, width).astype(jnp.bfloat16)
    pre = jnp.dot(feats, w_self, preferred_element_type=jnp.float32) + jnp.dot(
        agg, w_neigh, preferred_element_type=jnp.float32
    )
    sig = jax.nn.sigmoid(pre)
    out = (pre * sig).astype(jnp.bfloat16)
    dpre = (cotangent.astype(jnp.float32) * sig * (1.0 + pre * (1.0 - sig))).astype(jnp.bfloat16)
    contract_rows = (((0,), (0,)), ((), ()))
    local_ws = lax.dot_general(feats, dpre, contract_rows, preferred_element_type=jnp.float32)
    local_wn = lax.dot_general(agg, dpre, contract_rows, preferred_element_type=jnp.float32)
    summed_ws, summed_wn = lax.psum((local_ws, local_wn), ("dom", "dev"))
    scale = 1.0 / jnp.sqrt(jnp.float32(rows * peers))
    grad_ws = summed_ws * scale
    grad_wn = summed_wn * scale
    contract_cols = (((1,), (1,)), ((), ()))
    dagg = lax.dot_general(dpre, w_neigh, contract_cols, preferred_element_type=jnp.float32).astype(
        jnp.bfloat16
    )
    spread = select_blocks(dst_table, dagg.reshape(own_blocks, edge, width))
    back_terms = tile_backward(tile_val, spread, valid)
    dsource = add_blocks(src_sums, back_terms).reshape(source_blocks * edge, width)
    own = dsource[:rows]
    returning = dsource[rows : rows + peers * slots].reshape(peers, slots, width)
    hub_part = dsource[rows + peers * slots :]
    returned = lax.all_to_all(
        returning.astype(jnp.bfloat16), ("dom", "dev"), split_axis=0, concat_axis=0, tiled=True
    ).astype(returning.dtype)
    returned = jnp.where(live[:, :, None], returned, jnp.float32(0.0))
    grad = lax.dot_general(dpre, w_self, contract_cols, preferred_element_type=jnp.float32) + own
    grad = grad.at[send_rows[0].reshape(-1)].add(returned.reshape(peers * slots, width))
    hub_back = lax.psum_scatter(
        hub_part.astype(jnp.bfloat16), "dev", scatter_dimension=0, tiled=True
    ).astype(jnp.float32)
    grad = grad.at[hub_rows].add(hub_back)
    return (out, grad.astype(jnp.bfloat16), grad_ws, grad_wn)


def solution(mesh):
    return jax.shard_map(
        body,
        mesh=mesh,
        in_specs=(
            P(("dom", "dev"), None),
            P(),
            P(),
            P(("dom", "dev"), None),
            P(("dom", "dev")),
            P(("dom", "dev"), None, None),
            P(("dom", "dev"), None),
            P(("dom", "dev")),
            P(("dom", "dev")),
            P(("dom", "dev")),
            P(("dom", "dev"), None, None),
        ),
        out_specs=(P(("dom", "dev"), None), P(("dom", "dev"), None), P(), P()),
        check_vma=False,
    )
```

profile of v0, /device:TPU:0, one launch (start us, length us, event | category | flops | bytes accessed | tf_op | source)
XLA Modules:
  0.0 419.8 jit_solution(2449749782824793038)
XLA Ops:
  8.1 0.8 iota_compare_fusion.6
  8.9 0.7 compare_select_fusion
  9.6 0.1 copy.20
  9.7 0.1 reshape.128
  9.8 2.9 gather_fusion
  12.7 0.8 broadcast_select_fusion
  13.5 7.3 %all-to-all-start = ((bf16[32,16,256]{2,1,0:T(8,128)(2,1)}), bf16[32,16,256]{2,1,0:T(8,128)(2,1)S(1)}, u32[]{:S(2)}, u32[]{:S(2)}) async-start(bf16[32,16,256]{2,1,0:T(8,128)(2,1)} %broadcast_select_fusion), calls=%async_computation | async-start | bytes 524288 | tf_op jit(solution)/shard_map/all_to_all | solution.py:62
  20.9 0.1 copy.25
  21.0 0.6 copy-done.12
  21.6 0.6 gather_fusion.1
  22.2 15.7 %all-gather = bf16[256,256]{1,0:T(8,128)(2,1)S(1)} all-gather(bf16[32,256]{1,0:T(8,128)(2,1)S(1)} %gather_fusion.1), channel_id=2, replica_groups=mesh['dom'=4,'dev'=8] {'dev'}, dimensions={0}, use_global_device_ids=true | all-gather | bytes 147456 | tf_op jit(solution)/shard_map/all_gather | solution.py:59
  38.6 0.1 reshape_squeeze.3
  38.6 0.6 compare_select_fusion.1
  39.3 1.8 fusion.8
  41.0 1.2 pad_maximum_fusion
  42.2 2.5 reshape_reshape.6
  44.8 10.0 %convolution_convert_fusion.1 = bf16[320,32768]{1,0:T(8,128)(2,1)} fusion(bf16[22,32768]{1,0:T(8,128)(2,1)S(1)} %reshape_reshape.6, s32[320]{0:T(512)S(1)} %copy-done.5), kind=kOutput, calls=%fused_computation.5 | convolution fusion | flops 471866240 | bytes 22414592 | tf_op jit(solution)/shard_map/dot_general | solution.py:24
  54.8 19.3 %copy.32 = bf16[40,8,128,256]{3,2,1,0:T(8,128)(2,1)} copy(bf16[40,8,128,256]{3,1,2,0:T(8,128)(2,1)} %bitcast.53) | data formatting | bytes 41943040
  74.1 31.5 %select_bitcast_fusion.1 = f32[320,128,256]{1,2,0:T(8,128)} fusion(pred[320]{0:T(512)(128)(4,1)S(1)} %iota_compare_fusion.7, bf16[320,128,256]{2,1,0:T(8,128)(2,1)} %bitcast.52, bf16[320,128,128]{2,1,0:T(8,128)(2,1)} %param.21), kind=kOutput, calls=%fused_computation.7 | convolution fusion | flops 2694840320 | bytes 73400640 | tf_op jit(solution)/shard_map/tij,tjd->tid/dot_general | solution.py:8
  105.6 41.9 %copy.33 = f32[40,8,128,256]{3,1,2,0:T(8,128)} copy(f32[40,8,128,256]{2,3,1,0:T(8,128)} %bitcast.48) | data formatting | bytes 83886080
  147.6 18.6 %convolution_convert_fusion.2 = bf16[16,32768]{1,0:T(8,128)(2,1)S(1)} fusion(f32[320,32768]{1,0:T(8,128)} %bitcast.50, s32[320]{0:T(512)S(1)} %copy-done.7), kind=kOutput, calls=%fused_computation.8 | convolution fusion | flops 2013795328 | bytes 42992896 | tf_op jit(solution)/shard_map/dot_general | solution.py:31
  166.2 1.3 convert_element_type.47
  167.5 4.5 %multiply_convert_fusion = (bf16[2048,256]{1,0:T(8,128)(2,1)S(1)}, bf16[2048,256]{1,0:T(8,128)(2,1)}) fusion(bf16[2048,256]{1,0:T(8,128)(2,1)} %param.14, f32[2048,256]{1,0:T(8,128)} %fusion.8, bf16[2048,256]{1,0:T(8,128)(2,1)} %convert_element_type.47, bf16[256,256]{1,0:T(8,128)(2,1)S(1)} %copy-done), kind=kOutput, calls=%fused_computation.12 | convolution fusion | flops 275251200 | bytes 6422528 | tf_op jit(solution)/shard_map/dot_general | solution.py:73
  172.0 1.2 fusion.9
  173.2 1.2 convolution_bitcast_fusion
  174.4 0.5 convolution_convert_fusion.3
  174.9 0.5 reshape_reshape.7
  175.4 9.9 %convolution_convert_fusion = bf16[320,32768]{1,0:T(8,128)(2,1)} fusion(bf16[16,32768]{1,0:T(8,128)(2,1)S(1)} %reshape_reshape.7, s32[320]{0:T(512)S(1)} %copy-done.7), kind=kOutput, calls=%fused_computation.4 | convolution fusion | flops 346035200 | bytes 22021376 | tf_op jit(solution)/shard_map/dot_general | solution.py:24
  185.3 19.4 %copy.34 = bf16[40,8,128,256]{3,2,1,0:T(8,128)(2,1)} copy(bf16[40,8,128,256]{3,1,2,0:T(8,128)(2,1)} %bitcast.54) | data formatting | bytes 41943040
  204.7 27.8 %select_bitcast_fusion = f32[320,128,256]{1,2,0:T(8,128)} fusion(pred[320]{0:T(512)(128)(4,1)S(1)} %iota_compare_fusion.7, bf16[320,128,256]{2,1,0:T(8,128)(2,1)} %bitcast.51, bf16[320,128,128]{2,1,0:T(8,128)(2,1)} %param.21), kind=kOutput, calls=%fused_computation.6 | convolution fusion | flops 2694840320 | bytes 73400640 | tf_op jit(solution)/shard_map/tij,tid->tjd/dot_general | solution.py:13
  232.5 42.0 %copy.35 = f32[40,8,128,256]{3,1,2,0:T(8,128)} copy(f32[40,8,128,256]{2,3,1,0:T(8,128)} %bitcast.47) | data formatting | bytes 83886080
  274.5 19.1 %fusion.7 = (bf16[22,32768]{1,0:T(8,128)(2,1)S(1)}, f32[22,32768]{1,0:T(8,128)S(1)}) fusion(f32[320,32768]{1,0:T(8,128)} %bitcast.49, s32[320]{0:T(512)S(1)} %copy-done.6), kind=kOutput, calls=%fused_computation.37 | convolution fusion | flops 2768968704 | bytes 46269696 | tf_op jit(solution)/shard_map/dot_general | solution.py:31
  293.6 0.1 slice.25
  293.7 0.1 slice.26
  293.9 0.1 slice.24
  294.0 1.5 slice.17
  295.5 0.9 convert_element_type.53
  296.4 4.2 all-to-all-start.1
  300.6 0.7 convert_element_type.55
  301.4 2.1 convolution_add_fusion
  303.6 98.9 %all-reduce.3.cloned.1.call-done = (f32[256,256]{0,1:T(8,128)}, f32[256,256]{0,1:T(8,128)}) async-done(((f32[256,256]{0,1:T(8,128)}, f32[256,256]{0,1:T(8,128)}), (f32[256,256]{0,1:T(8,128)}, f32[256,256]{0,1:T(8,128)})) %all-reduce.3.cloned.1.call-update) | async-done | bytes 524304 | tf_op jit(solution)/shard_map/psum | solution.py:82
  402.4 1.1 broadcast_multiply_fusion
  403.5 0.8 copy.27
  404.4 0.8 copy.28
  405.2 0.1 convert_select_fusion
  405.4 4.1 scatter_fusion
  409.5 1.7 scatter_custom_fusion.1
  411.2 1.1 convert_element_type.57
  (38 shorter events, 0.2 us)
Async XLA Ops:
  8.0 159.5 %copy-start = (bf16[256,256]{1,0:T(8,128)(2,1)S(1)}, bf16[256,256]{1,0:T(8,128)(2,1)}, u32[]{:S(2)}) copy-start(bf16[256,256]{1,0:T(8,128)(2,1)} %param.13) | copy-start | bytes 393220
  8.0 12.9 %copy-start.10 = (s32[1,32,16]{1,2,0:T(8,128)S(1)}, s32[1,32,16]{1,2,0:T(8,128)}, u32[]{:S(2)}) copy-start(s32[1,32,16]{1,2,0:T(8,128)} %param.16) | copy-start | bytes 6148
  8.0 13.6 %copy-start.2 = (bf16[2048,256]{1,0:T(8,128)(2,1)S(1)}, bf16[2048,256]{1,0:T(8,128)(2,1)}, u32[]{:S(2)}) copy-start(bf16[2048,256]{1,0:T(8,128)(2,1)} %param.11) | copy-start | bytes 3145732
  8.0 12.9 %copy-start.13 = (s32[32]{0:T(128)S(1)}, s32[32]{0:T(128)}, u32[]{:S(2)}) copy-start(s32[32]{0:T(128)} %param.15) | copy-start | bytes 388
  8.0 31.2 %copy-start.4 = (bf16[256,256]{1,0:T(8,128)(2,1)S(1)}, bf16[256,256]{1,0:T(8,128)(2,1)}, u32[]{:S(2)}) copy-start(bf16[256,256]{1,0:T(8,128)(2,1)} %param.12) | copy-start | bytes 393220
  8.9 12.7 %copy-start.8 = (pred[32,16]{1,0:T(8,128)(4,1)}, pred[32,16]{1,0:T(8,128)(4,1)S(1)}, u32[]{:S(2)}) copy-start(pred[32,16]{1,0:T(8,128)(4,1)S(1)} %iota_compare_fusion.6) | copy-start | bytes 1540
  13.5 27.5 %all-to-all-start = ((bf16[32,16,256]{2,1,0:T(8,128)(2,1)}), bf16[32,16,256]{2,1,0:T(8,128)(2,1)S(1)}, u32[]{:S(2)}, u32[]{:S(2)}) async-start(bf16[32,16,256]{2,1,0:T(8,128)(2,1)} %broadcast_select_fusion), calls=%async_computation | async-start | bytes 524288 | tf_op jit(solution)/shard_map/all_to_all | solution.py:62
  20.8 381.6 %all-reduce.3.cloned.1.call-start = ((), (), s32[]{:S(2)}) async-start(), calls=%async_computation.4 | async-start | bytes 1048576 | tf_op jit(solution)/shard_map/psum | solution.py:82
  21.0 0.6 copy-start.12
  41.0 3.8 copy-start.5
  105.6 41.9 %copy-start.7 = (s32[320]{0:T(512)S(1)}, s32[320]{0:T(512)}, u32[]{:S(2)}) copy-start(s32[320]{0:T(512)} %param.18) | copy-start | bytes 3844
  167.5 4.5 %copy-start.3 = (bf16[2048,256]{1,0:T(8,128)(2,1)S(1)}, bf16[2048,256]{1,0:T(8,128)(2,1)}, u32[]{:S(2)}) copy-start(bf16[2048,256]{1,0:T(8,128)(2,1)} %convert_element_type.47) | copy-start | bytes 3145732
  232.5 42.0 %copy-start.6 = (s32[320]{0:T(512)S(1)}, s32[320]{0:T(512)}, u32[]{:S(2)}) copy-start(s32[320]{0:T(512)} %param.19) | copy-start | bytes 3844
  296.4 108.8 %all-to-all-start.1 = ((bf16[32,16,256]{2,1,0:T(8,128)(2,1)}), bf16[32,16,256]{2,1,0:T(8,128)(2,1)S(1)}, u32[]{:S(2)}, u32[]{:S(2)}) async-start(bf16[32,16,256]{2,1,0:T(8,128)(2,1)} %convert_element_type.53), calls=%async_computation.1 | async-start | bytes 524288 | tf_op jit(solution)/shard_map/all_to_all | solution.py:96
  300.6 108.9 %reduce-scatter.2.cloned.1.call-start = ((), (), s32[]{:S(2)}) async-start(), calls=%async_computation.3 | async-start | bytes 147456 | tf_op jit(solution)/shard_map/reduce_scatter | solution.py:102
  301.4 103.8 %copy-start.9 = (pred[32,16]{1,0:T(8,128)(4,1)S(1)}, pred[32,16]{1,0:T(8,128)(4,1)}, u32[]{:S(2)}) copy-start(pred[32,16]{1,0:T(8,128)(4,1)} %copy-done.8) | copy-start | bytes 1540
  301.4 103.9 %copy-start.11 = (s32[512,1]{0,1:T(1,128)S(1)}, s32[512,1]{0,1:T(1,128)}, u32[]{:S(2)}) copy-start(s32[512,1]{0,1:T(1,128)} %compare_select_fusion.1) | copy-start | bytes 6148
  405.3 7.0 %copy-start.1 = (bf16[256,256]{1,0:T(8,128)(2,1)S(1)}, bf16[256,256]{1,0:T(8,128)(2,1)}, u32[]{:S(2)}) copy-start(bf16[256,256]{1,0:T(8,128)(2,1)} %param.13) | copy-start | bytes 393220
Sparse Core Ops, SparseCore 0:
  274.6 127.7 all-reduce.2
Sparse Core Ops, SparseCore 1:
  303.3 31.4 reduce-scatter.1
where the time goes:
time: 422 us; the launch traced here: 420 us
  local copies, waits for them, and re-layouts  137 us (32%)
  matrix products  128 us (30%)
  waiting for transfers between devices  99 us (23%)
  between operations  16.4 us (4%)
  blocking collectives  15.7 us (4%)
  other arithmetic  12.3 us (3%)
  starting transfers between devices  11.5 us (3%)
    unnamed x35, local copies, waits for them, and re-layouts  125 us
    psum x1, waiting for transfers between devices, body(): summed_ws, summed_wn = lax.psum((local_ws, local_wn), ('dom', 'dev'))  98.9 us
    dot_general x2, matrix products, add_blocks(): lax.dot_general(table, flat, contract_rows, precision=lax.Precision.HIGHE...  37.8 us
    dot_general x1, matrix products, tile_forward(): jnp.einsum('tij,tjd->tid', tile_val, picked, preferred_element_type=jnp.f...  31.5 us
    dot_general x1, matrix products, tile_backward(): jnp.einsum('tij,tid->tjd', tile_val, spread, preferred_element_type=jnp.f...  27.8 us
    dot_general x2, matrix products, select_blocks(): chosen = jnp.dot(table, flat, preferred_element_type=jnp.float32)  19.9 us
    all_gather x1, blocking collectives, body(): hub_table = lax.all_gather(feats[hub_rows], 'dev', axis=0, tiled=True)  15.7 us
  transfers between devices with their start and end apart: 4, of which 1 were waited for; matrix products, arithmetic and copies ran while one was open for 8% of the time, Pallas kernels for 0%

commit v1 on v0

v1 whole, which is shorter than its diff:
```python
import functools

import jax
import jax.numpy as jnp
from jax import lax
from jax.experimental import pallas as pl
from jax.experimental.pallas import tpu as pltpu
from jax.sharding import PartitionSpec as P


def _tile_block(tiles):
    for size in (16, 8, 4, 2, 1):
        if tiles % size == 0:
            return size
    return 1


def _agg_kernel(src_ref, dst_ref, cnt_ref, val_ref, source_ref, out_ref, acc_ref, *, tb, edge, last_src):
    i = pl.program_id(0)

    @pl.when(i == 0)
    def _():
        acc_ref[...] = jnp.zeros_like(acc_ref)

    count = cnt_ref[0]
    last_dst = acc_ref.shape[0] // edge - 1

    def body(k, carry):
        t = i * tb + k

        @pl.when(t < count)
        def _():
            s = jnp.clip(src_ref[t], 0, last_src)
            d = jnp.clip(dst_ref[t], 0, last_dst)
            x = source_ref[pl.ds(pl.multiple_of(s * edge, edge), edge), :]
            rows = pl.ds(pl.multiple_of(d * edge, edge), edge)
            acc_ref[rows, :] += jnp.dot(val_ref[k], x, preferred_element_type=jnp.float32)

        return carry

    lax.fori_loop(0, tb, body, 0, unroll=True)

    @pl.when(i == pl.num_programs(0) - 1)
    def _():
        out_ref[...] = acc_ref[...].astype(out_ref.dtype)


def _back_kernel(src_ref, dst_ref, cnt_ref, val_ref, dagg_ref, out_ref, *, tb, edge, last_dst):
    i = pl.program_id(0)

    @pl.when(i == 0)
    def _():
        out_ref[...] = jnp.zeros_like(out_ref)

    count = cnt_ref[0]
    last_src = out_ref.shape[0] // edge - 1

    def body(k, carry):
        t = i * tb + k

        @pl.when(t < count)
        def _():
            s = jnp.clip(src_ref[t], 0, last_src)
            d = jnp.clip(dst_ref[t], 0, last_dst)
            y = dagg_ref[pl.ds(pl.multiple_of(d * edge, edge), edge), :]
            rows = pl.ds(pl.multiple_of(s * edge, edge), edge)
            term = lax.dot_general(
                val_ref[k], y, (((0,), (0,)), ((), ())), preferred_element_type=jnp.float32
            )
            out_ref[rows, :] += term

        return carry

    lax.fori_loop(0, tb, body, 0, unroll=True)


def _val_map(tb):
    def index_map(i, src, dst, cnt):
        last = jnp.maximum(cnt[0] - 1, 0) // tb
        return (jnp.minimum(i, last), 0, 0)

    return index_map


def tile_aggregate(tile_src, tile_dst, tile_count, tile_val, source, rows):
    tiles, edge, _ = tile_val.shape
    width = source.shape[1]
    tb = _tile_block(tiles)
    kernel = functools.partial(_agg_kernel, tb=tb, edge=edge, last_src=source.shape[0] // edge - 1)
    return pl.pallas_call(
        kernel,
        out_shape=jax.ShapeDtypeStruct((rows, width), jnp.bfloat16),
        grid_spec=pltpu.PrefetchScalarGridSpec(
            num_scalar_prefetch=3,
            grid=(tiles // tb,),
            in_specs=[
                pl.BlockSpec((tb, edge, edge), _val_map(tb)),
                pl.BlockSpec(source.shape, lambda i, s, d, c: (0, 0)),
            ],
            out_specs=pl.BlockSpec((rows, width), lambda i, s, d, c: (0, 0)),
            scratch_shapes=[pltpu.VMEM((rows, width), jnp.float32)],
        ),
        compiler_params=pltpu.CompilerParams(dimension_semantics=("arbitrary",)),
    )(tile_src, tile_dst, tile_count, tile_val, source)


def tile_backward(tile_src, tile_dst, tile_count, tile_val, dagg, src_rows):
    tiles, edge, _ = tile_val.shape
    width = dagg.shape[1]
    tb = _tile_block(tiles)
    kernel = functools.partial(_back_kernel, tb=tb, edge=edge, last_dst=dagg.shape[0] // edge - 1)
    return pl.pallas_call(
        kernel,
        out_shape=jax.ShapeDtypeStruct((src_rows, width), jnp.float32),
        grid_spec=pltpu.PrefetchScalarGridSpec(
            num_scalar_prefetch=3,
            grid=(tiles // tb,),
            in_specs=[
                pl.BlockSpec((tb, edge, edge), _val_map(tb)),
                pl.BlockSpec(dagg.shape, lambda i, s, d, c: (0, 0)),
            ],
            out_specs=pl.BlockSpec((src_rows, width), lambda i, s, d, c: (0, 0)),
        ),
        compiler_params=pltpu.CompilerParams(dimension_semantics=("arbitrary",)),
    )(tile_src, tile_dst, tile_count, tile_val, dagg)


def body(
    feats,
    w_self,
    w_neigh,
    cotangent,
    hub_rows,
    send_rows,
    send_count,
    tile_dst,
    tile_src,
    tile_count,
    tile_val,
):
    edge = tile_val.shape[1]
    rows, width = feats.shape
    peers = send_rows.shape[1]
    slots = send_rows.shape[2]
    group = lax.axis_size("dev")
    hubs_dev = hub_rows.shape[0]

    own_hubs = feats[hub_rows]
    hub_out = jnp.broadcast_to(own_hubs[None], (group, hubs_dev, width))
    hub_table = lax.all_to_all(hub_out, "dev", split_axis=0, concat_axis=0, tiled=True)
    hub_table = hub_table.reshape(group * hubs_dev, width)

    live = lax.broadcasted_iota(jnp.int32, (peers, slots), 1) < send_count[0][:, None]
    outgoing = jnp.where(live[:, :, None], feats[send_rows[0]], jnp.zeros((), jnp.bfloat16))
    incoming = lax.all_to_all(outgoing, ("dom", "dev"), split_axis=0, concat_axis=0, tiled=True)
    source = jnp.concatenate([feats, incoming.reshape(peers * slots, width), hub_table], axis=0)

    agg = tile_aggregate(tile_src, tile_dst, tile_count, tile_val, source, rows)

    pre = jnp.dot(feats, w_self, preferred_element_type=jnp.float32) + jnp.dot(
        agg, w_neigh, preferred_element_type=jnp.float32
    )
    sig = jax.nn.sigmoid(pre)
    out = (pre * sig).astype(jnp.bfloat16)
    dpre = (cotangent.astype(jnp.float32) * sig * (1.0 + pre * (1.0 - sig))).astype(jnp.bfloat16)

    contract_rows = (((0,), (0,)), ((), ()))
    local_ws = lax.dot_general(feats, dpre, contract_rows, preferred_element_type=jnp.float32)
    local_wn = lax.dot_general(agg, dpre, contract_rows, preferred_element_type=jnp.float32)
    partial = jnp.concatenate([local_ws, local_wn], axis=0)
    parts = partial.reshape(peers, -1, width)
    gathered = lax.all_to_all(parts, ("dom", "dev"), split_axis=0, concat_axis=0, tiled=True)
    piece = jnp.sum(gathered, axis=0)
    spread_piece = jnp.broadcast_to(piece[None], (peers,) + piece.shape)
    summed = lax.all_to_all(spread_piece, ("dom", "dev"), split_axis=0, concat_axis=0, tiled=True)
    summed = summed.reshape(partial.shape)
    scale = 1.0 / jnp.sqrt(jnp.float32(rows * peers))
    grad_ws = summed[: w_self.shape[0]] * scale
    grad_wn = summed[w_self.shape[0] :] * scale

    contract_cols = (((1,), (1,)), ((), ()))
    dagg = lax.dot_general(dpre, w_neigh, contract_cols, preferred_element_type=jnp.float32).astype(
        jnp.bfloat16
    )
    dsource = tile_backward(tile_src, tile_dst, tile_count, tile_val, dagg, source.shape[0])
    own = dsource[:rows]
    returning = dsource[rows : rows + peers * slots].reshape(peers, slots, width)
    hub_part = dsource[rows + peers * slots :]
    returned = lax.all_to_all(
        returning.astype(jnp.bfloat16), ("dom", "dev"), split_axis=0, concat_axis=0, tiled=True
    ).astype(jnp.float32)
    returned = jnp.where(live[:, :, None], returned, jnp.float32(0.0))
    hub_back = lax.all_to_all(
        hub_part.astype(jnp.bfloat16).reshape(group, hubs_dev, width),
        "dev",
        split_axis=0,
        concat_axis=0,
        tiled=True,
    )
    hub_back = jnp.sum(hub_back.astype(jnp.float32), axis=0)
    grad = lax.dot_general(dpre, w_self, contract_cols, preferred_element_type=jnp.float32) + own
    grad = grad.at[send_rows[0].reshape(-1)].add(returned.reshape(peers * slots, width))
    grad = grad.at[hub_rows].add(hub_back)
    return (out, grad.astype(jnp.bfloat16), grad_ws, grad_wn)


def solution(mesh):
    return jax.shard_map(
        body,
        mesh=mesh,
        in_specs=(
            P(("dom", "dev"), None),
            P(),
            P(),
            P(("dom", "dev"), None),
            P(("dom", "dev")),
            P(("dom", "dev"), None, None),
            P(("dom", "dev"), None),
            P(("dom", "dev")),
            P(("dom", "dev")),
            P(("dom", "dev")),
            P(("dom", "dev"), None, None),
        ),
        out_specs=(P(("dom", "dev"), None), P(("dom", "dev"), None), P(), P()),
        check_vma=False,
    )
```

time: 422 us -> 229 us (0.54)
  local copies, waits for them, and re-layouts: 137 us -> 10.2 us
  matrix products: 128 us -> 10.9 us
  Pallas kernels: 0 us -> 66.4 us
  starting transfers between devices: 11.5 us -> 76.3 us
  waiting for transfers between devices: 99 us -> 46.9 us
  blocking collectives: 15.7 us -> 0 us
  between operations: 16.4 us -> 1.47 us
    unnamed x35 -> x17, local copies, waits for them, and re-layouts: 125 us -> 1.23 us
    dot_general x6 -> x0, matrix products: 117 us -> none  [the longest x2 37.8 us: add_blocks(): lax.dot_general(table, flat, contract_rows, precision=lax.Precision.HIGHE...]
    psum x1 -> x0, waiting for transfers between devices: 98.9 us -> none  [body(): summed_ws, summed_wn = lax.psum((local_ws, local_wn), ('dom', 'dev'))]
    all_to_all x0 -> x4, starting transfers between devices: none -> 69 us  [the longest x1 55.8 us: body(): lax.all_to_all(hub_part.astype(jnp.bfloat16).reshape(group, hubs_dev, wid...]
    pallas_call x0 -> x2, Pallas kernels: none -> 66.4 us  [the longest x1 37.1 us: tile_backward(): pl.pallas_call(kernel, out_shape=jax.ShapeDtypeStruct((src_rows, width),...]
    all_to_all x0 -> x4, waiting for transfers between devices: none -> 28.6 us  [the longest x1 14.7 us: body(): lax.all_to_all(parts, ('dom', 'dev'), split_axis=0, concat_axis=0, tiled=...]
    all_gather x1 -> x0, blocking collectives: 15.7 us -> none  [body(): hub_table = lax.all_gather(feats[hub_rows], 'dev', axis=0, tiled=True)]
    all_to_all x1, waiting for transfers between devices: 0.01 us -> 10.3 us  [body(): lax.all_to_all(returning.astype(jnp.bfloat16), ('dom', 'dev'), split_axis...]
  transfers between devices with their start and end apart: 4 -> 6, of which waited for: 1 -> 6; matrix products, arithmetic and copies ran while one was open for 8% -> 9% of each run, Pallas kernels for 0% -> 0%
where the time goes in v1:
time: 229 us; the launch traced here: 228 us
  starting transfers between devices  76.3 us (33%)
  Pallas kernels  66.4 us (29%)
  waiting for transfers between devices  46.9 us (20%)
  other arithmetic  15.8 us (7%)
  matrix products  10.9 us (5%)
  local copies, waits for them, and re-layouts  10.2 us (4%)
    all_to_all x1, starting transfers between devices, body(): lax.all_to_all(hub_part.astype(jnp.bfloat16).reshape(group, hubs_dev, wid...  55.8 us
    pallas_call x1, Pallas kernels, tile_backward(): pl.pallas_call(kernel, out_shape=jax.ShapeDtypeStruct((src_rows, width),...  37.1 us
    pallas_call x1, Pallas kernels, tile_aggregate(): pl.pallas_call(kernel, out_shape=jax.ShapeDtypeStruct((rows, width), jnp....  29.3 us
    all_to_all x1, waiting for transfers between devices, body(): lax.all_to_all(parts, ('dom', 'dev'), split_axis=0, concat_axis=0, tiled=...  14.7 us
    all_to_all x1, waiting for transfers between devices, body(): lax.all_to_all(returning.astype(jnp.bfloat16), ('dom', 'dev'), split_axis...  10.3 us
    all_to_all x1, waiting for transfers between devices, body(): lax.all_to_all(outgoing, ('dom', 'dev'), split_axis=0, concat_axis=0, til...  7.95 us
    all_to_all x1, waiting for transfers between devices, body(): lax.all_to_all(spread_piece, ('dom', 'dev'), split_axis=0, concat_axis=0,...  7.06 us
    all_to_all x1, starting transfers between devices, body(): lax.all_to_all(hub_out, 'dev', split_axis=0, concat_axis=0, tiled=True)  6.33 us
  transfers between devices with their start and end apart: 6, of which 6 were waited for; matrix products, arithmetic and copies ran while one was open for 9% of the time, Pallas kernels for 0%

profile of v1, /device:TPU:0, one launch (start us, length us, event | category | flops | bytes accessed | tf_op | source)
XLA Modules:
  0.0 227.9 jit_solution(1398589068874471391)
XLA Ops:
  0.6 0.0 copy-start
  0.6 0.0 copy-start.1
  0.7 0.0 copy-start.6
  0.7 0.8 compare_select_fusion.2
  1.4 2.0 gather_fusion.1
  3.4 0.7 broadcast_in_dim.45
  4.1 6.3 %all-to-all-start.1 = ((bf16[8,32,256]{2,1,0:T(8,128)(2,1)}), bf16[8,32,256]{2,1,0:T(8,128)(2,1)S(1)}, u32[]{:S(2)}, u32[]{:S(2)}) async-start(bf16[8,32,256]{2,1,0:T(8,128)(2,1)} %broadcast_in_dim.45), calls=%async_computation.1 | async-start | bytes 262144 | tf_op jit(solution)/shard_map/all_to_all | solution.py:150
  10.4 0.7 iota_compare_fusion
  11.1 0.7 compare_select_fusion
  11.8 0.1 copy.15
  11.9 0.1 reshape.119
  12.0 2.9 %gather_fusion = bf16[512,256]{1,0:T(8,128)(2,1)S(1)} fusion(bf16[2048,256]{1,0:T(8,128)(2,1)} %param.11, s32[1024]{0:T(1024)S(1)} %pad_clamp_fusion.1), kind=kCustom, calls=%fused_computation | custom fusion | bytes 526336 | tf_op jit(solution)/shard_map/gather | solution.py:154
  14.9 0.8 broadcast_select_fusion
  15.8 1.4 all-to-all-done.1
  17.2 4.7 %all-to-all-start = ((bf16[32,16,256]{2,1,0:T(8,128)(2,1)}), bf16[32,16,256]{2,1,0:T(8,128)(2,1)S(1)}, u32[]{:S(2)}, u32[]{:S(2)}) async-start(bf16[32,16,256]{2,1,0:T(8,128)(2,1)} %broadcast_select_fusion), calls=%async_computation | async-start | bytes 524288 | tf_op jit(solution)/shard_map/all_to_all | solution.py:155
  22.5 1.8 fusion
  24.3 8.0 %all-to-all-done = bf16[32,16,256]{2,1,0:T(8,128)(2,1)S(1)} async-done(((bf16[32,16,256]{2,1,0:T(8,128)(2,1)}), bf16[32,16,256]{2,1,0:T(8,128)(2,1)S(1)}, u32[]{:S(2)}, u32[]{:S(2)}) %all-to-all-start) | async-done | bytes 262176 | tf_op jit(solution)/shard_map/all_to_all | solution.py:155
  32.2 1.2 pad_maximum_fusion.source_ref
  33.4 29.3 %shard_map.138 = bf16[2048,256]{1,0:T(8,128)(2,1)} custom-call(s32[320]{0:T(512)} %src_ref.3, s32[320]{0:T(512)} %dst_ref.3, s32[1]{0:T(128)S(6)} %copy.19.cnt_ref, bf16[320,128,128]{2,1,0:T(8,128)(2,1)} %val_ref.3, bf16[2816,256]{1,0:T(8,128)(2,1)} %pad_maximum_fusion.source_ref), custom_call_target="tpu_custom_call" | custom-call | tf_op jit(solution)/shard_map/pallas_call | solution.py:90
  62.8 4.5 %multiply_convert_fusion = (bf16[2048,256]{1,0:T(8,128)(2,1)S(1)}, bf16[2048,256]{1,0:T(8,128)(2,1)}) fusion(bf16[2048,256]{1,0:T(8,128)(2,1)} %param.14, f32[2048,256]{1,0:T(8,128)} %fusion, bf16[2048,256]{1,0:T(8,128)(2,1)} %shard_map.138, bf16[256,256]{1,0:T(8,128)(2,1)S(1)} %copy-done), kind=kOutput, calls=%fused_computation.7 | convolution fusion | flops 275251200 | bytes 6422528 | tf_op jit(solution)/shard_map/dot_general | solution.py:160
  67.3 0.5 fusion.1
  67.7 1.4 convolution_convert_fusion.dagg_ref
  69.2 37.1 %shard_map.139 = f32[2816,256]{1,0:T(8,128)} custom-call(s32[320]{0:T(512)} %src_ref.3, s32[320]{0:T(512)} %dst_ref.3, s32[1]{0:T(128)S(6)} %copy.19.cnt_ref, bf16[320,128,128]{2,1,0:T(8,128)(2,1)} %val_ref.3, bf16[2048,256]{1,0:T(8,128)(2,1)} %convolution_convert_fusion.dagg_ref), custom_call_target="tpu_custom_call" | custom-call | tf_op jit(solution)/shard_map/pallas_call | solution.py:112
  106.3 2.0 convert.4
  108.3 1.1 copy-done.3
  109.4 0.7 slice.30
  110.0 55.8 %all-to-all-start.3 = ((bf16[8,32,256]{2,1,0:T(8,128)(2,1)}), bf16[8,32,256]{2,1,0:T(8,128)(2,1)S(1)}, u32[]{:S(2)}, u32[]{:S(2)}) async-start(bf16[8,32,256]{2,1,0:T(8,128)(2,1)} %bitcast.8), calls=%async_computation.3 | async-start | bytes 262144 | tf_op jit(solution)/shard_map/all_to_all | solution.py:193
  165.8 0.5 convolution_bitcast_fusion
  166.3 0.8 pad_maximum_fusion.1
  167.2 5.4 %all-to-all-done.3 = bf16[8,32,256]{2,1,0:T(8,128)(2,1)S(1)} async-done(((bf16[8,32,256]{2,1,0:T(8,128)(2,1)}), bf16[8,32,256]{2,1,0:T(8,128)(2,1)S(1)}, u32[]{:S(2)}, u32[]{:S(2)}) %all-to-all-start.3) | async-done | bytes 131104 | tf_op jit(solution)/shard_map/all_to_all | solution.py:193
  172.6 3.6 %all-to-all-start.4 = ((f32[32,16,256]{2,1,0:T(8,128)}), f32[32,16,256]{2,1,0:T(8,128)S(1)}, u32[]{:S(2)}, u32[]{:S(2)}) async-start(f32[32,16,256]{2,1,0:T(8,128)} %bitcast.10), calls=%async_computation.4 | async-start | bytes 1048576 | tf_op jit(solution)/shard_map/all_to_all | solution.py:172
  176.2 1.7 slice.29
  177.9 14.7 %all-to-all-done.4 = f32[32,16,256]{2,1,0:T(8,128)S(1)} async-done(((f32[32,16,256]{2,1,0:T(8,128)}), f32[32,16,256]{2,1,0:T(8,128)S(1)}, u32[]{:S(2)}, u32[]{:S(2)}) %all-to-all-start.4) | async-done | bytes 524320 | tf_op jit(solution)/shard_map/all_to_all | solution.py:172
  192.6 2.6 %all-to-all-start.2 = ((bf16[32,16,256]{2,1,0:T(8,128)(2,1)}), bf16[32,16,256]{2,1,0:T(8,128)(2,1)S(1)}, u32[]{:S(2)}, u32[]{:S(2)}) async-start(bf16[32,16,256]{2,1,0:T(8,128)(2,1)} %bitcast.6), calls=%async_computation.2 | async-start | bytes 524288 | tf_op jit(solution)/shard_map/all_to_all | solution.py:189
  195.2 10.3 %all-to-all-done.2 = bf16[32,16,256]{2,1,0:T(8,128)(2,1)S(1)} async-done(((bf16[32,16,256]{2,1,0:T(8,128)(2,1)}), bf16[32,16,256]{2,1,0:T(8,128)(2,1)S(1)}, u32[]{:S(2)}, u32[]{:S(2)}) %all-to-all-start.2) | async-done | bytes 262176 | tf_op jit(solution)/shard_map/all_to_all | solution.py:189
  205.5 0.9 broadcast_in_dim.47
  206.4 0.0 copy-done.4
  206.4 3.3 %all-to-all-start.5 = ((f32[32,16,256]{2,1,0:T(8,128)}), f32[32,16,256]{2,1,0:T(8,128)}, u32[]{:S(2)}, u32[]{:S(2)}) async-start(f32[32,16,256]{2,1,0:T(8,128)} %broadcast_in_dim.47), calls=%async_computation.5 | async-start | bytes 1048576 | tf_op jit(solution)/shard_map/all_to_all | solution.py:175
  209.8 0.1 copy.16
  209.8 0.1 reshape_squeeze.3
  209.9 0.0 copy-start.5
  209.9 2.2 convolution_add_fusion
  212.2 0.1 convert_select_fusion
  212.3 4.1 %scatter_fusion = f32[2048,256]{1,0:T(8,128)S(1)} fusion(f32[2048,256]{1,0:T(8,128)S(1)} %convolution_add_fusion, s32[512]{0:T(512)S(1)} %bitcast.35, f32[512,256]{1,0:T(8,128)S(1)} %bitcast.29), kind=kCustom, calls=%fused_computation.2 | custom fusion | flops 131072 | bytes 1574912 | tf_op jit(solution)/shard_map/scatter-add | solution.py:202
  216.4 1.5 scatter_fusion.1
  217.9 1.1 convert_element_type.33
  219.0 7.1 %all-to-all-done.5 = f32[32,16,256]{2,1,0:T(8,128)} async-done(((f32[32,16,256]{2,1,0:T(8,128)}), f32[32,16,256]{2,1,0:T(8,128)}, u32[]{:S(2)}, u32[]{:S(2)}) %all-to-all-start.5) | async-done | bytes 524320 | tf_op jit(solution)/shard_map/all_to_all | solution.py:175
  226.1 1.9 slice_multiply_fusion
  (15 shorter events, 0.1 us)
Async XLA Ops:
  0.6 62.1 %copy-start = (bf16[256,256]{1,0:T(8,128)(2,1)S(1)}, bf16[256,256]{1,0:T(8,128)(2,1)}, u32[]{:S(2)}) copy-start(bf16[256,256]{1,0:T(8,128)(2,1)} %param.13) | copy-start | bytes 393220
  0.6 21.9 %copy-start.1 = (bf16[2048,256]{1,0:T(8,128)(2,1)S(1)}, bf16[2048,256]{1,0:T(8,128)(2,1)}, u32[]{:S(2)}) copy-start(bf16[2048,256]{1,0:T(8,128)(2,1)} %param.11) | copy-start | bytes 3145732
  0.7 21.8 %copy-start.6 = (bf16[256,256]{1,0:T(8,128)(2,1)S(1)}, bf16[256,256]{1,0:T(8,128)(2,1)}, u32[]{:S(2)}) copy-start(bf16[256,256]{1,0:T(8,128)(2,1)} %param.12) | copy-start | bytes 393220
  4.1 13.1 %all-to-all-start.1 = ((bf16[8,32,256]{2,1,0:T(8,128)(2,1)}), bf16[8,32,256]{2,1,0:T(8,128)(2,1)S(1)}, u32[]{:S(2)}, u32[]{:S(2)}) async-start(bf16[8,32,256]{2,1,0:T(8,128)(2,1)} %broadcast_in_dim.45), calls=%async_computation.1 | async-start | bytes 262144 | tf_op jit(solution)/shard_map/all_to_all | solution.py:150
  17.2 15.1 %all-to-all-start = ((bf16[32,16,256]{2,1,0:T(8,128)(2,1)}), bf16[32,16,256]{2,1,0:T(8,128)(2,1)S(1)}, u32[]{:S(2)}, u32[]{:S(2)}) async-start(bf16[32,16,256]{2,1,0:T(8,128)(2,1)} %broadcast_select_fusion), calls=%async_computation | async-start | bytes 524288 | tf_op jit(solution)/shard_map/all_to_all | solution.py:155
  62.8 4.5 %copy-start.2 = (bf16[2048,256]{1,0:T(8,128)(2,1)S(1)}, bf16[2048,256]{1,0:T(8,128)(2,1)}, u32[]{:S(2)}) copy-start(bf16[2048,256]{1,0:T(8,128)(2,1)} %shard_map.138) | copy-start | bytes 3145732
  108.3 1.1 copy-start.3
  110.0 62.5 %all-to-all-start.3 = ((bf16[8,32,256]{2,1,0:T(8,128)(2,1)}), bf16[8,32,256]{2,1,0:T(8,128)(2,1)S(1)}, u32[]{:S(2)}, u32[]{:S(2)}) async-start(bf16[8,32,256]{2,1,0:T(8,128)(2,1)} %bitcast.8), calls=%async_computation.3 | async-start | bytes 262144 | tf_op jit(solution)/shard_map/all_to_all | solution.py:193
  172.6 33.8 %copy-start.4 = (bf16[8,32,256]{2,1,0:T(8,128)(2,1)}, bf16[8,32,256]{2,1,0:T(8,128)(2,1)S(1)}, u32[]{:S(2)}) copy-start(bf16[8,32,256]{2,1,0:T(8,128)(2,1)S(1)} %all-to-all-done.3) | copy-start | bytes 393220
  172.6 37.2 %copy-start.7 = (s32[1,32,16]{1,2,0:T(8,128)S(1)}, s32[1,32,16]{1,2,0:T(8,128)}, u32[]{:S(2)}) copy-start(s32[1,32,16]{1,2,0:T(8,128)} %param.16) | copy-start | bytes 6148
  172.6 20.0 %all-to-all-start.4 = ((f32[32,16,256]{2,1,0:T(8,128)}), f32[32,16,256]{2,1,0:T(8,128)S(1)}, u32[]{:S(2)}, u32[]{:S(2)}) async-start(f32[32,16,256]{2,1,0:T(8,128)} %bitcast.10), calls=%async_computation.4 | async-start | bytes 1048576 | tf_op jit(solution)/shard_map/all_to_all | solution.py:172
  192.6 13.0 %all-to-all-start.2 = ((bf16[32,16,256]{2,1,0:T(8,128)(2,1)}), bf16[32,16,256]{2,1,0:T(8,128)(2,1)S(1)}, u32[]{:S(2)}, u32[]{:S(2)}) async-start(bf16[32,16,256]{2,1,0:T(8,128)(2,1)} %bitcast.6), calls=%async_computation.2 | async-start | bytes 524288 | tf_op jit(solution)/shard_map/all_to_all | solution.py:189
  206.4 19.7 %all-to-all-start.5 = ((f32[32,16,256]{2,1,0:T(8,128)}), f32[32,16,256]{2,1,0:T(8,128)}, u32[]{:S(2)}, u32[]{:S(2)}) async-start(f32[32,16,256]{2,1,0:T(8,128)} %broadcast_in_dim.47), calls=%async_computation.5 | async-start | bytes 1048576 | tf_op jit(solution)/shard_map/all_to_all | solution.py:175
  209.9 2.2 copy-start.5

commit v2 on v1

v2 whole, which is shorter than its diff:
```python
import functools

import jax
import jax.numpy as jnp
from jax import lax
from jax.experimental import pallas as pl
from jax.experimental.pallas import tpu as pltpu
from jax.sharding import PartitionSpec as P


def _tile_block(tiles):
    for size in (80, 64, 40, 32, 16, 8, 4, 2, 1):
        if tiles % size == 0:
            return size
    return 1


def _val_map(tb):
    def index_map(i, src, dst, cnt):
        last = jnp.maximum(cnt[0] - 1, 0) // tb
        return (jnp.minimum(i, last), 0, 0)
    return index_map

def _agg_kernel(src_ref, dst_ref, cnt_ref, val_ref, source_ref, out_ref, acc_ref, *, tb, edge, batch):
    i = pl.program_id(0)
    last_src = source_ref.shape[0] // edge - 1
    last_dst = acc_ref.shape[0] // edge - 1
    @pl.when(i == 0)
    def _():
        acc_ref[...] = jnp.zeros_like(acc_ref)
    count = cnt_ref[0]
    def one(t, k):
        s = jnp.clip(src_ref[t], 0, last_src)
        x = source_ref[pl.ds(pl.multiple_of(s * edge, edge), edge), :]
        return jnp.dot(val_ref[k], x, preferred_element_type=jnp.float32)
    def add(t, term):
        d = jnp.clip(dst_ref[t], 0, last_dst)
        rows = pl.ds(pl.multiple_of(d * edge, edge), edge)
        acc_ref[rows, :] += term
    full = (i + 1) * tb <= count
    @pl.when(full)
    def _():
        for k0 in range(0, tb, batch):
            terms = [one(i * tb + k, k) for k in range(k0, k0 + batch)]
            for k, term in zip(range(k0, k0 + batch), terms):
                add(i * tb + k, term)
    @pl.when(jnp.logical_and(jnp.logical_not(full), i * tb < count))
    def _():
        def body(k, carry):
            t = i * tb + k
            @pl.when(t < count)
            def _():
                add(t, one(t, k))
            return carry
        lax.fori_loop(0, tb, body, 0)
    @pl.when(i == pl.num_programs(0) - 1)
    def _():
        out_ref[...] = acc_ref[...].astype(out_ref.dtype)

def tile_aggregate(tile_src, tile_dst, tile_count, tile_val, source, rows, tb=16, batch=1):
    tiles, edge, _ = tile_val.shape
    width = source.shape[1]
    kernel = functools.partial(_agg_kernel, tb=tb, edge=edge, batch=batch)
    return pl.pallas_call(
        kernel,
        out_shape=jax.ShapeDtypeStruct((rows, width), jnp.bfloat16),
        grid_spec=pltpu.PrefetchScalarGridSpec(
            num_scalar_prefetch=3, grid=(tiles // tb,),
            in_specs=[pl.BlockSpec((tb, edge, edge), _val_map(tb)),
                      pl.BlockSpec(source.shape, lambda i, s, d, c: (0, 0))],
            out_specs=pl.BlockSpec((rows, width), lambda i, s, d, c: (0, 0)),
            scratch_shapes=[pltpu.VMEM((rows, width), jnp.float32)]),
        compiler_params=pltpu.CompilerParams(dimension_semantics=("arbitrary",)),
    )(tile_src, tile_dst, tile_count, tile_val, source)

def _back_kernel(src_ref, dst_ref, cnt_ref, val_ref, daggT_ref, out_ref, *, tb, edge, batch):
    i = pl.program_id(0)
    last_src = out_ref.shape[1] // edge - 1
    last_dst = daggT_ref.shape[1] // edge - 1
    @pl.when(i == 0)
    def _():
        out_ref[...] = jnp.zeros_like(out_ref)
    count = cnt_ref[0]
    def one(t, k):
        d = jnp.clip(dst_ref[t], 0, last_dst)
        y = daggT_ref[:, pl.ds(pl.multiple_of(d * edge, edge), edge)]
        return jnp.dot(y, val_ref[k], preferred_element_type=jnp.float32)
    def add(t, term):
        s = jnp.clip(src_ref[t], 0, last_src)
        cols = pl.ds(pl.multiple_of(s * edge, edge), edge)
        out_ref[:, cols] += term
    full = (i + 1) * tb <= count
    @pl.when(full)
    def _():
        for k0 in range(0, tb, batch):
            terms = [one(i * tb + k, k) for k in range(k0, k0 + batch)]
            for k, term in zip(range(k0, k0 + batch), terms):
                add(i * tb + k, term)
    @pl.when(jnp.logical_and(jnp.logical_not(full), i * tb < count))
    def _():
        def body(k, carry):
            t = i * tb + k
            @pl.when(t < count)
            def _():
                add(t, one(t, k))
            return carry
        lax.fori_loop(0, tb, body, 0)

def tile_backward_t(tile_src, tile_dst, tile_count, tile_val, daggT, src_rows, tb=16, batch=1):
    tiles, edge, _ = tile_val.shape
    width = daggT.shape[0]
    kernel = functools.partial(_back_kernel, tb=tb, edge=edge, batch=batch)
    return pl.pallas_call(
        kernel,
        out_shape=jax.ShapeDtypeStruct((width, src_rows), jnp.float32),
        grid_spec=pltpu.PrefetchScalarGridSpec(
            num_scalar_prefetch=3, grid=(tiles // tb,),
            in_specs=[pl.BlockSpec((tb, edge, edge), _val_map(tb)),
                      pl.BlockSpec(daggT.shape, lambda i, s, d, c: (0, 0))],
            out_specs=pl.BlockSpec((width, src_rows), lambda i, s, d, c: (0, 0))),
        compiler_params=pltpu.CompilerParams(dimension_semantics=("arbitrary",)),
    )(tile_src, tile_dst, tile_count, tile_val, daggT)


def body(
    feats,
    w_self,
    w_neigh,
    cotangent,
    hub_rows,
    send_rows,
    send_count,
    tile_dst,
    tile_src,
    tile_count,
    tile_val,
):
    edge = tile_val.shape[1]
    rows, width = feats.shape
    peers = send_rows.shape[1]
    slots = send_rows.shape[2]
    group = lax.axis_size("dev")
    hubs_dev = hub_rows.shape[0]

    own_hubs = feats[hub_rows]
    hub_out = jnp.broadcast_to(own_hubs[None], (group, hubs_dev, width))
    hub_table = lax.all_to_all(hub_out, "dev", split_axis=0, concat_axis=0, tiled=True)
    hub_table = hub_table.reshape(group * hubs_dev, width)

    live = lax.broadcasted_iota(jnp.int32, (peers, slots), 1) < send_count[0][:, None]
    outgoing = jnp.where(live[:, :, None], feats[send_rows[0]], jnp.zeros((), jnp.bfloat16))
    incoming = lax.all_to_all(outgoing, ("dom", "dev"), split_axis=0, concat_axis=0, tiled=True)
    source = jnp.concatenate([feats, incoming.reshape(peers * slots, width), hub_table], axis=0)

    tb = _tile_block(tile_val.shape[0])
    agg = tile_aggregate(tile_src, tile_dst, tile_count, tile_val, source, rows, tb=tb)

    pre = jnp.dot(feats, w_self, preferred_element_type=jnp.float32) + jnp.dot(
        agg, w_neigh, preferred_element_type=jnp.float32
    )
    sig = jax.nn.sigmoid(pre)
    out = (pre * sig).astype(jnp.bfloat16)
    dpre = (cotangent.astype(jnp.float32) * sig * (1.0 + pre * (1.0 - sig))).astype(jnp.bfloat16)

    contract_rows = (((0,), (0,)), ((), ()))
    local_ws = lax.dot_general(feats, dpre, contract_rows, preferred_element_type=jnp.float32)
    local_wn = lax.dot_general(agg, dpre, contract_rows, preferred_element_type=jnp.float32)
    partial = jnp.concatenate([local_ws, local_wn], axis=0)
    parts = partial.reshape(peers, -1, width)
    gathered = lax.all_to_all(parts, ("dom", "dev"), split_axis=0, concat_axis=0, tiled=True)
    piece = jnp.sum(gathered, axis=0)
    spread_piece = jnp.broadcast_to(piece[None], (peers,) + piece.shape)
    summed = lax.all_to_all(spread_piece, ("dom", "dev"), split_axis=0, concat_axis=0, tiled=True)
    summed = summed.reshape(partial.shape)
    scale = 1.0 / jnp.sqrt(jnp.float32(rows * peers))
    grad_ws = summed[: w_self.shape[0]] * scale
    grad_wn = summed[w_self.shape[0] :] * scale

    contract_cols = (((1,), (1,)), ((), ()))
    dagg_t = lax.dot_general(w_neigh, dpre, contract_cols, preferred_element_type=jnp.float32).astype(
        jnp.bfloat16
    )
    dsource_t = tile_backward_t(tile_src, tile_dst, tile_count, tile_val, dagg_t, source.shape[0], tb=tb)
    own = dsource_t[:, :rows].T
    returning = dsource_t[:, rows : rows + peers * slots].T.reshape(peers, slots, width)
    hub_part = dsource_t[:, rows + peers * slots :].T
    returned = lax.all_to_all(
        returning.astype(jnp.bfloat16), ("dom", "dev"), split_axis=0, concat_axis=0, tiled=True
    ).astype(jnp.float32)
    returned = jnp.where(live[:, :, None], returned, jnp.float32(0.0))
    hub_back = lax.all_to_all(
        hub_part.astype(jnp.bfloat16).reshape(group, hubs_dev, width),
        "dev",
        split_axis=0,
        concat_axis=0,
        tiled=True,
    )
    hub_back = jnp.sum(hub_back.astype(jnp.float32), axis=0)
    grad = lax.dot_general(dpre, w_self, contract_cols, preferred_element_type=jnp.float32) + own
    grad = grad.at[send_rows[0].reshape(-1)].add(returned.reshape(peers * slots, width))
    grad = grad.at[hub_rows].add(hub_back)
    return (out, grad.astype(jnp.bfloat16), grad_ws, grad_wn)


def solution(mesh):
    return jax.shard_map(
        body,
        mesh=mesh,
        in_specs=(
            P(("dom", "dev"), None),
            P(),
            P(),
            P(("dom", "dev"), None),
            P(("dom", "dev")),
            P(("dom", "dev"), None, None),
            P(("dom", "dev"), None),
            P(("dom", "dev")),
            P(("dom", "dev")),
            P(("dom", "dev")),
            P(("dom", "dev"), None, None),
        ),
        out_specs=(P(("dom", "dev"), None), P(("dom", "dev"), None), P(), P()),
        check_vma=False,
    )
```

time: 229 us -> 133 us (0.58)
  Pallas kernels: 66.4 us -> 16.9 us
  starting transfers between devices: 76.3 us -> 30.1 us
  waiting for transfers between devices: 46.9 us -> 39 us
  local copies, waits for them, and re-layouts: 10.2 us -> 16.7 us
    all_to_all x1, starting transfers between devices: 55.8 us -> 9.61 us  [body(): lax.all_to_all(hub_part.astype(jnp.bfloat16).reshape(group, hubs_dev, wid...]
    pallas_call x1, Pallas kernels: 37.1 us -> 9.4 us  [tile_backward_t(): pl.pallas_call(kernel, out_shape=jax.ShapeDtypeStruct((width, src_rows),...]
    pallas_call x1, Pallas kernels: 29.3 us -> 7.46 us  [tile_aggregate(): pl.pallas_call(kernel, out_shape=jax.ShapeDtypeStruct((rows, width), jnp....]
    all_to_all x1, waiting for transfers between devices: 7.06 us -> 1.16 us  [body(): lax.all_to_all(spread_piece, ('dom', 'dev'), split_axis=0, concat_axis=0,...]
    convert_element_type x0 -> x4, local copies, waits for them, and re-layouts: none -> 4.38 us  [the longest x2 3.61 us: body(): returning.astype(jnp.bfloat16)]
    slice x2 -> x0, local copies, waits for them, and re-layouts: 2.33 us -> none  [the longest x1 1.67 us: body(): returning = dsource[rows:rows + peers * slots].reshape(peers, slots, width)]
  transfers between devices with their start and end apart: 6 -> 6, of which waited for: 6 -> 6; matrix products, arithmetic and copies ran while one was open for 9% -> 21% of each run, Pallas kernels for 0% -> 0%
where the time goes in v2:
time: 133 us; the launch traced here: 132 us
  waiting for transfers between devices  39 us (29%)
  starting transfers between devices  30.1 us (23%)
  Pallas kernels  16.9 us (13%)
  local copies, waits for them, and re-layouts  16.7 us (13%)
  other arithmetic  16.6 us (12%)
  matrix products  11.4 us (9%)
  between operations  1.5 us (1%)
    all_to_all x1, waiting for transfers between devices, body(): lax.all_to_all(parts, ('dom', 'dev'), split_axis=0, concat_axis=0, tiled=...  12.7 us
    all_to_all x1, waiting for transfers between devices, body(): lax.all_to_all(returning.astype(jnp.bfloat16), ('dom', 'dev'), split_axis...  10.3 us
    all_to_all x1, starting transfers between devices, body(): lax.all_to_all(hub_part.astype(jnp.bfloat16).reshape(group, hubs_dev, wid...  9.61 us
    pallas_call x1, Pallas kernels, tile_backward_t(): pl.pallas_call(kernel, out_shape=jax.ShapeDtypeStruct((width, src_rows),...  9.4 us
    all_to_all x1, waiting for transfers between devices, body(): lax.all_to_all(outgoing, ('dom', 'dev'), split_axis=0, concat_axis=0, til...  7.95 us
    pallas_call x1, Pallas kernels, tile_aggregate(): pl.pallas_call(kernel, out_shape=jax.ShapeDtypeStruct((rows, width), jnp....  7.46 us
    all_to_all x1, starting transfers between devices, body(): lax.all_to_all(hub_out, 'dev', split_axis=0, concat_axis=0, tiled=True)  6.33 us
    all_to_all x1, waiting for transfers between devices, body(): lax.all_to_all(hub_part.astype(jnp.bfloat16).reshape(group, hubs_dev, wid...  5.42 us
  transfers between devices with their start and end apart: 6, of which 6 were waited for; matrix products, arithmetic and copies ran while one was open for 21% of the time, Pallas kernels for 0%

profile of v2, /device:TPU:0, one launch (start us, length us, event | category | flops | bytes accessed | tf_op | source)
XLA Modules:
  0.0 132.1 jit_solution(16631521825342749533)
XLA Ops:
  0.7 0.8 compare_select_fusion.2
  1.4 0.6 copy-done.11
  2.0 2.0 %gather_fusion.1 = bf16[32,256]{1,0:T(8,128)(2,1)S(1)} fusion(bf16[2048,256]{1,0:T(8,128)(2,1)} %param.11, s32[1024]{0:T(1024)S(1)} %pad_clamp_fusion), kind=kCustom, calls=%fused_computation.1 | custom fusion | bytes 32896 | tf_op jit(solution)/shard_map/gather | solution.py:145
  4.0 0.7 broadcast_in_dim.45
  4.6 6.3 %all-to-all-start.1 = ((bf16[8,32,256]{2,1,0:T(8,128)(2,1)}), bf16[8,32,256]{2,1,0:T(8,128)(2,1)S(1)}, u32[]{:S(2)}, u32[]{:S(2)}) async-start(bf16[8,32,256]{2,1,0:T(8,128)(2,1)} %broadcast_in_dim.45), calls=%async_computation.1 | async-start | bytes 262144 | tf_op jit(solution)/shard_map/all_to_all | solution.py:147
  11.0 0.7 iota_compare_fusion
  11.7 0.7 compare_select_fusion
  12.4 0.1 copy.20
  12.5 0.1 reshape.119
  12.6 2.9 %gather_fusion = bf16[512,256]{1,0:T(8,128)(2,1)S(1)} fusion(bf16[2048,256]{1,0:T(8,128)(2,1)} %param.11, s32[1024]{0:T(1024)S(1)} %pad_clamp_fusion.1), kind=kCustom, calls=%fused_computation | custom fusion | bytes 526336 | tf_op jit(solution)/shard_map/gather | solution.py:151
  15.5 0.8 broadcast_select_fusion
  16.3 1.4 %all-to-all-done.1 = bf16[8,32,256]{2,1,0:T(8,128)(2,1)S(1)} async-done(((bf16[8,32,256]{2,1,0:T(8,128)(2,1)}), bf16[8,32,256]{2,1,0:T(8,128)(2,1)S(1)}, u32[]{:S(2)}, u32[]{:S(2)}) %all-to-all-start.1) | async-done | bytes 131104 | tf_op jit(solution)/shard_map/all_to_all | solution.py:147
  17.7 4.7 %all-to-all-start = ((bf16[32,16,256]{2,1,0:T(8,128)(2,1)}), bf16[32,16,256]{2,1,0:T(8,128)(2,1)S(1)}, u32[]{:S(2)}, u32[]{:S(2)}) async-start(bf16[32,16,256]{2,1,0:T(8,128)(2,1)} %broadcast_select_fusion), calls=%async_computation | async-start | bytes 524288 | tf_op jit(solution)/shard_map/all_to_all | solution.py:152
  23.1 1.8 %fusion.1 = f32[2048,256]{1,0:T(8,128)} fusion(bf16[2048,256]{1,0:T(8,128)(2,1)S(1)} %copy-done.2, bf16[256,256]{1,0:T(8,128)(2,1)S(1)} %copy-done.8), kind=kOutput, calls=%fused_computation.28 | convolution fusion | flops 268435456 | bytes 3276800 | tf_op jit(solution)/shard_map/dot_general | solution.py:158
  24.9 7.9 %all-to-all-done = bf16[32,16,256]{2,1,0:T(8,128)(2,1)S(1)} async-done(((bf16[32,16,256]{2,1,0:T(8,128)(2,1)}), bf16[32,16,256]{2,1,0:T(8,128)(2,1)S(1)}, u32[]{:S(2)}, u32[]{:S(2)}) %all-to-all-start) | async-done | bytes 262176 | tf_op jit(solution)/shard_map/all_to_all | solution.py:152
  32.8 1.2 pad_maximum_fusion.source_ref
  34.0 7.5 %shard_map.138 = bf16[2048,256]{1,0:T(8,128)(2,1)} custom-call(s32[320]{0:T(512)} %src_ref.3, s32[320]{0:T(512)} %dst_ref.3, s32[1]{0:T(128)S(6)} %copy.31.cnt_ref, bf16[320,128,128]{2,1,0:T(8,128)(2,1)} %val_ref.3, bf16[2816,256]{1,0:T(8,128)(2,1)} %pad_maximum_fusion.source_ref), custom_call_target="tpu_custom_call" | custom-call | tf_op jit(solution)/shard_map/pallas_call | solution.py:64
  41.5 4.2 %multiply_convert_fusion = (bf16[2048,256]{1,0:T(8,128)(2,1)S(1)}, bf16[2048,256]{1,0:T(8,128)(2,1)}) fusion(bf16[2048,256]{1,0:T(8,128)(2,1)S(1)} %copy-done.13, f32[2048,256]{1,0:T(8,128)} %fusion.1, bf16[2048,256]{1,0:T(8,128)(2,1)} %shard_map.138, bf16[256,256]{1,0:T(8,128)(2,1)S(1)} %copy-done), kind=kOutput, calls=%fused_computation.9 | convolution fusion | flops 275251200 | bytes 6422528 | tf_op jit(solution)/shard_map/dot_general | solution.py:158
  45.7 0.5 fusion.2
  46.1 1.4 %fusion.daggT_ref = bf16[256,2048]{1,0:T(8,128)(2,1)} fusion(bf16[2048,256]{1,0:T(8,128)(2,1)S(1)} %get-tuple-element.8, bf16[256,256]{1,0:T(8,128)(2,1)S(1)} %copy-done), kind=kOutput, calls=%fused_computation.7 | convolution fusion | flops 268959744 | bytes 2228224 | tf_op jit(solution)/shard_map/dot_general | solution.py:180
  47.6 9.4 %shard_map.139 = f32[256,2816]{1,0:T(8,128)} custom-call(s32[320]{0:T(512)} %src_ref.3, s32[320]{0:T(512)} %dst_ref.3, s32[1]{0:T(128)S(6)} %copy.31.cnt_ref, bf16[320,128,128]{2,1,0:T(8,128)(2,1)} %val_ref.3, bf16[256,2048]{1,0:T(8,128)(2,1)} %fusion.daggT_ref), custom_call_target="tpu_custom_call" | custom-call | tf_op jit(solution)/shard_map/pallas_call | solution.py:113
  57.0 2.0 %convert.4 = bf16[256,2816]{1,0:T(8,128)(2,1)S(1)} convert(f32[256,2816]{1,0:T(8,128)} %shard_map.139) | non-fusion elementwise | flops 720896 | bytes 4325376 | tf_op jit(solution)/shard_map/convert.1
  59.0 1.1 copy-done.5
  60.1 0.8 copy.26
  60.8 9.6 %all-to-all-start.3 = ((bf16[8,32,256]{2,1,0:T(8,128)(2,1)}), bf16[8,32,256]{2,1,0:T(8,128)(2,1)S(1)}, u32[]{:S(2)}, u32[]{:S(2)}) async-start(bf16[8,32,256]{2,1,0:T(8,128)(2,1)} %bitcast.12), calls=%async_computation.3 | async-start | bytes 262144 | tf_op jit(solution)/shard_map/all_to_all | solution.py:191
  70.4 0.5 convolution_bitcast_fusion
  71.0 0.8 pad_maximum_fusion.1
  71.8 5.4 %all-to-all-done.3 = bf16[8,32,256]{2,1,0:T(8,128)(2,1)S(1)} async-done(((bf16[8,32,256]{2,1,0:T(8,128)(2,1)}), bf16[8,32,256]{2,1,0:T(8,128)(2,1)S(1)}, u32[]{:S(2)}, u32[]{:S(2)}) %all-to-all-start.3) | async-done | bytes 131104 | tf_op jit(solution)/shard_map/all_to_all | solution.py:191
  77.2 0.7 copy-done.6
  77.9 3.6 %all-to-all-start.4 = ((f32[32,16,256]{2,1,0:T(8,128)}), f32[32,16,256]{2,1,0:T(8,128)S(1)}, u32[]{:S(2)}, u32[]{:S(2)}) async-start(f32[32,16,256]{2,1,0:T(8,128)} %bitcast.14), calls=%async_computation.4 | async-start | bytes 1048576 | tf_op jit(solution)/shard_map/all_to_all | solution.py:170
  81.5 1.8 %slice_bitcast_fusion.1 = bf16[512,256]{0,1:T(8,128)(2,1)} fusion(bf16[256,2816]{1,0:T(8,128)(2,1)} %copy-done.5), kind=kLoop, calls=%fused_computation.18 | loop fusion | bytes 524288 | tf_op jit(solution)/shard_map/convert_element_type | solution.py:188
  83.3 1.8 %copy.24 = bf16[512,256]{1,0:T(8,128)(2,1)} copy(bf16[512,256]{0,1:T(8,128)(2,1)} %slice_bitcast_fusion.1) | data formatting | bytes 524288 | tf_op jit(solution)/shard_map/convert_element_type | solution.py:188
  85.1 12.7 %all-to-all-done.4 = f32[32,16,256]{2,1,0:T(8,128)S(1)} async-done(((f32[32,16,256]{2,1,0:T(8,128)}), f32[32,16,256]{2,1,0:T(8,128)S(1)}, u32[]{:S(2)}, u32[]{:S(2)}) %all-to-all-start.4) | async-done | bytes 524320 | tf_op jit(solution)/shard_map/all_to_all | solution.py:170
  97.8 3.3 %all-to-all-start.2 = ((bf16[32,16,256]{2,1,0:T(8,128)(2,1)}), bf16[32,16,256]{2,1,0:T(8,128)(2,1)}, u32[]{:S(2)}, u32[]{:S(2)}) async-start(bf16[32,16,256]{2,1,0:T(8,128)(2,1)} %bitcast.41), calls=%async_computation.2 | async-start | bytes 524288 | tf_op jit(solution)/shard_map/all_to_all | solution.py:187
  101.2 10.3 %all-to-all-done.2 = bf16[32,16,256]{2,1,0:T(8,128)(2,1)} async-done(((bf16[32,16,256]{2,1,0:T(8,128)(2,1)}), bf16[32,16,256]{2,1,0:T(8,128)(2,1)}, u32[]{:S(2)}, u32[]{:S(2)}) %all-to-all-start.2) | async-done | bytes 262176 | tf_op jit(solution)/shard_map/all_to_all | solution.py:187
  111.5 0.8 broadcast_in_dim.47
  112.3 2.6 %all-to-all-start.5 = ((f32[32,16,256]{2,1,0:T(8,128)}), f32[32,16,256]{2,1,0:T(8,128)S(1)}, u32[]{:S(2)}, u32[]{:S(2)}) async-start(f32[32,16,256]{2,1,0:T(8,128)} %broadcast_in_dim.47), calls=%async_computation.5 | async-start | bytes 1048576 | tf_op jit(solution)/shard_map/all_to_all | solution.py:173
  114.9 0.8 copy.23
  115.7 0.7 reshape_squeeze.3
  116.4 0.7 compare_select_fusion.1
  117.1 3.0 %convolution_add_fusion = f32[2048,256]{0,1:T(8,128)} fusion(bf16[2048,256]{1,0:T(8,128)(2,1)} %copy-done.3, bf16[256,256]{1,0:T(8,128)(2,1)} %param.12, f32[256,2816]{1,0:T(8,128)S(1)} %copy-done.1), kind=kOutput, calls=%fused_computation.4 | convolution fusion | flops 268959744 | bytes 5373952 | tf_op jit(solution)/shard_map/dot_general | solution.py:199
  120.1 2.0 %copy.25 = f32[2048,256]{1,0:T(8,128)S(1)} copy(f32[2048,256]{0,1:T(8,128)} %convolution_add_fusion) | data formatting | bytes 4194304 | tf_op jit(solution)/shard_map/add | solution.py:199
  122.1 1.1 convert_select_fusion
  123.2 4.3 %scatter_fusion = f32[2048,256]{1,0:T(8,128)S(1)} fusion(f32[2048,256]{1,0:T(8,128)S(1)} %copy.25, s32[512]{0:T(512)S(1)} %bitcast.46, f32[512,256]{1,0:T(8,128)S(1)} %bitcast.39), kind=kCustom, calls=%fused_computation.2 | custom fusion | flops 131072 | bytes 1574912 | tf_op jit(solution)/shard_map/scatter-add | solution.py:200
  127.5 1.5 %scatter_fusion.1 = f32[2048,256]{1,0:T(8,128)S(1)} fusion(f32[2048,256]{1,0:T(8,128)S(1)} %scatter_fusion, s32[32]{0:T(128)S(1)} %copy-done.12, f32[32,256]{1,0:T(8,128)S(1)} %convert_reduce_fusion), kind=kCustom, calls=%fused_computation.3 | custom fusion | flops 8192 | bytes 98432 | tf_op jit(solution)/shard_map/scatter-add | solution.py:201
  129.1 1.1 convert_element_type.44
  130.1 1.2 all-to-all-done.5
  131.3 0.8 slice_multiply_fusion
  (30 shorter events, 0.2 us)
Async XLA Ops:
  0.6 40.8 %copy-start = (bf16[256,256]{1,0:T(8,128)(2,1)S(1)}, bf16[256,256]{1,0:T(8,128)(2,1)}, u32[]{:S(2)}) copy-start(bf16[256,256]{1,0:T(8,128)(2,1)} %param.13) | copy-start | bytes 393220
  0.6 22.4 %copy-start.2 = (bf16[2048,256]{1,0:T(8,128)(2,1)S(1)}, bf16[2048,256]{1,0:T(8,128)(2,1)}, u32[]{:S(2)}) copy-start(bf16[2048,256]{1,0:T(8,128)(2,1)} %param.11) | copy-start | bytes 3145732
  0.7 22.4 %copy-start.8 = (bf16[256,256]{1,0:T(8,128)(2,1)S(1)}, bf16[256,256]{1,0:T(8,128)(2,1)}, u32[]{:S(2)}) copy-start(bf16[256,256]{1,0:T(8,128)(2,1)} %param.12) | copy-start | bytes 393220
  1.4 0.6 copy-start.11
  4.6 13.1 %all-to-all-start.1 = ((bf16[8,32,256]{2,1,0:T(8,128)(2,1)}), bf16[8,32,256]{2,1,0:T(8,128)(2,1)S(1)}, u32[]{:S(2)}, u32[]{:S(2)}) async-start(bf16[8,32,256]{2,1,0:T(8,128)(2,1)} %broadcast_in_dim.45), calls=%async_computation.1 | async-start | bytes 262144 | tf_op jit(solution)/shard_map/all_to_all | solution.py:147
  11.7 13.2 %copy-start.9 = (pred[32,16]{1,0:T(8,128)(4,1)}, pred[32,16]{1,0:T(8,128)(4,1)S(1)}, u32[]{:S(2)}) copy-start(pred[32,16]{1,0:T(8,128)(4,1)S(1)} %iota_compare_fusion) | copy-start | bytes 1540
  17.7 15.1 %all-to-all-start = ((bf16[32,16,256]{2,1,0:T(8,128)(2,1)}), bf16[32,16,256]{2,1,0:T(8,128)(2,1)S(1)}, u32[]{:S(2)}, u32[]{:S(2)}) async-start(bf16[32,16,256]{2,1,0:T(8,128)(2,1)} %broadcast_select_fusion), calls=%async_computation | async-start | bytes 524288 | tf_op jit(solution)/shard_map/all_to_all | solution.py:152
  34.0 7.5 %copy-start.13 = (bf16[2048,256]{1,0:T(8,128)(2,1)S(1)}, bf16[2048,256]{1,0:T(8,128)(2,1)}, u32[]{:S(2)}) copy-start(bf16[2048,256]{1,0:T(8,128)(2,1)} %param.14) | copy-start | bytes 3145732
  41.5 4.2 %copy-start.4 = (bf16[2048,256]{1,0:T(8,128)(2,1)S(1)}, bf16[2048,256]{1,0:T(8,128)(2,1)}, u32[]{:S(2)}) copy-start(bf16[2048,256]{1,0:T(8,128)(2,1)} %shard_map.138) | copy-start | bytes 3145732
  45.6 24.8 %copy-start.3 = (bf16[2048,256]{1,0:T(8,128)(2,1)}, bf16[2048,256]{1,0:T(8,128)(2,1)S(1)}, u32[]{:S(2)}) copy-start(bf16[2048,256]{1,0:T(8,128)(2,1)S(1)} %get-tuple-element.8) | copy-start | bytes 3145732
  58.9 1.1 copy-start.5
  60.8 16.4 %all-to-all-start.3 = ((bf16[8,32,256]{2,1,0:T(8,128)(2,1)}), bf16[8,32,256]{2,1,0:T(8,128)(2,1)S(1)}, u32[]{:S(2)}, u32[]{:S(2)}) async-start(bf16[8,32,256]{2,1,0:T(8,128)(2,1)} %bitcast.12), calls=%async_computation.3 | async-start | bytes 262144 | tf_op jit(solution)/shard_map/all_to_all | solution.py:191
  77.2 0.7 copy-start.6
  77.9 19.9 %all-to-all-start.4 = ((f32[32,16,256]{2,1,0:T(8,128)}), f32[32,16,256]{2,1,0:T(8,128)S(1)}, u32[]{:S(2)}, u32[]{:S(2)}) async-start(f32[32,16,256]{2,1,0:T(8,128)} %bitcast.14), calls=%async_computation.4 | async-start | bytes 1048576 | tf_op jit(solution)/shard_map/all_to_all | solution.py:170
  81.5 35.6 %copy-start.1 = (f32[256,2816]{1,0:T(8,128)S(1)}, f32[256,2816]{1,0:T(8,128)}, u32[]{:S(2)}) copy-start(f32[256,2816]{1,0:T(8,128)} %shard_map.139) | copy-start | bytes 8650756
  97.8 13.7 %all-to-all-start.2 = ((bf16[32,16,256]{2,1,0:T(8,128)(2,1)}), bf16[32,16,256]{2,1,0:T(8,128)(2,1)}, u32[]{:S(2)}, u32[]{:S(2)}) async-start(bf16[32,16,256]{2,1,0:T(8,128)(2,1)} %bitcast.41), calls=%async_computation.2 | async-start | bytes 524288 | tf_op jit(solution)/shard_map/all_to_all | solution.py:187
  112.3 19.0 %all-to-all-start.5 = ((f32[32,16,256]{2,1,0:T(8,128)}), f32[32,16,256]{2,1,0:T(8,128)S(1)}, u32[]{:S(2)}, u32[]{:S(2)}) async-start(f32[32,16,256]{2,1,0:T(8,128)} %broadcast_in_dim.47), calls=%async_computation.5 | async-start | bytes 1048576 | tf_op jit(solution)/shard_map/all_to_all | solution.py:173
  120.1 2.0 %copy-start.7 = (bf16[8,32,256]{2,1,0:T(8,128)(2,1)S(1)}, bf16[8,32,256]{2,1,0:T(8,128)(2,1)}, u32[]{:S(2)}) copy-start(bf16[8,32,256]{2,1,0:T(8,128)(2,1)} %copy-done.6) | copy-start | bytes 393220
  120.1 2.0 %copy-start.10 = (pred[32,16]{1,0:T(8,128)(4,1)S(1)}, pred[32,16]{1,0:T(8,128)(4,1)}, u32[]{:S(2)}) copy-start(pred[32,16]{1,0:T(8,128)(4,1)} %copy-done.9) | copy-start | bytes 1540
  123.2 4.3 %copy-start.12 = (s32[32]{0:T(128)S(1)}, s32[32]{0:T(128)}, u32[]{:S(2)}) copy-start(s32[32]{0:T(128)} %copy-done.11) | copy-start | bytes 388

commit v3 on v2

--- a/solution.py
+++ b/solution.py
@@ -143,13 +143,15 @@
     hubs_dev = hub_rows.shape[0]
 
     own_hubs = feats[hub_rows]
-    hub_out = jnp.broadcast_to(own_hubs[None], (group, hubs_dev, width))
-    hub_table = lax.all_to_all(hub_out, "dev", split_axis=0, concat_axis=0, tiled=True)
-    hub_table = hub_table.reshape(group * hubs_dev, width)
+    hub_out = jnp.broadcast_to(own_hubs[None], (peers, hubs_dev, width))
 
     live = lax.broadcasted_iota(jnp.int32, (peers, slots), 1) < send_count[0][:, None]
     outgoing = jnp.where(live[:, :, None], feats[send_rows[0]], jnp.zeros((), jnp.bfloat16))
-    incoming = lax.all_to_all(outgoing, ("dom", "dev"), split_axis=0, concat_axis=0, tiled=True)
+    packed = jnp.concatenate([outgoing, hub_out], axis=1)
+    arrived = lax.all_to_all(packed, ("dom", "dev"), split_axis=0, concat_axis=0, tiled=True)
+    incoming = arrived[:, :slots]
+    group_hubs = arrived[:, slots:].reshape(peers // group, group * hubs_dev, width)
+    hub_table = lax.dynamic_index_in_dim(group_hubs, lax.axis_index("dom"), axis=0, keepdims=False)
     source = jnp.concatenate([feats, incoming.reshape(peers * slots, width), hub_table], axis=0)
 
     tb = _tile_block(tile_val.shape[0])
@@ -165,40 +167,38 @@
     contract_rows = (((0,), (0,)), ((), ()))
     local_ws = lax.dot_general(feats, dpre, contract_rows, preferred_element_type=jnp.float32)
     local_wn = lax.dot_general(agg, dpre, contract_rows, preferred_element_type=jnp.float32)
+
+    contract_cols = (((1,), (1,)), ((), ()))
+    dagg_t = lax.dot_general(w_neigh, dpre, contract_cols, preferred_element_type=jnp.float32).astype(
+        jnp.bfloat16
+    )
+    dsource_t = tile_backward_t(tile_src, tile_dst, tile_count, tile_val, dagg_t, source.shape[0], tb=tb)
+    own = dsource_t[:, :rows].T
+    returning = dsource_t[:, rows : rows + peers * slots].T.reshape(peers, slots, width)
+    hub_part = dsource_t[:, rows + peers * slots :].T
     partial = jnp.concatenate([local_ws, local_wn], axis=0)
     parts = partial.reshape(peers, -1, width)
-    gathered = lax.all_to_all(parts, ("dom", "dev"), split_axis=0, concat_axis=0, tiled=True)
-    piece = jnp.sum(gathered, axis=0)
+    back_packed = jnp.concatenate([returning, parts], axis=1)
+    back = lax.all_to_all(back_packed, ("dom", "dev"), split_axis=0, concat_axis=0, tiled=True)
+    returned = jnp.where(live[:, :, None], back[:, :slots], jnp.float32(0.0))
+    piece = jnp.sum(back[:, slots:], axis=0)
+    hub_back = lax.all_to_all(
+        hub_part.astype(jnp.bfloat16).reshape(group, hubs_dev, width),
+        "dev",
+        split_axis=0,
+        concat_axis=0,
+        tiled=True,
+    )
+    hub_back = jnp.sum(hub_back.astype(jnp.float32), axis=0)
+    grad = lax.dot_general(dpre, w_self, contract_cols, preferred_element_type=jnp.float32) + own
+    grad = grad.at[send_rows[0].reshape(-1)].add(returned.reshape(peers * slots, width))
+    grad = grad.at[hub_rows].add(hub_back)
     spread_piece = jnp.broadcast_to(piece[None], (peers,) + piece.shape)
     summed = lax.all_to_all(spread_piece, ("dom", "dev"), split_axis=0, concat_axis=0, tiled=True)
     summed = summed.reshape(partial.shape)
     scale = 1.0 / jnp.sqrt(jnp.float32(rows * peers))
     grad_ws = summed[: w_self.shape[0]] * scale
     grad_wn = summed[w_self.shape[0] :] * scale
-
-    contract_cols = (((1,), (1,)), ((), ()))
-    dagg_t = lax.dot_general(w_neigh, dpre, contract_cols, preferred_element_type=jnp.float32).astype(
-        jnp.bfloat16
-    )
-    dsource_t = tile_backward_t(tile_src, tile_dst, tile_count, tile_val, dagg_t, source.shape[0], tb=tb)
-    own = dsource_t[:, :rows].T
-    returning = dsource_t[:, rows : rows + peers * slots].T.reshape(peers, slots, width)
-    hub_part = dsource_t[:, rows + peers * slots :].T
-    returned = lax.all_to_all(
-        returning.astype(jnp.bfloat16), ("dom", "dev"), split_axis=0, concat_axis=0, tiled=True
-    ).astype(jnp.float32)
-    returned = jnp.where(live[:, :, None], returned, jnp.float32(0.0))
-    hub_back = lax.all_to_all(
-        hub_part.astype(jnp.bfloat16).reshape(group, hubs_dev, width),
-        "dev",
-        split_axis=0,
-        concat_axis=0,
-        tiled=True,
-    )
-    hub_back = jnp.sum(hub_back.astype(jnp.float32), axis=0)
-    grad = lax.dot_general(dpre, w_self, contract_cols, preferred_element_type=jnp.float32) + own
-    grad = grad.at[send_rows[0].reshape(-1)].add(returned.reshape(peers * slots, width))
-    grad = grad.at[hub_rows].add(hub_back)
     return (out, grad.astype(jnp.bfloat16), grad_ws, grad_wn)
 
 

time: 133 us -> 136 us (1.023)
  waiting for transfers between devices: 39 us -> 53.1 us
  local copies, waits for them, and re-layouts: 16.7 us -> 11.5 us
  Pallas kernels: 16.9 us -> 13 us
  starting transfers between devices: 30.1 us -> 27.9 us
    all_to_all x4 -> x2, waiting for transfers between devices: 32.4 us -> 46.3 us  [the longest x1 26.8 us: body(): lax.all_to_all(back_packed, ('dom', 'dev'), split_axis=0, concat_axis=0,...]
    all_to_all x1, starting transfers between devices: 9.61 us -> 4 us  [body(): lax.all_to_all(hub_part.astype(jnp.bfloat16).reshape(group, hubs_dev, wid...]
    convert_element_type x2 -> x0, local copies, waits for them, and re-layouts: 3.61 us -> none  [body(): returning.astype(jnp.bfloat16)]
    all_to_all x4 -> x2, starting transfers between devices: 17.9 us -> 20.6 us  [the longest x1 13.3 us: body(): lax.all_to_all(back_packed, ('dom', 'dev'), split_axis=0, concat_axis=0,...]
    pallas_call x1, Pallas kernels: 9.4 us -> 7.02 us  [tile_backward_t(): pl.pallas_call(kernel, out_shape=jax.ShapeDtypeStruct((width, src_rows),...]
    unnamed x29 -> x21, local copies, waits for them, and re-layouts: 3.14 us -> 0.82 us
    concatenate x0 -> x2, other arithmetic: none -> 2 us  [the longest x1 1.06 us: body(): back_packed = jnp.concatenate([returning, parts], axis=1)]
    another operation x1 -> x0, other arithmetic: 1.96 us -> none
  transfers between devices with their start and end apart: 6 -> 4, of which waited for: 6 -> 4; matrix products, arithmetic and copies ran while one was open for 21% -> 14% of each run, Pallas kernels for 0% -> 0%
where the time goes in v3:
time: 136 us; the launch traced here: 135 us
  waiting for transfers between devices  53.1 us (39%)
  starting transfers between devices  27.9 us (21%)
  other arithmetic  17.2 us (13%)
  Pallas kernels  13 us (10%)
  local copies, waits for them, and re-layouts  11.5 us (8%)
  matrix products  11.1 us (8%)
  between operations  1.55 us (1%)
    all_to_all x1, waiting for transfers between devices, body(): lax.all_to_all(back_packed, ('dom', 'dev'), split_axis=0, concat_axis=0,...  26.8 us
    all_to_all x1, waiting for transfers between devices, body(): lax.all_to_all(packed, ('dom', 'dev'), split_axis=0, concat_axis=0, tiled...  19.5 us
    all_to_all x1, starting transfers between devices, body(): lax.all_to_all(back_packed, ('dom', 'dev'), split_axis=0, concat_axis=0,...  13.3 us
    all_to_all x1, starting transfers between devices, body(): lax.all_to_all(packed, ('dom', 'dev'), split_axis=0, concat_axis=0, tiled...  7.3 us
    pallas_call x1, Pallas kernels, tile_backward_t(): pl.pallas_call(kernel, out_shape=jax.ShapeDtypeStruct((width, src_rows),...  7.02 us
    pallas_call x1, Pallas kernels, tile_aggregate(): pl.pallas_call(kernel, out_shape=jax.ShapeDtypeStruct((rows, width), jnp....  5.93 us
    all_to_all x1, waiting for transfers between devices, body(): lax.all_to_all(hub_part.astype(jnp.bfloat16).reshape(group, hubs_dev, wid...  5.44 us
    scatter-add x1, other arithmetic, body(): grad.at[send_rows[0].reshape(-1)]  4.27 us
  transfers between devices with their start and end apart: 4, of which 4 were waited for; matrix products, arithmetic and copies ran while one was open for 14% of the time, Pallas kernels for 0%

profile of v3, /device:TPU:0, one launch (start us, length us, event | category | flops | bytes accessed | tf_op | source)
XLA Modules:
  0.0 135.3 jit_solution(8744141251824624359)
XLA Ops:
  0.6 0.0 copy-start
  0.6 0.7 compare_select_fusion.2
  1.3 0.7 iota_compare_fusion
  2.1 0.7 compare_select_fusion
  2.8 0.1 copy.21
  2.9 0.1 reshape.121
  3.0 2.0 %gather_fusion.1 = bf16[32,256]{1,0:T(8,128)(2,1)S(1)} fusion(bf16[2048,256]{1,0:T(8,128)(2,1)} %param.11, s32[1024]{0:T(1024)S(1)} %pad_clamp_fusion), kind=kCustom, calls=%fused_computation.1 | custom fusion | bytes 32896 | tf_op jit(solution)/shard_map/gather | solution.py:145
  4.9 2.9 %gather_fusion = bf16[512,256]{1,0:T(8,128)(2,1)S(1)} fusion(bf16[2048,256]{1,0:T(8,128)(2,1)} %param.11, s32[1024]{0:T(1024)S(1)} %pad_clamp_fusion.1), kind=kCustom, calls=%fused_computation | custom fusion | bytes 526336 | tf_op jit(solution)/shard_map/gather | solution.py:149
  7.9 0.0 copy-done.8
  7.9 0.0 copy-start.1
  7.9 0.0 copy-start.6
  7.9 0.1 broadcast_select_fusion
  8.0 0.1 broadcast_in_dim.45
  8.1 0.9 pad_maximum_fusion.2
  9.0 7.3 %all-to-all-start = ((bf16[32,48,256]{2,1,0:T(8,128)(2,1)}), bf16[32,48,256]{2,1,0:T(8,128)(2,1)S(1)}, u32[]{:S(2)}, u32[]{:S(2)}) async-start(bf16[32,48,256]{2,1,0:T(8,128)(2,1)} %pad_maximum_fusion.2), calls=%async_computation | async-start | bytes 1572864 | tf_op jit(solution)/shard_map/all_to_all | solution.py:151
  17.0 1.8 %fusion.2 = f32[2048,256]{1,0:T(8,128)} fusion(bf16[2048,256]{1,0:T(8,128)(2,1)S(1)} %copy-done.1, bf16[256,256]{1,0:T(8,128)(2,1)S(1)} %copy-done.6), kind=kOutput, calls=%fused_computation.33 | convolution fusion | flops 268435456 | bytes 3276800 | tf_op jit(solution)/shard_map/dot_general | solution.py:160
  18.8 19.5 %all-to-all-done = bf16[32,48,256]{2,1,0:T(8,128)(2,1)S(1)} async-done(((bf16[32,48,256]{2,1,0:T(8,128)(2,1)}), bf16[32,48,256]{2,1,0:T(8,128)(2,1)S(1)}, u32[]{:S(2)}, u32[]{:S(2)}) %all-to-all-start) | async-done | bytes 786464 | tf_op jit(solution)/shard_map/all_to_all | solution.py:151
  38.4 1.2 pad_maximum_fusion.source_ref
  39.6 5.9 %shard_map.138 = bf16[2048,256]{1,0:T(8,128)(2,1)} custom-call(s32[320]{0:T(512)} %src_ref.3, s32[320]{0:T(512)} %dst_ref.3, s32[1]{0:T(128)S(6)} %copy.32.cnt_ref, bf16[320,128,128]{2,1,0:T(8,128)(2,1)} %val_ref.3, bf16[2816,256]{1,0:T(8,128)(2,1)} %pad_maximum_fusion.source_ref), custom_call_target="tpu_custom_call" | custom-call | tf_op jit(solution)/shard_map/pallas_call | solution.py:64
  45.6 3.8 %multiply_convert_fusion = (bf16[2048,256]{1,0:T(8,128)(2,1)S(1)}, bf16[2048,256]{1,0:T(8,128)(2,1)}) fusion(bf16[2048,256]{1,0:T(8,128)(2,1)} %param.14, f32[2048,256]{1,0:T(8,128)S(1)} %copy-done.5, bf16[2048,256]{1,0:T(8,128)(2,1)} %shard_map.138, bf16[256,256]{1,0:T(8,128)(2,1)S(1)} %copy-done), kind=kOutput, calls=%fused_computation.9 | convolution fusion | flops 275251200 | bytes 6422528 | tf_op jit(solution)/shard_map/dot_general | solution.py:160
  49.4 0.5 fusion.3
  49.8 0.5 convolution_bitcast_fusion
  50.4 0.0 copy-done.3
  50.4 1.4 %fusion.daggT_ref = bf16[256,2048]{1,0:T(8,128)(2,1)} fusion(bf16[2048,256]{1,0:T(8,128)(2,1)S(1)} %get-tuple-element.8, bf16[256,256]{1,0:T(8,128)(2,1)S(1)} %copy-done), kind=kOutput, calls=%fused_computation.7 | convolution fusion | flops 268959744 | bytes 2228224 | tf_op jit(solution)/shard_map/dot_general | solution.py:172
  51.8 7.0 %shard_map.139 = f32[256,2816]{1,0:T(8,128)} custom-call(s32[320]{0:T(512)} %src_ref.3, s32[320]{0:T(512)} %dst_ref.3, s32[1]{0:T(128)S(6)} %copy.32.cnt_ref, bf16[320,128,128]{2,1,0:T(8,128)(2,1)} %val_ref.3, bf16[256,2048]{1,0:T(8,128)(2,1)} %fusion.daggT_ref), custom_call_target="tpu_custom_call" | custom-call | tf_op jit(solution)/shard_map/pallas_call | solution.py:113
  58.9 1.1 slice_bitcast_fusion.1
  59.9 0.2 copy.25
  60.2 0.0 copy-start.2
  60.2 1.1 pad_maximum_fusion.1
  61.3 13.3 %all-to-all-start.1 = ((f32[32,32,256]{2,1,0:T(8,128)}), f32[32,32,256]{2,1,0:T(8,128)}, u32[]{:S(2)}, u32[]{:S(2)}) async-start(f32[32,32,256]{2,1,0:T(8,128)} %pad_maximum_fusion.1), calls=%async_computation.1 | async-start | bytes 2097152 | tf_op jit(solution)/shard_map/all_to_all | solution.py:182
  74.6 0.8 copy.27
  75.3 26.8 %all-to-all-done.1 = f32[32,32,256]{2,1,0:T(8,128)} async-done(((f32[32,32,256]{2,1,0:T(8,128)}), f32[32,32,256]{2,1,0:T(8,128)}, u32[]{:S(2)}, u32[]{:S(2)}) %all-to-all-start.1) | async-done | bytes 1048608 | tf_op jit(solution)/shard_map/all_to_all | solution.py:182
  102.1 4.0 %all-to-all-start.2 = ((bf16[8,32,256]{2,1,0:T(8,128)(2,1)}), bf16[8,32,256]{2,1,0:T(8,128)(2,1)}, u32[]{:S(2)}, u32[]{:S(2)}) async-start(bf16[8,32,256]{2,1,0:T(8,128)(2,1)} %bitcast.15), calls=%async_computation.2 | async-start | bytes 262144 | tf_op jit(solution)/shard_map/all_to_all | solution.py:185
  106.1 1.3 slice_reduce_fusion
  107.5 5.4 %all-to-all-done.2 = bf16[8,32,256]{2,1,0:T(8,128)(2,1)} async-done(((bf16[8,32,256]{2,1,0:T(8,128)(2,1)}), bf16[8,32,256]{2,1,0:T(8,128)(2,1)}, u32[]{:S(2)}, u32[]{:S(2)}) %all-to-all-start.2) | async-done | bytes 131104 | tf_op jit(solution)/shard_map/all_to_all | solution.py:185
  112.9 0.8 broadcast_in_dim.47
  113.8 3.3 %all-to-all-start.3 = ((f32[32,16,256]{2,1,0:T(8,128)}), f32[32,16,256]{2,1,0:T(8,128)}, u32[]{:S(2)}, u32[]{:S(2)}) async-start(f32[32,16,256]{2,1,0:T(8,128)} %broadcast_in_dim.47), calls=%async_computation.3 | async-start | bytes 1048576 | tf_op jit(solution)/shard_map/all_to_all | solution.py:197
  117.1 0.8 copy.24
  117.9 0.7 reshape_squeeze.3
  118.5 0.7 compare_select_fusion.1
  119.2 3.0 %convolution_add_fusion = f32[2048,256]{0,1:T(8,128)} fusion(bf16[2048,256]{1,0:T(8,128)(2,1)} %copy-done.3, bf16[256,256]{1,0:T(8,128)(2,1)} %param.12, f32[256,2816]{1,0:T(8,128)S(1)} %copy-done.2), kind=kOutput, calls=%fused_computation.4 | convolution fusion | flops 268959744 | bytes 5373952 | tf_op jit(solution)/shard_map/dot_general | solution.py:193
  122.3 1.9 %copy.26 = f32[2048,256]{1,0:T(8,128)S(1)} copy(f32[2048,256]{0,1:T(8,128)} %convolution_add_fusion) | data formatting | bytes 4194304 | tf_op jit(solution)/shard_map/add | solution.py:193
  124.2 0.9 convert_reduce_fusion
  125.1 4.3 %scatter_fusion = f32[2048,256]{1,0:T(8,128)S(1)} fusion(f32[2048,256]{1,0:T(8,128)S(1)} %copy.26, s32[512]{0:T(512)S(1)} %bitcast.49, f32[512,256]{1,0:T(8,128)S(1)} %bitcast.41), kind=kCustom, calls=%fused_computation.2 | custom fusion | flops 131072 | bytes 1574912 | tf_op jit(solution)/shard_map/scatter-add | solution.py:194
  129.4 1.5 %scatter_fusion.1 = f32[2048,256]{1,0:T(8,128)S(1)} fusion(f32[2048,256]{1,0:T(8,128)S(1)} %scatter_fusion, s32[32]{0:T(128)S(1)} %copy-done.9, f32[32,256]{1,0:T(8,128)S(1)} %convert_reduce_fusion), kind=kCustom, calls=%fused_computation.3 | custom fusion | flops 8192 | bytes 98432 | tf_op jit(solution)/shard_map/scatter-add | solution.py:195
  131.0 1.1 convert_element_type.31
  132.0 1.4 %all-to-all-done.3 = f32[32,16,256]{2,1,0:T(8,128)} async-done(((f32[32,16,256]{2,1,0:T(8,128)}), f32[32,16,256]{2,1,0:T(8,128)}, u32[]{:S(2)}, u32[]{:S(2)}) %all-to-all-start.3) | async-done | bytes 524320 | tf_op jit(solution)/shard_map/all_to_all | solution.py:197
  133.4 1.9 %slice_multiply_fusion = (f32[16,16,256]{2,1,0:T(8,128)}, f32[16,16,256]{2,1,0:T(8,128)}) fusion(f32[32,16,256]{2,1,0:T(8,128)} %all-to-all-done.3), kind=kLoop, calls=%fused_computation.20 | loop fusion | flops 131072 | bytes 1048576 | tf_op jit(solution)/shard_map/mul | solution.py:201
  (21 shorter events, 0.2 us)
Async XLA Ops:
  0.6 44.9 %copy-start = (bf16[256,256]{1,0:T(8,128)(2,1)S(1)}, bf16[256,256]{1,0:T(8,128)(2,1)}, u32[]{:S(2)}) copy-start(bf16[256,256]{1,0:T(8,128)(2,1)} %param.13) | copy-start | bytes 393220
  1.3 6.5 %copy-start.8 = (s32[32]{0:T(128)}, s32[32]{0:T(128)S(1)}, u32[]{:S(2)}) copy-start(s32[32]{0:T(128)S(1)} %compare_select_fusion.2) | copy-start | bytes 388
  2.1 7.0 %copy-start.7 = (pred[32,16]{1,0:T(8,128)(4,1)}, pred[32,16]{1,0:T(8,128)(4,1)S(1)}, u32[]{:S(2)}) copy-start(pred[32,16]{1,0:T(8,128)(4,1)S(1)} %iota_compare_fusion) | copy-start | bytes 1540
  7.9 9.1 %copy-start.1 = (bf16[2048,256]{1,0:T(8,128)(2,1)S(1)}, bf16[2048,256]{1,0:T(8,128)(2,1)}, u32[]{:S(2)}) copy-start(bf16[2048,256]{1,0:T(8,128)(2,1)} %param.11) | copy-start | bytes 3145732
  7.9 9.1 %copy-start.6 = (bf16[256,256]{1,0:T(8,128)(2,1)S(1)}, bf16[256,256]{1,0:T(8,128)(2,1)}, u32[]{:S(2)}) copy-start(bf16[256,256]{1,0:T(8,128)(2,1)} %param.12) | copy-start | bytes 393220
  9.0 29.3 %all-to-all-start = ((bf16[32,48,256]{2,1,0:T(8,128)(2,1)}), bf16[32,48,256]{2,1,0:T(8,128)(2,1)S(1)}, u32[]{:S(2)}, u32[]{:S(2)}) async-start(bf16[32,48,256]{2,1,0:T(8,128)(2,1)} %pad_maximum_fusion.2), calls=%async_computation | async-start | bytes 1572864 | tf_op jit(solution)/shard_map/all_to_all | solution.py:151
  39.6 5.9 %copy-start.5 = (f32[2048,256]{1,0:T(8,128)S(1)}, f32[2048,256]{1,0:T(8,128)}, u32[]{:S(2)}) copy-start(f32[2048,256]{1,0:T(8,128)} %fusion.2) | copy-start | bytes 6291460
  45.5 3.8 %copy-start.4 = (bf16[2048,256]{1,0:T(8,128)(2,1)S(1)}, bf16[2048,256]{1,0:T(8,128)(2,1)}, u32[]{:S(2)}) copy-start(bf16[2048,256]{1,0:T(8,128)(2,1)} %shard_map.138) | copy-start | bytes 3145732
  49.4 1.0 copy-start.3
  60.2 14.4 %copy-start.2 = (f32[256,2816]{1,0:T(8,128)S(1)}, f32[256,2816]{1,0:T(8,128)}, u32[]{:S(2)}) copy-start(f32[256,2816]{1,0:T(8,128)} %shard_map.139) | copy-start | bytes 8650756
  61.3 40.8 %all-to-all-start.1 = ((f32[32,32,256]{2,1,0:T(8,128)}), f32[32,32,256]{2,1,0:T(8,128)}, u32[]{:S(2)}, u32[]{:S(2)}) async-start(f32[32,32,256]{2,1,0:T(8,128)} %pad_maximum_fusion.1), calls=%async_computation.1 | async-start | bytes 2097152 | tf_op jit(solution)/shard_map/all_to_all | solution.py:182
  102.1 10.8 %all-to-all-start.2 = ((bf16[8,32,256]{2,1,0:T(8,128)(2,1)}), bf16[8,32,256]{2,1,0:T(8,128)(2,1)}, u32[]{:S(2)}, u32[]{:S(2)}) async-start(bf16[8,32,256]{2,1,0:T(8,128)(2,1)} %bitcast.15), calls=%async_computation.2 | async-start | bytes 262144 | tf_op jit(solution)/shard_map/all_to_all | solution.py:185
  113.8 19.7 %all-to-all-start.3 = ((f32[32,16,256]{2,1,0:T(8,128)}), f32[32,16,256]{2,1,0:T(8,128)}, u32[]{:S(2)}, u32[]{:S(2)}) async-start(f32[32,16,256]{2,1,0:T(8,128)} %broadcast_in_dim.47), calls=%async_computation.3 | async-start | bytes 1048576 | tf_op jit(solution)/shard_map/all_to_all | solution.py:197
  125.1 4.3 %copy-start.9 = (s32[32]{0:T(128)S(1)}, s32[32]{0:T(128)}, u32[]{:S(2)}) copy-start(s32[32]{0:T(128)} %copy-done.8) | copy-start | bytes 388

commit v4 on v2

--- a/solution.py
+++ b/solution.py
@@ -165,16 +165,6 @@
     contract_rows = (((0,), (0,)), ((), ()))
     local_ws = lax.dot_general(feats, dpre, contract_rows, preferred_element_type=jnp.float32)
     local_wn = lax.dot_general(agg, dpre, contract_rows, preferred_element_type=jnp.float32)
-    partial = jnp.concatenate([local_ws, local_wn], axis=0)
-    parts = partial.reshape(peers, -1, width)
-    gathered = lax.all_to_all(parts, ("dom", "dev"), split_axis=0, concat_axis=0, tiled=True)
-    piece = jnp.sum(gathered, axis=0)
-    spread_piece = jnp.broadcast_to(piece[None], (peers,) + piece.shape)
-    summed = lax.all_to_all(spread_piece, ("dom", "dev"), split_axis=0, concat_axis=0, tiled=True)
-    summed = summed.reshape(partial.shape)
-    scale = 1.0 / jnp.sqrt(jnp.float32(rows * peers))
-    grad_ws = summed[: w_self.shape[0]] * scale
-    grad_wn = summed[w_self.shape[0] :] * scale
 
     contract_cols = (((1,), (1,)), ((), ()))
     dagg_t = lax.dot_general(w_neigh, dpre, contract_cols, preferred_element_type=jnp.float32).astype(
@@ -188,6 +178,17 @@
         returning.astype(jnp.bfloat16), ("dom", "dev"), split_axis=0, concat_axis=0, tiled=True
     ).astype(jnp.float32)
     returned = jnp.where(live[:, :, None], returned, jnp.float32(0.0))
+    partial = jnp.concatenate([local_ws, local_wn], axis=0)
+    partial, returned = lax.optimization_barrier((partial, returned))
+    parts = partial.reshape(peers, -1, width)
+    gathered = lax.all_to_all(parts, ("dom", "dev"), split_axis=0, concat_axis=0, tiled=True)
+    scale = 1.0 / jnp.sqrt(jnp.float32(rows * peers))
+    piece = (jnp.sum(gathered, axis=0) * scale).astype(jnp.bfloat16)
+    spread_piece = jnp.broadcast_to(piece[None], (peers,) + piece.shape)
+    summed = lax.all_to_all(spread_piece, ("dom", "dev"), split_axis=0, concat_axis=0, tiled=True)
+    summed = summed.reshape(partial.shape).astype(jnp.float32)
+    grad_ws = summed[: w_self.shape[0]]
+    grad_wn = summed[w_self.shape[0] :]
     hub_back = lax.all_to_all(
         hub_part.astype(jnp.bfloat16).reshape(group, hubs_dev, width),
         "dev",

time: 133 us -> 131 us (0.985)
  Pallas kernels: 16.9 us -> 24.9 us
  starting transfers between devices: 30.1 us -> 22.8 us
  waiting for transfers between devices: 39 us -> 36.3 us
    all_to_all x1, starting transfers between devices: 9.61 us -> 4 us  [body(): lax.all_to_all(hub_part.astype(jnp.bfloat16).reshape(group, hubs_dev, wid...]
    pallas_call x1, Pallas kernels: 9.4 us -> 14.2 us  [tile_backward_t(): pl.pallas_call(kernel, out_shape=jax.ShapeDtypeStruct((width, src_rows),...]
    pallas_call x1, Pallas kernels: 7.46 us -> 10.7 us  [tile_aggregate(): pl.pallas_call(kernel, out_shape=jax.ShapeDtypeStruct((rows, width), jnp....]
    convert_element_type x2, local copies, waits for them, and re-layouts: 3.61 us -> 0.86 us  [body(): returning.astype(jnp.bfloat16)]
    convert_element_type x2, local copies, waits for them, and re-layouts: 0.77 us -> 3.23 us  [body(): hub_part.astype(jnp.bfloat16).reshape(group, hubs_dev, width)]
    all_to_all x1, waiting for transfers between devices: 10.3 us -> 8.51 us  [body(): lax.all_to_all(returning.astype(jnp.bfloat16), ('dom', 'dev'), split_axis...]
    unnamed x29 -> x23, local copies, waits for them, and re-layouts: 3.14 us -> 2.51 us
  transfers between devices with their start and end apart: 6 -> 6, of which waited for: 6 -> 5; matrix products, arithmetic and copies ran while one was open for 21% -> 21% of each run, Pallas kernels for 0% -> 0%
where the time goes in v4:
time: 131 us; the launch traced here: 130 us
  waiting for transfers between devices  36.3 us (28%)
  Pallas kernels  24.9 us (19%)
  starting transfers between devices  22.8 us (17%)
  other arithmetic  16.6 us (13%)
  local copies, waits for them, and re-layouts  16.5 us (13%)
  matrix products  11.3 us (9%)
  between operations  1.49 us (1%)
    pallas_call x1, Pallas kernels, tile_backward_t(): pl.pallas_call(kernel, out_shape=jax.ShapeDtypeStruct((width, src_rows),...  14.2 us
    all_to_all x1, waiting for transfers between devices, body(): lax.all_to_all(parts, ('dom', 'dev'), split_axis=0, concat_axis=0, tiled=...  13.1 us
    pallas_call x1, Pallas kernels, tile_aggregate(): pl.pallas_call(kernel, out_shape=jax.ShapeDtypeStruct((rows, width), jnp....  10.7 us
    all_to_all x1, waiting for transfers between devices, body(): lax.all_to_all(returning.astype(jnp.bfloat16), ('dom', 'dev'), split_axis...  8.51 us
    all_to_all x1, waiting for transfers between devices, body(): lax.all_to_all(outgoing, ('dom', 'dev'), split_axis=0, concat_axis=0, til...  7.96 us
    all_to_all x1, starting transfers between devices, body(): lax.all_to_all(hub_out, 'dev', split_axis=0, concat_axis=0, tiled=True)  6.33 us
    all_to_all x1, waiting for transfers between devices, body(): lax.all_to_all(hub_part.astype(jnp.bfloat16).reshape(group, hubs_dev, wid...  5.28 us
    all_to_all x1, starting transfers between devices, body(): lax.all_to_all(outgoing, ('dom', 'dev'), split_axis=0, concat_axis=0, til...  4.66 us
  transfers between devices with their start and end apart: 6, of which 5 were waited for; matrix products, arithmetic and copies ran while one was open for 21% of the time, Pallas kernels for 0%

profile of v4, /device:TPU:0, one launch (start us, length us, event | category | flops | bytes accessed | tf_op | source)
XLA Modules:
  0.0 129.9 jit_solution(9322285421428282877)
XLA Ops:
  0.6 0.0 copy-start
  0.7 0.8 compare_select_fusion.2
  1.4 0.6 copy-done.8
  2.0 2.0 %gather_fusion.1 = bf16[32,256]{1,0:T(8,128)(2,1)S(1)} fusion(bf16[2048,256]{1,0:T(8,128)(2,1)} %param.11, s32[1024]{0:T(1024)S(1)} %pad_clamp_fusion), kind=kCustom, calls=%fused_computation.1 | custom fusion | bytes 32896 | tf_op jit(solution)/shard_map/gather | solution.py:145
  4.0 0.7 broadcast_in_dim.45
  4.7 6.3 %all-to-all-start.1 = ((bf16[8,32,256]{2,1,0:T(8,128)(2,1)}), bf16[8,32,256]{2,1,0:T(8,128)(2,1)S(1)}, u32[]{:S(2)}, u32[]{:S(2)}) async-start(bf16[8,32,256]{2,1,0:T(8,128)(2,1)} %broadcast_in_dim.45), calls=%async_computation.1 | async-start | bytes 262144 | tf_op jit(solution)/shard_map/all_to_all | solution.py:147
  11.0 0.7 iota_compare_fusion
  11.7 0.7 compare_select_fusion
  12.4 0.1 copy.20
  12.5 0.1 reshape.119
  12.6 2.9 %gather_fusion = bf16[512,256]{1,0:T(8,128)(2,1)S(1)} fusion(bf16[2048,256]{1,0:T(8,128)(2,1)} %param.11, s32[1024]{0:T(1024)S(1)} %pad_clamp_fusion.1), kind=kCustom, calls=%fused_computation | custom fusion | bytes 526336 | tf_op jit(solution)/shard_map/gather | solution.py:151
  15.5 0.8 broadcast_select_fusion
  16.4 1.4 %all-to-all-done.1 = bf16[8,32,256]{2,1,0:T(8,128)(2,1)S(1)} async-done(((bf16[8,32,256]{2,1,0:T(8,128)(2,1)}), bf16[8,32,256]{2,1,0:T(8,128)(2,1)S(1)}, u32[]{:S(2)}, u32[]{:S(2)}) %all-to-all-start.1) | async-done | bytes 131104 | tf_op jit(solution)/shard_map/all_to_all | solution.py:147
  17.8 4.7 %all-to-all-start = ((bf16[32,16,256]{2,1,0:T(8,128)(2,1)}), bf16[32,16,256]{2,1,0:T(8,128)(2,1)S(1)}, u32[]{:S(2)}, u32[]{:S(2)}) async-start(bf16[32,16,256]{2,1,0:T(8,128)(2,1)} %broadcast_select_fusion), calls=%async_computation | async-start | bytes 524288 | tf_op jit(solution)/shard_map/all_to_all | solution.py:152
  23.1 1.8 %fusion.2 = f32[2048,256]{1,0:T(8,128)} fusion(bf16[2048,256]{1,0:T(8,128)(2,1)S(1)} %copy-done.2, bf16[256,256]{1,0:T(8,128)(2,1)S(1)} %copy-done.7), kind=kOutput, calls=%fused_computation.28 | convolution fusion | flops 268435456 | bytes 3276800 | tf_op jit(solution)/shard_map/dot_general | solution.py:158
  24.9 8.0 %all-to-all-done = bf16[32,16,256]{2,1,0:T(8,128)(2,1)S(1)} async-done(((bf16[32,16,256]{2,1,0:T(8,128)(2,1)}), bf16[32,16,256]{2,1,0:T(8,128)(2,1)S(1)}, u32[]{:S(2)}, u32[]{:S(2)}) %all-to-all-start) | async-done | bytes 262176 | tf_op jit(solution)/shard_map/all_to_all | solution.py:152
  32.8 1.2 pad_maximum_fusion.source_ref
  34.0 10.7 %shard_map.138 = bf16[2048,256]{1,0:T(8,128)(2,1)} custom-call(s32[320]{0:T(512)} %src_ref.3, s32[320]{0:T(512)} %dst_ref.3, s32[1]{0:T(128)S(6)} %copy.31.cnt_ref, bf16[320,128,128]{2,1,0:T(8,128)(2,1)} %val_ref.3, bf16[2816,256]{1,0:T(8,128)(2,1)} %pad_maximum_fusion.source_ref), custom_call_target="tpu_custom_call" | custom-call | tf_op jit(solution)/shard_map/pallas_call | solution.py:64
  44.7 4.1 %multiply_convert_fusion = (bf16[2048,256]{1,0:T(8,128)(2,1)S(1)}, bf16[2048,256]{1,0:T(8,128)(2,1)}) fusion(bf16[2048,256]{1,0:T(8,128)(2,1)S(1)} %copy-done.10, f32[2048,256]{1,0:T(8,128)} %fusion.2, bf16[2048,256]{1,0:T(8,128)(2,1)} %shard_map.138, bf16[256,256]{1,0:T(8,128)(2,1)S(1)} %copy-done), kind=kOutput, calls=%fused_computation.9 | convolution fusion | flops 275251200 | bytes 6422528 | tf_op jit(solution)/shard_map/dot_general | solution.py:158
  48.8 1.4 %fusion.daggT_ref = bf16[256,2048]{1,0:T(8,128)(2,1)} fusion(bf16[2048,256]{1,0:T(8,128)(2,1)S(1)} %get-tuple-element.12, bf16[256,256]{1,0:T(8,128)(2,1)S(1)} %copy-done), kind=kOutput, calls=%fused_computation.7 | convolution fusion | flops 268959744 | bytes 2228224 | tf_op jit(solution)/shard_map/dot_general | solution.py:170
  50.3 14.2 %shard_map.139 = f32[256,2816]{1,0:T(8,128)} custom-call(s32[320]{0:T(512)} %src_ref.3, s32[320]{0:T(512)} %dst_ref.3, s32[1]{0:T(128)S(6)} %copy.31.cnt_ref, bf16[320,128,128]{2,1,0:T(8,128)(2,1)} %val_ref.3, bf16[256,2048]{1,0:T(8,128)(2,1)} %fusion.daggT_ref), custom_call_target="tpu_custom_call" | custom-call | tf_op jit(solution)/shard_map/pallas_call | solution.py:113
  64.4 2.0 %convert.4 = bf16[256,2816]{1,0:T(8,128)(2,1)S(1)} convert(f32[256,2816]{1,0:T(8,128)} %shard_map.139) | non-fusion elementwise | flops 720896 | bytes 4325376 | tf_op jit(solution)/shard_map/convert.1
  66.5 1.1 copy-done.5
  67.6 0.8 copy.24
  68.5 2.6 %all-to-all-start.2 = ((bf16[32,16,256]{2,1,0:T(8,128)(2,1)}), bf16[32,16,256]{2,1,0:T(8,128)(2,1)S(1)}, u32[]{:S(2)}, u32[]{:S(2)}) async-start(bf16[32,16,256]{2,1,0:T(8,128)(2,1)} %bitcast.42), calls=%async_computation.2 | async-start | bytes 524288 | tf_op jit(solution)/shard_map/all_to_all | solution.py:177
  71.1 0.5 fusion.3
  71.6 0.5 convolution_bitcast_fusion
  72.1 0.8 pad_maximum_fusion.1
  72.9 8.5 %all-to-all-done.2 = bf16[32,16,256]{2,1,0:T(8,128)(2,1)S(1)} async-done(((bf16[32,16,256]{2,1,0:T(8,128)(2,1)}), bf16[32,16,256]{2,1,0:T(8,128)(2,1)S(1)}, u32[]{:S(2)}, u32[]{:S(2)}) %all-to-all-start.2) | async-done | bytes 262176 | tf_op jit(solution)/shard_map/all_to_all | solution.py:177
  81.4 0.9 convert_select_fusion
  82.4 2.6 %all-to-all-start.4 = ((f32[32,16,256]{2,1,0:T(8,128)}), f32[32,16,256]{2,1,0:T(8,128)S(1)}, u32[]{:S(2)}, u32[]{:S(2)}) async-start(f32[32,16,256]{2,1,0:T(8,128)} %bitcast.40), calls=%async_computation.4 | async-start | bytes 1048576 | tf_op jit(solution)/shard_map/all_to_all | solution.py:184
  85.0 1.6 %slice_bitcast_fusion.2 = bf16[256,256]{0,1:T(8,128)(2,1)} fusion(bf16[256,2816]{1,0:T(8,128)(2,1)} %copy-done.5), kind=kLoop, calls=%fused_computation.19 | loop fusion | bytes 262144 | tf_op jit(solution)/shard_map/convert_element_type | solution.py:193
  86.6 1.7 %copy.26 = bf16[256,256]{1,0:T(8,128)(2,1)} copy(bf16[256,256]{0,1:T(8,128)(2,1)} %slice_bitcast_fusion.2) | data formatting | bytes 262144 | tf_op jit(solution)/shard_map/convert_element_type | solution.py:193
  88.2 13.1 %all-to-all-done.4 = f32[32,16,256]{2,1,0:T(8,128)S(1)} async-done(((f32[32,16,256]{2,1,0:T(8,128)}), f32[32,16,256]{2,1,0:T(8,128)S(1)}, u32[]{:S(2)}, u32[]{:S(2)}) %all-to-all-start.4) | async-done | bytes 524320 | tf_op jit(solution)/shard_map/all_to_all | solution.py:184
  101.3 4.0 %all-to-all-start.3 = ((bf16[8,32,256]{2,1,0:T(8,128)(2,1)}), bf16[8,32,256]{2,1,0:T(8,128)(2,1)}, u32[]{:S(2)}, u32[]{:S(2)}) async-start(bf16[8,32,256]{2,1,0:T(8,128)(2,1)} %bitcast.45), calls=%async_computation.3 | async-start | bytes 262144 | tf_op jit(solution)/shard_map/all_to_all | solution.py:192
  105.3 0.8 copy.23
  106.1 0.7 reshape_squeeze.3
  106.9 5.3 %all-to-all-done.3 = bf16[8,32,256]{2,1,0:T(8,128)(2,1)} async-done(((bf16[8,32,256]{2,1,0:T(8,128)(2,1)}), bf16[8,32,256]{2,1,0:T(8,128)(2,1)}, u32[]{:S(2)}, u32[]{:S(2)}) %all-to-all-start.3) | async-done | bytes 131104 | tf_op jit(solution)/shard_map/all_to_all | solution.py:192
  112.1 0.7 broadcast_in_dim.47
  112.9 2.6 %all-to-all-start.5 = ((bf16[32,16,256]{2,1,0:T(8,128)(2,1)}), bf16[32,16,256]{2,1,0:T(8,128)(2,1)S(1)}, u32[]{:S(2)}, u32[]{:S(2)}) async-start(bf16[32,16,256]{2,1,0:T(8,128)(2,1)} %broadcast_in_dim.47), calls=%async_computation.5 | async-start | bytes 524288 | tf_op jit(solution)/shard_map/all_to_all | solution.py:188
  115.5 0.7 compare_select_fusion.1
  116.1 3.0 %convolution_add_fusion = f32[2048,256]{0,1:T(8,128)} fusion(bf16[2048,256]{1,0:T(8,128)(2,1)} %copy-done.3, bf16[256,256]{1,0:T(8,128)(2,1)} %param.12, f32[256,2816]{1,0:T(8,128)S(1)} %copy-done.1), kind=kOutput, calls=%fused_computation.4 | convolution fusion | flops 268959744 | bytes 5373952 | tf_op jit(solution)/shard_map/dot_general | solution.py:200
  119.2 2.0 %copy.25 = f32[2048,256]{1,0:T(8,128)S(1)} copy(f32[2048,256]{0,1:T(8,128)} %convolution_add_fusion) | data formatting | bytes 4194304 | tf_op jit(solution)/shard_map/add | solution.py:200
  121.2 0.9 convert_reduce_fusion
  122.1 4.3 %scatter_fusion = f32[2048,256]{1,0:T(8,128)S(1)} fusion(f32[2048,256]{1,0:T(8,128)S(1)} %copy.25, s32[512]{0:T(512)S(1)} %bitcast.48, f32[512,256]{1,0:T(8,128)S(1)} %bitcast.39), kind=kCustom, calls=%fused_computation.2 | custom fusion | flops 131072 | bytes 1574912 | tf_op jit(solution)/shard_map/scatter-add | solution.py:201
  126.4 1.5 %scatter_fusion.1 = f32[2048,256]{1,0:T(8,128)S(1)} fusion(f32[2048,256]{1,0:T(8,128)S(1)} %scatter_fusion, s32[32]{0:T(128)S(1)} %copy-done.9, f32[32,256]{1,0:T(8,128)S(1)} %convert_reduce_fusion), kind=kCustom, calls=%fused_computation.3 | custom fusion | flops 8192 | bytes 98432 | tf_op jit(solution)/shard_map/scatter-add | solution.py:202
  127.9 1.1 convert_element_type.55
  129.0 0.8 fusion.1
  (25 shorter events, 0.1 us)
Async XLA Ops:
  0.6 44.1 %copy-start = (bf16[256,256]{1,0:T(8,128)(2,1)S(1)}, bf16[256,256]{1,0:T(8,128)(2,1)}, u32[]{:S(2)}) copy-start(bf16[256,256]{1,0:T(8,128)(2,1)} %param.13) | copy-start | bytes 393220
  0.6 22.4 %copy-start.2 = (bf16[2048,256]{1,0:T(8,128)(2,1)S(1)}, bf16[2048,256]{1,0:T(8,128)(2,1)}, u32[]{:S(2)}) copy-start(bf16[2048,256]{1,0:T(8,128)(2,1)} %param.11) | copy-start | bytes 3145732
  0.7 22.4 %copy-start.7 = (bf16[256,256]{1,0:T(8,128)(2,1)S(1)}, bf16[256,256]{1,0:T(8,128)(2,1)}, u32[]{:S(2)}) copy-start(bf16[256,256]{1,0:T(8,128)(2,1)} %param.12) | copy-start | bytes 393220
  1.4 0.6 copy-start.8
  4.7 13.1 %all-to-all-start.1 = ((bf16[8,32,256]{2,1,0:T(8,128)(2,1)}), bf16[8,32,256]{2,1,0:T(8,128)(2,1)S(1)}, u32[]{:S(2)}, u32[]{:S(2)}) async-start(bf16[8,32,256]{2,1,0:T(8,128)(2,1)} %broadcast_in_dim.45), calls=%async_computation.1 | async-start | bytes 262144 | tf_op jit(solution)/shard_map/all_to_all | solution.py:147
  17.8 15.1 %all-to-all-start = ((bf16[32,16,256]{2,1,0:T(8,128)(2,1)}), bf16[32,16,256]{2,1,0:T(8,128)(2,1)S(1)}, u32[]{:S(2)}, u32[]{:S(2)}) async-start(bf16[32,16,256]{2,1,0:T(8,128)(2,1)} %broadcast_select_fusion), calls=%async_computation | async-start | bytes 524288 | tf_op jit(solution)/shard_map/all_to_all | solution.py:152
  34.0 10.7 %copy-start.10 = (bf16[2048,256]{1,0:T(8,128)(2,1)S(1)}, bf16[2048,256]{1,0:T(8,128)(2,1)}, u32[]{:S(2)}) copy-start(bf16[2048,256]{1,0:T(8,128)(2,1)} %param.14) | copy-start | bytes 3145732
  48.8 22.7 %copy-start.3 = (bf16[2048,256]{1,0:T(8,128)(2,1)}, bf16[2048,256]{1,0:T(8,128)(2,1)S(1)}, u32[]{:S(2)}) copy-start(bf16[2048,256]{1,0:T(8,128)(2,1)S(1)} %get-tuple-element.12) | copy-start | bytes 3145732
  64.4 6.6 %copy-start.4 = (bf16[2048,256]{1,0:T(8,128)(2,1)S(1)}, bf16[2048,256]{1,0:T(8,128)(2,1)}, u32[]{:S(2)}) copy-start(bf16[2048,256]{1,0:T(8,128)(2,1)} %shard_map.138) | copy-start | bytes 3145732
  66.5 1.1 copy-start.5
  68.5 13.0 %all-to-all-start.2 = ((bf16[32,16,256]{2,1,0:T(8,128)(2,1)}), bf16[32,16,256]{2,1,0:T(8,128)(2,1)S(1)}, u32[]{:S(2)}, u32[]{:S(2)}) async-start(bf16[32,16,256]{2,1,0:T(8,128)(2,1)} %bitcast.42), calls=%async_computation.2 | async-start | bytes 524288 | tf_op jit(solution)/shard_map/all_to_all | solution.py:177
  72.9 43.2 %copy-start.1 = (f32[256,2816]{1,0:T(8,128)S(1)}, f32[256,2816]{1,0:T(8,128)}, u32[]{:S(2)}) copy-start(f32[256,2816]{1,0:T(8,128)} %shard_map.139) | copy-start | bytes 8650756
  82.4 19.0 %all-to-all-start.4 = ((f32[32,16,256]{2,1,0:T(8,128)}), f32[32,16,256]{2,1,0:T(8,128)S(1)}, u32[]{:S(2)}, u32[]{:S(2)}) async-start(f32[32,16,256]{2,1,0:T(8,128)} %bitcast.40), calls=%async_computation.4 | async-start | bytes 1048576 | tf_op jit(solution)/shard_map/all_to_all | solution.py:184
  101.3 10.8 %all-to-all-start.3 = ((bf16[8,32,256]{2,1,0:T(8,128)(2,1)}), bf16[8,32,256]{2,1,0:T(8,128)(2,1)}, u32[]{:S(2)}, u32[]{:S(2)}) async-start(bf16[8,32,256]{2,1,0:T(8,128)(2,1)} %bitcast.45), calls=%async_computation.3 | async-start | bytes 262144 | tf_op jit(solution)/shard_map/all_to_all | solution.py:192
  112.9 16.2 %all-to-all-start.5 = ((bf16[32,16,256]{2,1,0:T(8,128)(2,1)}), bf16[32,16,256]{2,1,0:T(8,128)(2,1)S(1)}, u32[]{:S(2)}, u32[]{:S(2)}) async-start(bf16[32,16,256]{2,1,0:T(8,128)(2,1)} %broadcast_in_dim.47), calls=%async_computation.5 | async-start | bytes 524288 | tf_op jit(solution)/shard_map/all_to_all | solution.py:188
  119.2 2.9 %copy-start.6 = (f32[32,16,256]{2,1,0:T(8,128)S(1)}, f32[32,16,256]{2,1,0:T(8,128)}, u32[]{:S(2)}) copy-start(f32[32,16,256]{2,1,0:T(8,128)} %convert_select_fusion) | copy-start | bytes 1572868
  122.1 4.3 %copy-start.9 = (s32[32]{0:T(128)S(1)}, s32[32]{0:T(128)}, u32[]{:S(2)}) copy-start(s32[32]{0:T(128)} %copy-done.8) | copy-start | bytes 388

commit v5 on v4

--- a/solution.py
+++ b/solution.py
@@ -120,6 +120,11 @@
             out_specs=pl.BlockSpec((width, src_rows), lambda i, s, d, c: (0, 0))),
         compiler_params=pltpu.CompilerParams(dimension_semantics=("arbitrary",)),
     )(tile_src, tile_dst, tile_count, tile_val, daggT)
+
+
+def one_hot_rows(index, count):
+    columns = lax.broadcasted_iota(jnp.int32, (index.shape[0], count), 1)
+    return (columns == index[:, None]).astype(jnp.bfloat16)
 
 
 def body(
@@ -142,13 +147,17 @@
     group = lax.axis_size("dev")
     hubs_dev = hub_rows.shape[0]
 
-    own_hubs = feats[hub_rows]
+    hub_pick = one_hot_rows(hub_rows, rows)
+    own_hubs = jnp.dot(hub_pick, feats, preferred_element_type=jnp.float32).astype(jnp.bfloat16)
     hub_out = jnp.broadcast_to(own_hubs[None], (group, hubs_dev, width))
     hub_table = lax.all_to_all(hub_out, "dev", split_axis=0, concat_axis=0, tiled=True)
     hub_table = hub_table.reshape(group * hubs_dev, width)
 
     live = lax.broadcasted_iota(jnp.int32, (peers, slots), 1) < send_count[0][:, None]
-    outgoing = jnp.where(live[:, :, None], feats[send_rows[0]], jnp.zeros((), jnp.bfloat16))
+    send_pick = one_hot_rows(send_rows[0].reshape(-1), rows)
+    send_pick = jnp.where(live.reshape(-1, 1), send_pick, jnp.zeros((), jnp.bfloat16))
+    outgoing = jnp.dot(send_pick, feats, preferred_element_type=jnp.float32).astype(jnp.bfloat16)
+    outgoing = outgoing.reshape(peers, slots, width)
     incoming = lax.all_to_all(outgoing, ("dom", "dev"), split_axis=0, concat_axis=0, tiled=True)
     source = jnp.concatenate([feats, incoming.reshape(peers * slots, width), hub_table], axis=0)
 
@@ -176,8 +185,7 @@
     hub_part = dsource_t[:, rows + peers * slots :].T
     returned = lax.all_to_all(
         returning.astype(jnp.bfloat16), ("dom", "dev"), split_axis=0, concat_axis=0, tiled=True
-    ).astype(jnp.float32)
-    returned = jnp.where(live[:, :, None], returned, jnp.float32(0.0))
+    )
     partial = jnp.concatenate([local_ws, local_wn], axis=0)
     partial, returned = lax.optimization_barrier((partial, returned))
     parts = partial.reshape(peers, -1, width)
@@ -196,10 +204,17 @@
         concat_axis=0,
         tiled=True,
     )
-    hub_back = jnp.sum(hub_back.astype(jnp.float32), axis=0)
+    hub_spread = jnp.broadcast_to(hub_pick[None], (group,) + hub_pick.shape)
     grad = lax.dot_general(dpre, w_self, contract_cols, preferred_element_type=jnp.float32) + own
-    grad = grad.at[send_rows[0].reshape(-1)].add(returned.reshape(peers * slots, width))
-    grad = grad.at[hub_rows].add(hub_back)
+    grad = grad + lax.dot_general(
+        send_pick, returned.reshape(peers * slots, width), contract_rows, preferred_element_type=jnp.float32
+    )
+    grad = grad + lax.dot_general(
+        hub_spread.reshape(group * hubs_dev, rows),
+        hub_back.reshape(group * hubs_dev, width),
+        contract_rows,
+        preferred_element_type=jnp.float32,
+    )
     return (out, grad.astype(jnp.bfloat16), grad_ws, grad_wn)
 
 

time: 131 us -> 124 us (0.947)
  Pallas kernels: 24.9 us -> 13 us
  other arithmetic: 16.6 us -> 5.64 us
  starting transfers between devices: 22.8 us -> 33.7 us
  matrix products: 11.3 us -> 19.2 us
  local copies, waits for them, and re-layouts: 16.5 us -> 10.4 us
  waiting for transfers between devices: 36.3 us -> 40.4 us
    all_to_all x1, starting transfers between devices: 2.59 us -> 14.4 us  [body(): lax.all_to_all(returning.astype(jnp.bfloat16), ('dom', 'dev'), split_axis...]
    dot_general x0 -> x4, matrix products: none -> 7.81 us  [the longest x1 2.79 us: body(): jnp.dot(send_pick, feats, preferred_element_type=jnp.float32)]
    pallas_call x1, Pallas kernels: 14.2 us -> 7.03 us  [tile_backward_t(): pl.pallas_call(kernel, out_shape=jax.ShapeDtypeStruct((width, src_rows),...]
    scatter-add x2 -> x0, other arithmetic: 5.82 us -> none  [the longest x1 4.27 us: body(): grad.at[send_rows[0].reshape(-1)]]
    all_to_all x1, waiting for transfers between devices: 0.01 us -> 5.62 us  [body(): lax.all_to_all(spread_piece, ('dom', 'dev'), split_axis=0, concat_axis=0,...]
    gather x2 -> x0, local copies, waits for them, and re-layouts: 4.89 us -> none  [the longest x1 2.92 us: body(): feats[send_rows[0]]]
    pallas_call x1, Pallas kernels: 10.7 us -> 5.93 us  [tile_aggregate(): pl.pallas_call(kernel, out_shape=jax.ShapeDtypeStruct((rows, width), jnp....]
    select_n x5 -> x0, other arithmetic: 3.92 us -> none  [the longest x1 0.93 us: body(): returned = jnp.where(live[:, :, None], returned, jnp.float32(0.0))]
  transfers between devices with their start and end apart: 6 -> 6, of which waited for: 5 -> 6; matrix products, arithmetic and copies ran while one was open for 21% -> 16% of each run, Pallas kernels for 0% -> 0%
where the time goes in v5:
time: 124 us
  waiting for transfers between devices  40.4 us (33%)
  starting transfers between devices  33.7 us (27%)
  matrix products  19.2 us (15%)
  Pallas kernels  13 us (10%)
  local copies, waits for them, and re-layouts  10.4 us (8%)
  other arithmetic  5.64 us (5%)
  between operations  1.48 us (1%)
    all_to_all x1, starting transfers between devices, body(): lax.all_to_all(returning.astype(jnp.bfloat16), ('dom', 'dev'), split_axis...  14.4 us
    all_to_all x1, waiting for transfers between devices, body(): lax.all_to_all(parts, ('dom', 'dev'), split_axis=0, concat_axis=0, tiled=...  12.3 us
    all_to_all x1, waiting for transfers between devices, body(): lax.all_to_all(returning.astype(jnp.bfloat16), ('dom', 'dev'), split_axis...  8.51 us
    all_to_all x1, waiting for transfers between devices, body(): lax.all_to_all(outgoing, ('dom', 'dev'), split_axis=0, concat_axis=0, til...  7.95 us
    pallas_call x1, Pallas kernels, tile_backward_t(): pl.pallas_call(kernel, out_shape=jax.ShapeDtypeStruct((width, src_rows),...  7.03 us
    all_to_all x1, starting transfers between devices, body(): lax.all_to_all(hub_out, 'dev', split_axis=0, concat_axis=0, tiled=True)  6.32 us
    pallas_call x1, Pallas kernels, tile_aggregate(): pl.pallas_call(kernel, out_shape=jax.ShapeDtypeStruct((rows, width), jnp....  5.93 us
    all_to_all x1, waiting for transfers between devices, body(): lax.all_to_all(spread_piece, ('dom', 'dev'), split_axis=0, concat_axis=0,...  5.62 us
  transfers between devices with their start and end apart: 6, of which 6 were waited for; matrix products, arithmetic and copies ran while one was open for 16% of the time, Pallas kernels for 0%

profile of v5, /device:TPU:0, one launch (start us, length us, event | category | flops | bytes accessed | tf_op | source)
XLA Modules:
  0.0 123.7 jit_solution(8400177438965844422)
XLA Ops:
  0.6 0.0 copy-start
  0.6 1.6 %convolution_convert_fusion.1 = bf16[32,256]{1,0:T(8,128)(2,1)S(1)} fusion(bf16[2048,256]{1,0:T(8,128)(2,1)} %param.11, s32[32]{0:T(128)} %param.15), kind=kOutput, calls=%fused_computation.23 | convolution fusion | flops 33628160 | bytes 1065088 | tf_op jit(solution)/shard_map/dot_general | solution.py:151
  2.2 0.7 broadcast_in_dim.20
  2.9 6.3 %all-to-all-start.1 = ((bf16[8,32,256]{2,1,0:T(8,128)(2,1)}), bf16[8,32,256]{2,1,0:T(8,128)(2,1)S(1)}, u32[]{:S(2)}, u32[]{:S(2)}) async-start(bf16[8,32,256]{2,1,0:T(8,128)(2,1)} %broadcast_in_dim.20), calls=%async_computation.1 | async-start | bytes 262144 | tf_op jit(solution)/shard_map/all_to_all | solution.py:153
  9.2 0.7 iota_compare_fusion.3
  10.0 0.1 lt.20
  10.1 0.8 copy.21
  10.8 0.1 eq.22
  10.9 2.8 %fusion.12 = bf16[512,256]{1,0:T(8,128)(2,1)} fusion(bf16[2048,256]{1,0:T(8,128)(2,1)} %param.11, s32[512]{0:T(512)S(1)} %eq.22, pred[512]{0:T(512)(128)(4,1)S(1)} %lt.20), kind=kOutput, calls=%fused_computation.21 | convolution fusion | flops 540147712 | bytes 1313280 | tf_op jit(solution)/shard_map/dot_general | solution.py:159
  13.7 2.3 %all-to-all-done.1 = bf16[8,32,256]{2,1,0:T(8,128)(2,1)S(1)} async-done(((bf16[8,32,256]{2,1,0:T(8,128)(2,1)}), bf16[8,32,256]{2,1,0:T(8,128)(2,1)S(1)}, u32[]{:S(2)}, u32[]{:S(2)}) %all-to-all-start.1) | async-done | bytes 131104 | tf_op jit(solution)/shard_map/all_to_all | solution.py:153
  16.0 3.8 %all-to-all-start = ((bf16[32,16,256]{2,1,0:T(8,128)(2,1)}), bf16[32,16,256]{2,1,0:T(8,128)(2,1)S(1)}, u32[]{:S(2)}, u32[]{:S(2)}) async-start(bf16[32,16,256]{2,1,0:T(8,128)(2,1)} %bitcast.1), calls=%async_computation | async-start | bytes 524288 | tf_op jit(solution)/shard_map/all_to_all | solution.py:161
  20.4 0.0 copy-done.2
  20.4 0.0 copy-done.7
  20.5 1.8 %fusion.23 = f32[2048,256]{1,0:T(8,128)} fusion(bf16[2048,256]{1,0:T(8,128)(2,1)S(1)} %copy-done.2, bf16[256,256]{1,0:T(8,128)(2,1)S(1)} %copy-done.7), kind=kOutput, calls=%fused_computation.38 | convolution fusion | flops 268435456 | bytes 3276800 | tf_op jit(solution)/shard_map/dot_general | solution.py:167
  22.2 8.0 %all-to-all-done = bf16[32,16,256]{2,1,0:T(8,128)(2,1)S(1)} async-done(((bf16[32,16,256]{2,1,0:T(8,128)(2,1)}), bf16[32,16,256]{2,1,0:T(8,128)(2,1)S(1)}, u32[]{:S(2)}, u32[]{:S(2)}) %all-to-all-start) | async-done | bytes 262176 | tf_op jit(solution)/shard_map/all_to_all | solution.py:161
  30.2 1.2 pad_maximum_fusion.source_ref
  31.4 5.9 %shard_map.138 = bf16[2048,256]{1,0:T(8,128)(2,1)} custom-call(s32[320]{0:T(512)} %src_ref.3, s32[320]{0:T(512)} %dst_ref.3, s32[1]{0:T(128)S(6)} %copy.34.cnt_ref, bf16[320,128,128]{2,1,0:T(8,128)(2,1)} %val_ref.3, bf16[2816,256]{1,0:T(8,128)(2,1)} %pad_maximum_fusion.source_ref), custom_call_target="tpu_custom_call" | custom-call | tf_op jit(solution)/shard_map/pallas_call | solution.py:64
  37.3 0.0 copy-done
  37.3 0.0 copy-done.10
  37.3 4.1 %multiply_convert_fusion = (bf16[2048,256]{1,0:T(8,128)(2,1)S(1)}, bf16[2048,256]{1,0:T(8,128)(2,1)}) fusion(bf16[2048,256]{1,0:T(8,128)(2,1)S(1)} %copy-done.10, f32[2048,256]{1,0:T(8,128)} %fusion.23, bf16[2048,256]{1,0:T(8,128)(2,1)} %shard_map.138, bf16[256,256]{1,0:T(8,128)(2,1)S(1)} %copy-done), kind=kOutput, calls=%fused_computation.13 | convolution fusion | flops 275251200 | bytes 6422528 | tf_op jit(solution)/shard_map/dot_general | solution.py:167
  41.4 1.5 %fusion.3.daggT_ref = bf16[256,2048]{1,0:T(8,128)(2,1)} fusion(bf16[2048,256]{1,0:T(8,128)(2,1)S(1)} %get-tuple-element.16, bf16[256,256]{1,0:T(8,128)(2,1)S(1)} %copy-done), kind=kOutput, calls=%fused_computation.9 | convolution fusion | flops 268959744 | bytes 2228224 | tf_op jit(solution)/shard_map/dot_general | solution.py:179
  42.9 7.0 %shard_map.139 = f32[256,2816]{1,0:T(8,128)} custom-call(s32[320]{0:T(512)} %src_ref.3, s32[320]{0:T(512)} %dst_ref.3, s32[1]{0:T(128)S(6)} %copy.34.cnt_ref, bf16[320,128,128]{2,1,0:T(8,128)(2,1)} %val_ref.3, bf16[256,2048]{1,0:T(8,128)(2,1)} %fusion.3.daggT_ref), custom_call_target="tpu_custom_call" | custom-call | tf_op jit(solution)/shard_map/pallas_call | solution.py:113
  49.9 2.0 %convert.4 = bf16[256,2816]{1,0:T(8,128)(2,1)S(1)} convert(f32[256,2816]{1,0:T(8,128)} %shard_map.139) | non-fusion elementwise | flops 720896 | bytes 4325376 | tf_op jit(solution)/shard_map/convert.1
  52.0 0.0 copy-start.5
  52.0 1.1 copy-done.5
  53.1 0.8 copy.24
  53.9 14.4 %all-to-all-start.2 = ((bf16[32,16,256]{2,1,0:T(8,128)(2,1)}), bf16[32,16,256]{2,1,0:T(8,128)(2,1)S(1)}, u32[]{:S(2)}, u32[]{:S(2)}) async-start(bf16[32,16,256]{2,1,0:T(8,128)(2,1)} %bitcast.8), calls=%async_computation.2 | async-start | bytes 524288 | tf_op jit(solution)/shard_map/all_to_all | solution.py:186
  68.3 0.5 fusion.24
  68.8 0.0 copy-start.9
  68.8 0.5 convolution_bitcast_fusion.1
  69.4 0.8 pad_maximum_fusion.1
  70.2 8.5 %all-to-all-done.2 = bf16[32,16,256]{2,1,0:T(8,128)(2,1)S(1)} async-done(((bf16[32,16,256]{2,1,0:T(8,128)(2,1)}), bf16[32,16,256]{2,1,0:T(8,128)(2,1)S(1)}, u32[]{:S(2)}, u32[]{:S(2)}) %all-to-all-start.2) | async-done | bytes 262176 | tf_op jit(solution)/shard_map/all_to_all | solution.py:186
  78.7 0.7 copy-done.8
  79.4 2.6 %all-to-all-start.4 = ((f32[32,16,256]{2,1,0:T(8,128)}), f32[32,16,256]{2,1,0:T(8,128)S(1)}, u32[]{:S(2)}, u32[]{:S(2)}) async-start(f32[32,16,256]{2,1,0:T(8,128)} %bitcast.40), calls=%async_computation.4 | async-start | bytes 1048576 | tf_op jit(solution)/shard_map/all_to_all | solution.py:192
  82.0 0.8 fusion.18
  82.8 1.6 %slice_bitcast_fusion.2 = bf16[256,256]{0,1:T(8,128)(2,1)} fusion(bf16[256,2816]{1,0:T(8,128)(2,1)} %copy-done.5), kind=kLoop, calls=%fused_computation.31 | loop fusion | bytes 262144 | tf_op jit(solution)/shard_map/convert_element_type | solution.py:201
  84.4 1.7 %copy.26 = bf16[256,256]{1,0:T(8,128)(2,1)} copy(bf16[256,256]{0,1:T(8,128)(2,1)} %slice_bitcast_fusion.2) | data formatting | bytes 262144 | tf_op jit(solution)/shard_map/convert_element_type | solution.py:201
  86.0 12.3 %all-to-all-done.4 = f32[32,16,256]{2,1,0:T(8,128)S(1)} async-done(((f32[32,16,256]{2,1,0:T(8,128)}), f32[32,16,256]{2,1,0:T(8,128)S(1)}, u32[]{:S(2)}, u32[]{:S(2)}) %all-to-all-start.4) | async-done | bytes 524320 | tf_op jit(solution)/shard_map/all_to_all | solution.py:192
  98.4 4.0 %all-to-all-start.3 = ((bf16[8,32,256]{2,1,0:T(8,128)(2,1)}), bf16[8,32,256]{2,1,0:T(8,128)(2,1)}, u32[]{:S(2)}, u32[]{:S(2)}) async-start(bf16[8,32,256]{2,1,0:T(8,128)(2,1)} %bitcast.43), calls=%async_computation.3 | async-start | bytes 262144 | tf_op jit(solution)/shard_map/all_to_all | solution.py:200
  102.4 3.0 %convolution_add_fusion.1 = f32[2048,256]{0,1:T(8,128)} fusion(bf16[2048,256]{1,0:T(8,128)(2,1)} %copy-done.3, bf16[256,256]{1,0:T(8,128)(2,1)} %param.12, f32[256,2816]{1,0:T(8,128)S(1)} %copy-done.1), kind=kOutput, calls=%fused_computation.5 | convolution fusion | flops 268959744 | bytes 5373952 | tf_op jit(solution)/shard_map/dot_general | solution.py:208
  105.5 3.7 %all-to-all-done.3 = bf16[8,32,256]{2,1,0:T(8,128)(2,1)} async-done(((bf16[8,32,256]{2,1,0:T(8,128)(2,1)}), bf16[8,32,256]{2,1,0:T(8,128)(2,1)}, u32[]{:S(2)}, u32[]{:S(2)}) %all-to-all-start.3) | async-done | bytes 131104 | tf_op jit(solution)/shard_map/all_to_all | solution.py:200
  109.2 0.7 broadcast_in_dim.35
  109.9 2.6 %all-to-all-start.5 = ((bf16[32,16,256]{2,1,0:T(8,128)(2,1)}), bf16[32,16,256]{2,1,0:T(8,128)(2,1)S(1)}, u32[]{:S(2)}, u32[]{:S(2)}) async-start(bf16[32,16,256]{2,1,0:T(8,128)(2,1)} %broadcast_in_dim.35), calls=%async_computation.5 | async-start | bytes 524288 | tf_op jit(solution)/shard_map/all_to_all | solution.py:196
  112.5 1.4 %convolution_bitcast_fusion = f32[2048,256]{0,1:T(8,128)S(1)} fusion(bf16[8,32,256]{2,1,0:T(8,128)(2,1)} %all-to-all-done.3, bf16[32,2048]{1,0:T(8,128)(2,1)} %fusion.18), kind=kOutput, calls=%fused_computation.2 | convolution fusion | flops 268435456 | bytes 2359296 | tf_op jit(solution)/shard_map/dot_general | solution.py:212
  114.0 2.0 %fusion.2 = bf16[2048,256]{0,1:T(8,128)(2,1)S(1)} fusion(f32[2048,256]{0,1:T(8,128)S(1)} %convolution_bitcast_fusion, f32[2048,256]{0,1:T(8,128)S(1)} %copy-done.6, bf16[512,256]{1,0:T(8,128)(2,1)} %bitcast.44, s32[512]{0:T(512)S(1)} %eq.22, pred[512]{0:T(512)(128)(4,1)S(1)} %lt.20), kind=kOutput, calls=%fused_computation.7 | convolution fusion | flops 541589504 | bytes 5507584 | tf_op jit(solution)/shard_map/dot_general | solution.py:209
  115.9 1.3 %copy.28 = bf16[2048,256]{1,0:T(8,128)(2,1)} copy(bf16[2048,256]{0,1:T(8,128)(2,1)S(1)} %fusion.2) | data formatting | bytes 2097152
  117.3 5.6 %all-to-all-done.5 = bf16[32,16,256]{2,1,0:T(8,128)(2,1)S(1)} async-done(((bf16[32,16,256]{2,1,0:T(8,128)(2,1)}), bf16[32,16,256]{2,1,0:T(8,128)(2,1)S(1)}, u32[]{:S(2)}, u32[]{:S(2)}) %all-to-all-start.5) | async-done | bytes 262176 | tf_op jit(solution)/shard_map/all_to_all | solution.py:196
  122.9 0.8 fusion.22
  (16 shorter events, 0.1 us)
Async XLA Ops:
  0.6 36.7 %copy-start = (bf16[256,256]{1,0:T(8,128)(2,1)S(1)}, bf16[256,256]{1,0:T(8,128)(2,1)}, u32[]{:S(2)}) copy-start(bf16[256,256]{1,0:T(8,128)(2,1)} %param.13) | copy-start | bytes 393220
  2.9 13.1 %all-to-all-start.1 = ((bf16[8,32,256]{2,1,0:T(8,128)(2,1)}), bf16[8,32,256]{2,1,0:T(8,128)(2,1)S(1)}, u32[]{:S(2)}, u32[]{:S(2)}) async-start(bf16[8,32,256]{2,1,0:T(8,128)(2,1)} %broadcast_in_dim.20), calls=%async_computation.1 | async-start | bytes 262144 | tf_op jit(solution)/shard_map/all_to_all | solution.py:153
  10.9 9.5 %copy-start.2 = (bf16[2048,256]{1,0:T(8,128)(2,1)S(1)}, bf16[2048,256]{1,0:T(8,128)(2,1)}, u32[]{:S(2)}) copy-start(bf16[2048,256]{1,0:T(8,128)(2,1)} %param.11) | copy-start | bytes 3145732
  10.9 9.5 %copy-start.7 = (bf16[256,256]{1,0:T(8,128)(2,1)S(1)}, bf16[256,256]{1,0:T(8,128)(2,1)}, u32[]{:S(2)}) copy-start(bf16[256,256]{1,0:T(8,128)(2,1)} %param.12) | copy-start | bytes 393220
  16.0 14.2 %all-to-all-start = ((bf16[32,16,256]{2,1,0:T(8,128)(2,1)}), bf16[32,16,256]{2,1,0:T(8,128)(2,1)S(1)}, u32[]{:S(2)}, u32[]{:S(2)}) async-start(bf16[32,16,256]{2,1,0:T(8,128)(2,1)} %bitcast.1), calls=%async_computation | async-start | bytes 524288 | tf_op jit(solution)/shard_map/all_to_all | solution.py:161
  31.4 5.9 %copy-start.10 = (bf16[2048,256]{1,0:T(8,128)(2,1)S(1)}, bf16[2048,256]{1,0:T(8,128)(2,1)}, u32[]{:S(2)}) copy-start(bf16[2048,256]{1,0:T(8,128)(2,1)} %param.14) | copy-start | bytes 3145732
  41.4 27.4 %copy-start.3 = (bf16[2048,256]{1,0:T(8,128)(2,1)}, bf16[2048,256]{1,0:T(8,128)(2,1)S(1)}, u32[]{:S(2)}) copy-start(bf16[2048,256]{1,0:T(8,128)(2,1)S(1)} %get-tuple-element.16) | copy-start | bytes 3145732
  49.9 18.4 %copy-start.4 = (bf16[2048,256]{1,0:T(8,128)(2,1)S(1)}, bf16[2048,256]{1,0:T(8,128)(2,1)}, u32[]{:S(2)}) copy-start(bf16[2048,256]{1,0:T(8,128)(2,1)} %shard_map.138) | copy-start | bytes 3145732
  52.0 1.1 copy-start.5
  53.9 24.8 %all-to-all-start.2 = ((bf16[32,16,256]{2,1,0:T(8,128)(2,1)}), bf16[32,16,256]{2,1,0:T(8,128)(2,1)S(1)}, u32[]{:S(2)}, u32[]{:S(2)}) async-start(bf16[32,16,256]{2,1,0:T(8,128)(2,1)} %bitcast.8), calls=%async_computation.2 | async-start | bytes 524288 | tf_op jit(solution)/shard_map/all_to_all | solution.py:186
  68.8 13.2 %copy-start.9 = (s32[32]{0:T(128)S(1)}, s32[32]{0:T(128)}, u32[]{:S(2)}) copy-start(s32[32]{0:T(128)} %param.15) | copy-start | bytes 388
  69.4 33.0 %copy-start.1 = (f32[256,2816]{1,0:T(8,128)S(1)}, f32[256,2816]{1,0:T(8,128)}, u32[]{:S(2)}) copy-start(f32[256,2816]{1,0:T(8,128)} %shard_map.139) | copy-start | bytes 8650756
  78.7 0.7 copy-start.8
  79.4 19.0 %all-to-all-start.4 = ((f32[32,16,256]{2,1,0:T(8,128)}), f32[32,16,256]{2,1,0:T(8,128)S(1)}, u32[]{:S(2)}, u32[]{:S(2)}) async-start(f32[32,16,256]{2,1,0:T(8,128)} %bitcast.40), calls=%async_computation.4 | async-start | bytes 1048576 | tf_op jit(solution)/shard_map/all_to_all | solution.py:192
  98.4 10.8 %all-to-all-start.3 = ((bf16[8,32,256]{2,1,0:T(8,128)(2,1)}), bf16[8,32,256]{2,1,0:T(8,128)(2,1)}, u32[]{:S(2)}, u32[]{:S(2)}) async-start(bf16[8,32,256]{2,1,0:T(8,128)(2,1)} %bitcast.43), calls=%async_computation.3 | async-start | bytes 262144 | tf_op jit(solution)/shard_map/all_to_all | solution.py:200
  105.4 8.5 %copy-start.6 = (f32[2048,256]{0,1:T(8,128)S(1)}, f32[2048,256]{0,1:T(8,128)}, u32[]{:S(2)}) copy-start(f32[2048,256]{0,1:T(8,128)} %convolution_add_fusion.1) | copy-start | bytes 6291460
  109.9 13.0 %all-to-all-start.5 = ((bf16[32,16,256]{2,1,0:T(8,128)(2,1)}), bf16[32,16,256]{2,1,0:T(8,128)(2,1)S(1)}, u32[]{:S(2)}, u32[]{:S(2)}) async-start(bf16[32,16,256]{2,1,0:T(8,128)(2,1)} %broadcast_in_dim.35), calls=%async_computation.5 | async-start | bytes 524288 | tf_op jit(solution)/shard_map/all_to_all | solution.py:196

commit v6 on v5

--- a/solution.py
+++ b/solution.py
@@ -73,51 +73,73 @@
         compiler_params=pltpu.CompilerParams(dimension_semantics=("arbitrary",)),
     )(tile_src, tile_dst, tile_count, tile_val, source)
 
-def _back_kernel(src_ref, dst_ref, cnt_ref, val_ref, daggT_ref, out_ref, *, tb, edge, batch):
+def _back_kernel(src_ref, dst_ref, cnt_ref, val_ref, daggT_ref, own_ref, rest_ref, acc_ref, *, tb, edge, batch):
     i = pl.program_id(0)
-    last_src = out_ref.shape[1] // edge - 1
+    last_src = acc_ref.shape[1] // edge - 1
     last_dst = daggT_ref.shape[1] // edge - 1
+    rows = own_ref.shape[0]
+
     @pl.when(i == 0)
     def _():
-        out_ref[...] = jnp.zeros_like(out_ref)
+        acc_ref[...] = jnp.zeros_like(acc_ref)
+
     count = cnt_ref[0]
+
     def one(t, k):
         d = jnp.clip(dst_ref[t], 0, last_dst)
         y = daggT_ref[:, pl.ds(pl.multiple_of(d * edge, edge), edge)]
         return jnp.dot(y, val_ref[k], preferred_element_type=jnp.float32)
+
     def add(t, term):
         s = jnp.clip(src_ref[t], 0, last_src)
         cols = pl.ds(pl.multiple_of(s * edge, edge), edge)
-        out_ref[:, cols] += term
+        acc_ref[:, cols] += term
+
     full = (i + 1) * tb <= count
+
     @pl.when(full)
     def _():
         for k0 in range(0, tb, batch):
             terms = [one(i * tb + k, k) for k in range(k0, k0 + batch)]
             for k, term in zip(range(k0, k0 + batch), terms):
                 add(i * tb + k, term)
+
     @pl.when(jnp.logical_and(jnp.logical_not(full), i * tb < count))
     def _():
         def body(k, carry):
             t = i * tb + k
+
             @pl.when(t < count)
             def _():
                 add(t, one(t, k))
+
             return carry
+
         lax.fori_loop(0, tb, body, 0)
+
+    @pl.when(i == pl.num_programs(0) - 1)
+    def _():
+        own_ref[...] = acc_ref[:, :rows].T
+        rest_ref[...] = acc_ref[:, rows:].T.astype(rest_ref.dtype)
+
 
 def tile_backward_t(tile_src, tile_dst, tile_count, tile_val, daggT, src_rows, tb=16, batch=1):
     tiles, edge, _ = tile_val.shape
-    width = daggT.shape[0]
+    width, rows = daggT.shape
     kernel = functools.partial(_back_kernel, tb=tb, edge=edge, batch=batch)
     return pl.pallas_call(
         kernel,
-        out_shape=jax.ShapeDtypeStruct((width, src_rows), jnp.float32),
+        out_shape=(
+            jax.ShapeDtypeStruct((rows, width), jnp.float32),
+            jax.ShapeDtypeStruct((src_rows - rows, width), jnp.bfloat16),
+        ),
         grid_spec=pltpu.PrefetchScalarGridSpec(
             num_scalar_prefetch=3, grid=(tiles // tb,),
             in_specs=[pl.BlockSpec((tb, edge, edge), _val_map(tb)),
                       pl.BlockSpec(daggT.shape, lambda i, s, d, c: (0, 0))],
-            out_specs=pl.BlockSpec((width, src_rows), lambda i, s, d, c: (0, 0))),
+            out_specs=[pl.BlockSpec((rows, width), lambda i, s, d, c: (0, 0)),
+                       pl.BlockSpec((src_rows - rows, width), lambda i, s, d, c: (0, 0))],
+            scratch_shapes=[pltpu.VMEM((width, src_rows), jnp.float32)]),
         compiler_params=pltpu.CompilerParams(dimension_semantics=("arbitrary",)),
     )(tile_src, tile_dst, tile_count, tile_val, daggT)
 
@@ -179,12 +201,11 @@
     dagg_t = lax.dot_general(w_neigh, dpre, contract_cols, preferred_element_type=jnp.float32).astype(
         jnp.bfloat16
     )
-    dsource_t = tile_backward_t(tile_src, tile_dst, tile_count, tile_val, dagg_t, source.shape[0], tb=tb)
-    own = dsource_t[:, :rows].T
-    returning = dsource_t[:, rows : rows + peers * slots].T.reshape(peers, slots, width)
-    hub_part = dsource_t[:, rows + peers * slots :].T
+    own, rest = tile_backward_t(tile_src, tile_dst, tile_count, tile_val, dagg_t, source.shape[0], tb=tb)
+    returning = rest[: peers * slots].reshape(peers, slots, width)
+    hub_part = rest[peers * slots :]
     returned = lax.all_to_all(
-        returning.astype(jnp.bfloat16), ("dom", "dev"), split_axis=0, concat_axis=0, tiled=True
+        returning, ("dom", "dev"), split_axis=0, concat_axis=0, tiled=True
     )
     partial = jnp.concatenate([local_ws, local_wn], axis=0)
     partial, returned = lax.optimization_barrier((partial, returned))
@@ -198,7 +219,7 @@
     grad_ws = summed[: w_self.shape[0]]
     grad_wn = summed[w_self.shape[0] :]
     hub_back = lax.all_to_all(
-        hub_part.astype(jnp.bfloat16).reshape(group, hubs_dev, width),
+        hub_part.reshape(group, hubs_dev, width),
         "dev",
         split_axis=0,
         concat_axis=0,

time: 124 us -> 122 us (0.984); the launches traced: 124 us -> 120 us
  starting transfers between devices: 33.7 us -> 28.7 us
  Pallas kernels: 13 us -> 17.6 us
  local copies, waits for them, and re-layouts: 10.4 us -> 7.54 us
  other arithmetic: 5.64 us -> 2.92 us
  waiting for transfers between devices: 40.4 us -> 42.2 us
    all_to_all x2, starting transfers between devices: 18.4 us -> 13.4 us  [the longest x1 10 us: body(): lax.all_to_all(returning, ('dom', 'dev'), split_axis=0, concat_axis=0, ti...]
    convert_element_type x4 -> x0, local copies, waits for them, and re-layouts: 4.09 us -> none  [the longest x2 3.23 us: body(): hub_part.astype(jnp.bfloat16).reshape(group, hubs_dev, width)]
    slice x0 -> x2, local copies, waits for them, and re-layouts: none -> 3.24 us  [the longest x1 1.67 us: body(): returning = rest[:peers * slots].reshape(peers, slots, width)]
    pallas_call x1, Pallas kernels: 7.03 us -> 10.1 us  [tile_backward_t(): pl.pallas_call(kernel, out_shape=(jax.ShapeDtypeStruct((rows, width), jnp...]
    all_to_all x1, waiting for transfers between devices: 12.3 us -> 14.7 us  [body(): lax.all_to_all(parts, ('dom', 'dev'), split_axis=0, concat_axis=0, tiled=...]
    another operation x1 -> x0, other arithmetic: 2.05 us -> none
    unnamed x24 -> x15, local copies, waits for them, and re-layouts: 3.92 us -> 1.9 us
    pallas_call x1, Pallas kernels: 5.93 us -> 7.46 us  [tile_aggregate(): pl.pallas_call(kernel, out_shape=jax.ShapeDtypeStruct((rows, width), jnp....]
  transfers between devices with their start and end apart: 6 -> 6, of which waited for: 6 -> 6; matrix products, arithmetic and copies ran while one was open for 16% -> 14% of each run, Pallas kernels for 0% -> 0%
where the time goes in v6:
time: 122 us; the launch traced here: 120 us
  waiting for transfers between devices  42.2 us (35%)
  starting transfers between devices  28.7 us (24%)
  matrix products  19.8 us (16%)
  Pallas kernels  17.6 us (14%)
  local copies, waits for them, and re-layouts  7.54 us (6%)
  other arithmetic  2.92 us (2%)
  between operations  1.43 us (1%)
    all_to_all x1, waiting for transfers between devices, body(): lax.all_to_all(parts, ('dom', 'dev'), split_axis=0, concat_axis=0, tiled=...  14.7 us
    pallas_call x1, Pallas kernels, tile_backward_t(): pl.pallas_call(kernel, out_shape=(jax.ShapeDtypeStruct((rows, width), jnp...  10.1 us
    all_to_all x1, starting transfers between devices, body(): lax.all_to_all(returning, ('dom', 'dev'), split_axis=0, concat_axis=0, ti...  10 us
    all_to_all x1, waiting for transfers between devices, body(): lax.all_to_all(returning, ('dom', 'dev'), split_axis=0, concat_axis=0, ti...  8.5 us
    all_to_all x1, waiting for transfers between devices, body(): lax.all_to_all(outgoing, ('dom', 'dev'), split_axis=0, concat_axis=0, til...  7.94 us
    pallas_call x1, Pallas kernels, tile_aggregate(): pl.pallas_call(kernel, out_shape=jax.ShapeDtypeStruct((rows, width), jnp....  7.46 us
    all_to_all x1, starting transfers between devices, body(): lax.all_to_all(hub_out, 'dev', split_axis=0, concat_axis=0, tiled=True)  6.32 us
    all_to_all x1, waiting for transfers between devices, body(): lax.all_to_all(spread_piece, ('dom', 'dev'), split_axis=0, concat_axis=0,...  5.53 us
  transfers between devices with their start and end apart: 6, of which 6 were waited for; matrix products, arithmetic and copies ran while one was open for 14% of the time, Pallas kernels for 0%

profile of v6, /device:TPU:0, one launch (start us, length us, event | category | flops | bytes accessed | tf_op | source)
XLA Modules:
  0.0 120.2 jit_solution(4850096686143235613)
XLA Ops:
  0.6 0.0 copy-start
  0.6 1.6 %convolution_convert_fusion.1 = bf16[32,256]{1,0:T(8,128)(2,1)S(1)} fusion(bf16[2048,256]{1,0:T(8,128)(2,1)} %param.11, s32[32]{0:T(128)} %param.15), kind=kOutput, calls=%fused_computation.22 | convolution fusion | flops 33628160 | bytes 1065088 | tf_op jit(solution)/shard_map/dot_general | solution.py:173
  2.2 0.7 broadcast_in_dim.20
  2.9 6.3 %all-to-all-start.1 = ((bf16[8,32,256]{2,1,0:T(8,128)(2,1)}), bf16[8,32,256]{2,1,0:T(8,128)(2,1)S(1)}, u32[]{:S(2)}, u32[]{:S(2)}) async-start(bf16[8,32,256]{2,1,0:T(8,128)(2,1)} %broadcast_in_dim.20), calls=%async_computation.1 | async-start | bytes 262144 | tf_op jit(solution)/shard_map/all_to_all | solution.py:175
  9.2 0.7 iota_compare_fusion.3
  10.0 0.1 lt.20
  10.1 0.8 copy.16
  10.8 0.1 eq.22
  10.9 0.0 copy-start.1
  10.9 0.0 copy-start.4
  10.9 2.8 %fusion.12 = bf16[512,256]{1,0:T(8,128)(2,1)} fusion(bf16[2048,256]{1,0:T(8,128)(2,1)} %param.11, s32[512]{0:T(512)S(1)} %eq.22, pred[512]{0:T(512)(128)(4,1)S(1)} %lt.20), kind=kOutput, calls=%fused_computation.20 | convolution fusion | flops 540147712 | bytes 1313280 | tf_op jit(solution)/shard_map/dot_general | solution.py:181
  13.7 2.3 %all-to-all-done.1 = bf16[8,32,256]{2,1,0:T(8,128)(2,1)S(1)} async-done(((bf16[8,32,256]{2,1,0:T(8,128)(2,1)}), bf16[8,32,256]{2,1,0:T(8,128)(2,1)S(1)}, u32[]{:S(2)}, u32[]{:S(2)}) %all-to-all-start.1) | async-done | bytes 131104 | tf_op jit(solution)/shard_map/all_to_all | solution.py:175
  16.0 3.8 %all-to-all-start = ((bf16[32,16,256]{2,1,0:T(8,128)(2,1)}), bf16[32,16,256]{2,1,0:T(8,128)(2,1)S(1)}, u32[]{:S(2)}, u32[]{:S(2)}) async-start(bf16[32,16,256]{2,1,0:T(8,128)(2,1)} %bitcast.1), calls=%async_computation | async-start | bytes 524288 | tf_op jit(solution)/shard_map/all_to_all | solution.py:183
  20.4 0.0 copy-done.1
  20.4 0.0 copy-done.4
  20.5 1.8 %fusion.23 = f32[2048,256]{1,0:T(8,128)} fusion(bf16[2048,256]{1,0:T(8,128)(2,1)S(1)} %copy-done.1, bf16[256,256]{1,0:T(8,128)(2,1)S(1)} %copy-done.4), kind=kOutput, calls=%fused_computation.35 | convolution fusion | flops 268435456 | bytes 3276800 | tf_op jit(solution)/shard_map/dot_general | solution.py:189
  22.2 7.9 %all-to-all-done = bf16[32,16,256]{2,1,0:T(8,128)(2,1)S(1)} async-done(((bf16[32,16,256]{2,1,0:T(8,128)(2,1)}), bf16[32,16,256]{2,1,0:T(8,128)(2,1)S(1)}, u32[]{:S(2)}, u32[]{:S(2)}) %all-to-all-start) | async-done | bytes 262176 | tf_op jit(solution)/shard_map/all_to_all | solution.py:183
  30.2 1.2 %pad_maximum_fusion.source_ref = bf16[2816,256]{1,0:T(8,128)(2,1)} fusion(bf16[256,256]{1,0:T(8,128)(2,1)S(1)} %bitcast.33, bf16[512,256]{1,0:T(8,128)(2,1)S(1)} %bitcast.32, bf16[2048,256]{1,0:T(8,128)(2,1)S(1)} %copy-done.1), kind=kLoop, calls=%fused_computation.19 | loop fusion | flops 4325376 | bytes 2883584 | tf_op jit(solution)/shard_map/concatenate | solution.py:184
  31.4 7.5 %shard_map.138 = bf16[2048,256]{1,0:T(8,128)(2,1)} custom-call(s32[320]{0:T(512)} %src_ref.3, s32[320]{0:T(512)} %dst_ref.3, s32[1]{0:T(128)S(6)} %copy.19.cnt_ref, bf16[320,128,128]{2,1,0:T(8,128)(2,1)} %val_ref.3, bf16[2816,256]{1,0:T(8,128)(2,1)} %pad_maximum_fusion.source_ref), custom_call_target="tpu_custom_call" | custom-call | tf_op jit(solution)/shard_map/pallas_call | solution.py:64
  38.9 0.0 copy-done
  38.9 0.0 copy-done.6
  38.9 4.1 %multiply_convert_fusion = (bf16[2048,256]{1,0:T(8,128)(2,1)S(1)}, bf16[2048,256]{1,0:T(8,128)(2,1)}) fusion(bf16[2048,256]{1,0:T(8,128)(2,1)S(1)} %copy-done.6, f32[2048,256]{1,0:T(8,128)} %fusion.23, bf16[2048,256]{1,0:T(8,128)(2,1)} %shard_map.138, bf16[256,256]{1,0:T(8,128)(2,1)S(1)} %copy-done), kind=kOutput, calls=%fused_computation.12 | convolution fusion | flops 275251200 | bytes 6422528 | tf_op jit(solution)/shard_map/dot_general | solution.py:189
  43.0 1.4 %fusion.3.daggT_ref = bf16[256,2048]{1,0:T(8,128)(2,1)} fusion(bf16[2048,256]{1,0:T(8,128)(2,1)S(1)} %get-tuple-element.12, bf16[256,256]{1,0:T(8,128)(2,1)S(1)} %copy-done), kind=kOutput, calls=%fused_computation.9 | convolution fusion | flops 268959744 | bytes 2228224 | tf_op jit(solution)/shard_map/dot_general | solution.py:201
  44.4 10.1 %shard_map.139 = (f32[2048,256]{1,0:T(8,128)}, bf16[768,256]{1,0:T(8,128)(2,1)}) custom-call(s32[320]{0:T(512)} %src_ref.3, s32[320]{0:T(512)} %dst_ref.3, s32[1]{0:T(128)S(6)} %copy.19.cnt_ref, bf16[320,128,128]{2,1,0:T(8,128)(2,1)} %val_ref.3, bf16[256,2048]{1,0:T(8,128)(2,1)} %fusion.3.daggT_ref), custom_call_target="tpu_custom_call" | custom-call | tf_op jit(solution)/shard_map/pallas_call | solution.py:130
  54.5 1.7 %slice.18 = bf16[512,256]{1,0:T(8,128)(2,1)} slice(bf16[768,256]{1,0:T(8,128)(2,1)} %get-tuple-element.9), slice={[0:512], [0:256]} | slice | bytes 524288 | tf_op jit(solution)/shard_map/slice | solution.py:205
  56.2 10.0 %all-to-all-start.2 = ((bf16[32,16,256]{2,1,0:T(8,128)(2,1)}), bf16[32,16,256]{2,1,0:T(8,128)(2,1)}, u32[]{:S(2)}, u32[]{:S(2)}) async-start(bf16[32,16,256]{2,1,0:T(8,128)(2,1)} %bitcast.6), calls=%async_computation.2 | async-start | bytes 524288 | tf_op jit(solution)/shard_map/all_to_all | solution.py:207
  66.2 0.0 copy-done.2
  66.2 0.5 fusion.24
  66.7 0.0 copy-start.5
  66.7 0.5 convolution_bitcast_fusion.1
  67.3 0.8 pad_maximum_fusion.1
  68.1 8.5 %all-to-all-done.2 = bf16[32,16,256]{2,1,0:T(8,128)(2,1)} async-done(((bf16[32,16,256]{2,1,0:T(8,128)(2,1)}), bf16[32,16,256]{2,1,0:T(8,128)(2,1)}, u32[]{:S(2)}, u32[]{:S(2)}) %all-to-all-start.2) | async-done | bytes 262176 | tf_op jit(solution)/shard_map/all_to_all | solution.py:207
  76.6 2.6 %all-to-all-start.4 = ((f32[32,16,256]{2,1,0:T(8,128)}), f32[32,16,256]{2,1,0:T(8,128)S(1)}, u32[]{:S(2)}, u32[]{:S(2)}) async-start(f32[32,16,256]{2,1,0:T(8,128)} %bitcast.10), calls=%async_computation.4 | async-start | bytes 1048576 | tf_op jit(solution)/shard_map/all_to_all | solution.py:213
  79.2 0.0 copy-done.5
  79.2 0.1 fusion.18
  79.3 1.6 %slice.19 = bf16[256,256]{1,0:T(8,128)(2,1)} slice(bf16[768,256]{1,0:T(8,128)(2,1)} %get-tuple-element.9), slice={[512:768], [0:256]} | slice | bytes 262144 | tf_op jit(solution)/shard_map/slice | solution.py:206
  80.9 14.7 %all-to-all-done.4 = f32[32,16,256]{2,1,0:T(8,128)S(1)} async-done(((f32[32,16,256]{2,1,0:T(8,128)}), f32[32,16,256]{2,1,0:T(8,128)S(1)}, u32[]{:S(2)}, u32[]{:S(2)}) %all-to-all-start.4) | async-done | bytes 524320 | tf_op jit(solution)/shard_map/all_to_all | solution.py:213
  95.6 3.4 %all-to-all-start.3 = ((bf16[8,32,256]{2,1,0:T(8,128)(2,1)}), bf16[8,32,256]{2,1,0:T(8,128)(2,1)S(1)}, u32[]{:S(2)}, u32[]{:S(2)}) async-start(bf16[8,32,256]{2,1,0:T(8,128)(2,1)} %bitcast.8), calls=%async_computation.3 | async-start | bytes 262144 | tf_op jit(solution)/shard_map/all_to_all | solution.py:221
  98.9 3.4 %convolution_add_fusion.1 = f32[2048,256]{1,0:T(8,128)} fusion(f32[2048,256]{1,0:T(8,128)} %get-tuple-element.8, bf16[2048,256]{1,0:T(8,128)(2,1)S(1)} %get-tuple-element.12, bf16[256,256]{1,0:T(8,128)(2,1)S(1)} %copy-done.4), kind=kOutput, calls=%fused_computation.5 | convolution fusion | flops 268959744 | bytes 5373952 | tf_op jit(solution)/shard_map/dot_general | solution.py:229
  102.4 3.3 %all-to-all-done.3 = bf16[8,32,256]{2,1,0:T(8,128)(2,1)S(1)} async-done(((bf16[8,32,256]{2,1,0:T(8,128)(2,1)}), bf16[8,32,256]{2,1,0:T(8,128)(2,1)S(1)}, u32[]{:S(2)}, u32[]{:S(2)}) %all-to-all-start.3) | async-done | bytes 131104 | tf_op jit(solution)/shard_map/all_to_all | solution.py:221
  105.7 0.7 broadcast_in_dim.35
  106.4 2.6 %all-to-all-start.5 = ((bf16[32,16,256]{2,1,0:T(8,128)(2,1)}), bf16[32,16,256]{2,1,0:T(8,128)(2,1)S(1)}, u32[]{:S(2)}, u32[]{:S(2)}) async-start(bf16[32,16,256]{2,1,0:T(8,128)(2,1)} %broadcast_in_dim.35), calls=%async_computation.5 | async-start | bytes 524288 | tf_op jit(solution)/shard_map/all_to_all | solution.py:217
  109.0 0.0 copy-start.3
  109.0 0.5 convolution_bitcast_fusion
  109.5 1.1 copy-done.3
  110.6 3.3 %fusion.2 = bf16[2048,256]{1,0:T(8,128)(2,1)} fusion(f32[2048,256]{1,0:T(8,128)S(1)} %convolution_bitcast_fusion, f32[2048,256]{1,0:T(8,128)S(1)} %copy-done.3, bf16[512,256]{1,0:T(8,128)(2,1)} %bitcast.7, s32[512]{0:T(512)S(1)} %eq.22, pred[512]{0:T(512)(128)(4,1)S(1)} %lt.20), kind=kOutput, calls=%fused_computation.7 | convolution fusion | flops 541589504 | bytes 5507584 | tf_op jit(solution)/shard_map/dot_general | solution.py:230
  113.8 5.5 %all-to-all-done.5 = bf16[32,16,256]{2,1,0:T(8,128)(2,1)S(1)} async-done(((bf16[32,16,256]{2,1,0:T(8,128)(2,1)}), bf16[32,16,256]{2,1,0:T(8,128)(2,1)S(1)}, u32[]{:S(2)}, u32[]{:S(2)}) %all-to-all-start.5) | async-done | bytes 262176 | tf_op jit(solution)/shard_map/all_to_all | solution.py:217
  119.3 0.8 fusion.22
  (4 shorter events, 0.1 us)
Async XLA Ops:
  0.6 38.2 %copy-start = (bf16[256,256]{1,0:T(8,128)(2,1)S(1)}, bf16[256,256]{1,0:T(8,128)(2,1)}, u32[]{:S(2)}) copy-start(bf16[256,256]{1,0:T(8,128)(2,1)} %param.13) | copy-start | bytes 393220
  2.9 13.1 %all-to-all-start.1 = ((bf16[8,32,256]{2,1,0:T(8,128)(2,1)}), bf16[8,32,256]{2,1,0:T(8,128)(2,1)S(1)}, u32[]{:S(2)}, u32[]{:S(2)}) async-start(bf16[8,32,256]{2,1,0:T(8,128)(2,1)} %broadcast_in_dim.20), calls=%async_computation.1 | async-start | bytes 262144 | tf_op jit(solution)/shard_map/all_to_all | solution.py:175
  10.9 9.5 %copy-start.1 = (bf16[2048,256]{1,0:T(8,128)(2,1)S(1)}, bf16[2048,256]{1,0:T(8,128)(2,1)}, u32[]{:S(2)}) copy-start(bf16[2048,256]{1,0:T(8,128)(2,1)} %param.11) | copy-start | bytes 3145732
  10.9 9.5 %copy-start.4 = (bf16[256,256]{1,0:T(8,128)(2,1)S(1)}, bf16[256,256]{1,0:T(8,128)(2,1)}, u32[]{:S(2)}) copy-start(bf16[256,256]{1,0:T(8,128)(2,1)} %param.12) | copy-start | bytes 393220
  16.0 14.2 %all-to-all-start = ((bf16[32,16,256]{2,1,0:T(8,128)(2,1)}), bf16[32,16,256]{2,1,0:T(8,128)(2,1)S(1)}, u32[]{:S(2)}, u32[]{:S(2)}) async-start(bf16[32,16,256]{2,1,0:T(8,128)(2,1)} %bitcast.1), calls=%async_computation | async-start | bytes 524288 | tf_op jit(solution)/shard_map/all_to_all | solution.py:183
  31.4 7.5 %copy-start.6 = (bf16[2048,256]{1,0:T(8,128)(2,1)S(1)}, bf16[2048,256]{1,0:T(8,128)(2,1)}, u32[]{:S(2)}) copy-start(bf16[2048,256]{1,0:T(8,128)(2,1)} %param.14) | copy-start | bytes 3145732
  44.4 21.8 %copy-start.2 = (bf16[2048,256]{1,0:T(8,128)(2,1)S(1)}, bf16[2048,256]{1,0:T(8,128)(2,1)}, u32[]{:S(2)}) copy-start(bf16[2048,256]{1,0:T(8,128)(2,1)} %shard_map.138) | copy-start | bytes 3145732
  56.2 20.4 %all-to-all-start.2 = ((bf16[32,16,256]{2,1,0:T(8,128)(2,1)}), bf16[32,16,256]{2,1,0:T(8,128)(2,1)}, u32[]{:S(2)}, u32[]{:S(2)}) async-start(bf16[32,16,256]{2,1,0:T(8,128)(2,1)} %bitcast.6), calls=%async_computation.2 | async-start | bytes 524288 | tf_op jit(solution)/shard_map/all_to_all | solution.py:207
  66.7 12.5 %copy-start.5 = (s32[32]{0:T(128)S(1)}, s32[32]{0:T(128)}, u32[]{:S(2)}) copy-start(s32[32]{0:T(128)} %param.15) | copy-start | bytes 388
  76.6 19.0 %all-to-all-start.4 = ((f32[32,16,256]{2,1,0:T(8,128)}), f32[32,16,256]{2,1,0:T(8,128)S(1)}, u32[]{:S(2)}, u32[]{:S(2)}) async-start(f32[32,16,256]{2,1,0:T(8,128)} %bitcast.10), calls=%async_computation.4 | async-start | bytes 1048576 | tf_op jit(solution)/shard_map/all_to_all | solution.py:213
  95.6 10.1 %all-to-all-start.3 = ((bf16[8,32,256]{2,1,0:T(8,128)(2,1)}), bf16[8,32,256]{2,1,0:T(8,128)(2,1)S(1)}, u32[]{:S(2)}, u32[]{:S(2)}) async-start(bf16[8,32,256]{2,1,0:T(8,128)(2,1)} %bitcast.8), calls=%async_computation.3 | async-start | bytes 262144 | tf_op jit(solution)/shard_map/all_to_all | solution.py:221
  106.4 13.0 %all-to-all-start.5 = ((bf16[32,16,256]{2,1,0:T(8,128)(2,1)}), bf16[32,16,256]{2,1,0:T(8,128)(2,1)S(1)}, u32[]{:S(2)}, u32[]{:S(2)}) async-start(bf16[32,16,256]{2,1,0:T(8,128)(2,1)} %broadcast_in_dim.35), calls=%async_computation.5 | async-start | bytes 524288 | tf_op jit(solution)/shard_map/all_to_all | solution.py:217
  109.0 1.6 %copy-start.3 = (f32[2048,256]{1,0:T(8,128)S(1)}, f32[2048,256]{1,0:T(8,128)}, u32[]{:S(2)}) copy-start(f32[2048,256]{1,0:T(8,128)} %convolution_add_fusion.1) | copy-start | bytes 6291460

commit v7 on v6

--- a/solution.py
+++ b/solution.py
@@ -73,7 +73,7 @@
         compiler_params=pltpu.CompilerParams(dimension_semantics=("arbitrary",)),
     )(tile_src, tile_dst, tile_count, tile_val, source)
 
-def _back_kernel(src_ref, dst_ref, cnt_ref, val_ref, daggT_ref, own_ref, rest_ref, acc_ref, *, tb, edge, batch):
+def _back_kernel(src_ref, dst_ref, cnt_ref, val_ref, daggT_ref, own_ref, ret_ref, hub_ref, acc_ref, *, tb, edge, batch):
     i = pl.program_id(0)
     last_src = acc_ref.shape[1] // edge - 1
     last_dst = daggT_ref.shape[1] // edge - 1
@@ -120,10 +120,12 @@
     @pl.when(i == pl.num_programs(0) - 1)
     def _():
         own_ref[...] = acc_ref[:, :rows].T
-        rest_ref[...] = acc_ref[:, rows:].T.astype(rest_ref.dtype)
-
-
-def tile_backward_t(tile_src, tile_dst, tile_count, tile_val, daggT, src_rows, tb=16, batch=1):
+        split = rows + ret_ref.shape[0]
+        ret_ref[...] = acc_ref[:, rows:split].T.astype(ret_ref.dtype)
+        hub_ref[...] = acc_ref[:, split:].T.astype(hub_ref.dtype)
+
+
+def tile_backward_t(tile_src, tile_dst, tile_count, tile_val, daggT, src_rows, ret_rows, tb=16, batch=1):
     tiles, edge, _ = tile_val.shape
     width, rows = daggT.shape
     kernel = functools.partial(_back_kernel, tb=tb, edge=edge, batch=batch)
@@ -131,14 +133,16 @@
         kernel,
         out_shape=(
             jax.ShapeDtypeStruct((rows, width), jnp.float32),
-            jax.ShapeDtypeStruct((src_rows - rows, width), jnp.bfloat16),
+            jax.ShapeDtypeStruct((ret_rows, width), jnp.bfloat16),
+            jax.ShapeDtypeStruct((src_rows - rows - ret_rows, width), jnp.bfloat16),
         ),
         grid_spec=pltpu.PrefetchScalarGridSpec(
             num_scalar_prefetch=3, grid=(tiles // tb,),
             in_specs=[pl.BlockSpec((tb, edge, edge), _val_map(tb)),
                       pl.BlockSpec(daggT.shape, lambda i, s, d, c: (0, 0))],
             out_specs=[pl.BlockSpec((rows, width), lambda i, s, d, c: (0, 0)),
-                       pl.BlockSpec((src_rows - rows, width), lambda i, s, d, c: (0, 0))],
+                       pl.BlockSpec((ret_rows, width), lambda i, s, d, c: (0, 0)),
+                       pl.BlockSpec((src_rows - rows - ret_rows, width), lambda i, s, d, c: (0, 0))],
             scratch_shapes=[pltpu.VMEM((width, src_rows), jnp.float32)]),
         compiler_params=pltpu.CompilerParams(dimension_semantics=("arbitrary",)),
     )(tile_src, tile_dst, tile_count, tile_val, daggT)
@@ -201,9 +205,10 @@
     dagg_t = lax.dot_general(w_neigh, dpre, contract_cols, preferred_element_type=jnp.float32).astype(
         jnp.bfloat16
     )
-    own, rest = tile_backward_t(tile_src, tile_dst, tile_count, tile_val, dagg_t, source.shape[0], tb=tb)
-    returning = rest[: peers * slots].reshape(peers, slots, width)
-    hub_part = rest[peers * slots :]
+    own, returning, hub_part = tile_backward_t(
+        tile_src, tile_dst, tile_count, tile_val, dagg_t, source.shape[0], peers * slots, tb=tb
+    )
+    returning = returning.reshape(peers, slots, width)
     returned = lax.all_to_all(
         returning, ("dom", "dev"), split_axis=0, concat_axis=0, tiled=True
     )

time: 122 us -> 119 us (0.975); the launches traced: 120 us -> 119 us
  Pallas kernels: 17.6 us -> 13.7 us
  starting transfers between devices: 28.7 us -> 32.5 us
  local copies, waits for them, and re-layouts: 7.54 us -> 4.3 us
  waiting for transfers between devices: 42.2 us -> 43.8 us
    all_to_all x1, starting transfers between devices: 10 us -> 13.9 us  [body(): lax.all_to_all(returning, ('dom', 'dev'), split_axis=0, concat_axis=0, ti...]
    slice x2 -> x0, local copies, waits for them, and re-layouts: 3.24 us -> none  [the longest x1 1.67 us: body(): returning = rest[:peers * slots].reshape(peers, slots, width)]
    pallas_call x1, Pallas kernels: 10.1 us -> 7.78 us  [tile_backward_t(): pl.pallas_call(kernel, out_shape=(jax.ShapeDtypeStruct((rows, width), jnp...]
    all_to_all x1, waiting for transfers between devices: 14.7 us -> 16.2 us  [body(): lax.all_to_all(parts, ('dom', 'dev'), split_axis=0, concat_axis=0, tiled=...]
    pallas_call x1, Pallas kernels: 7.46 us -> 5.93 us  [tile_aggregate(): pl.pallas_call(kernel, out_shape=jax.ShapeDtypeStruct((rows, width), jnp....]
  transfers between devices with their start and end apart: 6 -> 6, of which waited for: 6 -> 6; matrix products, arithmetic and copies ran while one was open for 14% -> 13% of each run, Pallas kernels for 0% -> 0%
where the time goes in v7:
time: 119 us
  waiting for transfers between devices  43.8 us (37%)
  starting transfers between devices  32.5 us (27%)
  matrix products  19.8 us (17%)
  Pallas kernels  13.7 us (12%)
  local copies, waits for them, and re-layouts  4.3 us (4%)
  other arithmetic  2.93 us (2%)
  between operations  1.43 us (1%)
    all_to_all x1, waiting for transfers between devices, body(): lax.all_to_all(parts, ('dom', 'dev'), split_axis=0, concat_axis=0, tiled=...  16.2 us
    all_to_all x1, starting transfers between devices, body(): lax.all_to_all(returning, ('dom', 'dev'), split_axis=0, concat_axis=0, ti...  13.9 us
    all_to_all x1, waiting for transfers between devices, body(): lax.all_to_all(returning, ('dom', 'dev'), split_axis=0, concat_axis=0, ti...  8.5 us
    all_to_all x1, waiting for transfers between devices, body(): lax.all_to_all(outgoing, ('dom', 'dev'), split_axis=0, concat_axis=0, til...  7.94 us
    pallas_call x1, Pallas kernels, tile_backward_t(): pl.pallas_call(kernel, out_shape=(jax.ShapeDtypeStruct((rows, width), jnp...  7.78 us
    all_to_all x1, starting transfers between devices, body(): lax.all_to_all(hub_out, 'dev', split_axis=0, concat_axis=0, tiled=True)  6.32 us
    pallas_call x1, Pallas kernels, tile_aggregate(): pl.pallas_call(kernel, out_shape=jax.ShapeDtypeStruct((rows, width), jnp....  5.93 us
    all_to_all x1, waiting for transfers between devices, body(): lax.all_to_all(spread_piece, ('dom', 'dev'), split_axis=0, concat_axis=0,...  5.54 us
  transfers between devices with their start and end apart: 6, of which 6 were waited for; matrix products, arithmetic and copies ran while one was open for 13% of the time, Pallas kernels for 0%

profile of v7, /device:TPU:0, one launch (start us, length us, event | category | flops | bytes accessed | tf_op | source)
XLA Modules:
  0.0 118.5 jit_solution(12100067510297184256)
XLA Ops:
  0.6 0.0 copy-start
  0.6 1.6 %convolution_convert_fusion.1 = bf16[32,256]{1,0:T(8,128)(2,1)S(1)} fusion(bf16[2048,256]{1,0:T(8,128)(2,1)} %param.11, s32[32]{0:T(128)} %param.15), kind=kOutput, calls=%fused_computation.22 | convolution fusion | flops 33628160 | bytes 1065088 | tf_op jit(solution)/shard_map/dot_general | solution.py:177
  2.2 0.7 broadcast_in_dim.20
  2.9 6.3 %all-to-all-start.1 = ((bf16[8,32,256]{2,1,0:T(8,128)(2,1)}), bf16[8,32,256]{2,1,0:T(8,128)(2,1)S(1)}, u32[]{:S(2)}, u32[]{:S(2)}) async-start(bf16[8,32,256]{2,1,0:T(8,128)(2,1)} %broadcast_in_dim.20), calls=%async_computation.1 | async-start | bytes 262144 | tf_op jit(solution)/shard_map/all_to_all | solution.py:179
  9.2 0.8 copy.16
  10.0 0.1 eq.22
  10.1 0.7 iota_compare_fusion.3
  10.8 0.1 lt.20
  10.9 0.0 copy-start.1
  10.9 0.0 copy-start.4
  10.9 2.8 %fusion.12 = bf16[512,256]{1,0:T(8,128)(2,1)} fusion(bf16[2048,256]{1,0:T(8,128)(2,1)} %param.11, s32[512]{0:T(512)S(1)} %eq.22, pred[512]{0:T(512)(128)(4,1)S(1)} %lt.20), kind=kOutput, calls=%fused_computation.20 | convolution fusion | flops 540147712 | bytes 1313280 | tf_op jit(solution)/shard_map/dot_general | solution.py:185
  13.7 2.3 %all-to-all-done.1 = bf16[8,32,256]{2,1,0:T(8,128)(2,1)S(1)} async-done(((bf16[8,32,256]{2,1,0:T(8,128)(2,1)}), bf16[8,32,256]{2,1,0:T(8,128)(2,1)S(1)}, u32[]{:S(2)}, u32[]{:S(2)}) %all-to-all-start.1) | async-done | bytes 131104 | tf_op jit(solution)/shard_map/all_to_all | solution.py:179
  16.0 3.8 %all-to-all-start = ((bf16[32,16,256]{2,1,0:T(8,128)(2,1)}), bf16[32,16,256]{2,1,0:T(8,128)(2,1)S(1)}, u32[]{:S(2)}, u32[]{:S(2)}) async-start(bf16[32,16,256]{2,1,0:T(8,128)(2,1)} %bitcast.1), calls=%async_computation | async-start | bytes 524288 | tf_op jit(solution)/shard_map/all_to_all | solution.py:187
  20.4 0.0 copy-done.1
  20.5 0.0 copy-done.4
  20.5 1.8 %fusion.23 = f32[2048,256]{1,0:T(8,128)} fusion(bf16[2048,256]{1,0:T(8,128)(2,1)S(1)} %copy-done.1, bf16[256,256]{1,0:T(8,128)(2,1)S(1)} %copy-done.4), kind=kOutput, calls=%fused_computation.35 | convolution fusion | flops 268435456 | bytes 3276800 | tf_op jit(solution)/shard_map/dot_general | solution.py:193
  22.2 7.9 %all-to-all-done = bf16[32,16,256]{2,1,0:T(8,128)(2,1)S(1)} async-done(((bf16[32,16,256]{2,1,0:T(8,128)(2,1)}), bf16[32,16,256]{2,1,0:T(8,128)(2,1)S(1)}, u32[]{:S(2)}, u32[]{:S(2)}) %all-to-all-start) | async-done | bytes 262176 | tf_op jit(solution)/shard_map/all_to_all | solution.py:187
  30.2 1.2 %pad_maximum_fusion.source_ref = bf16[2816,256]{1,0:T(8,128)(2,1)} fusion(bf16[256,256]{1,0:T(8,128)(2,1)S(1)} %bitcast.33, bf16[512,256]{1,0:T(8,128)(2,1)S(1)} %bitcast.32, bf16[2048,256]{1,0:T(8,128)(2,1)S(1)} %copy-done.1), kind=kLoop, calls=%fused_computation.19 | loop fusion | flops 4325376 | bytes 2883584 | tf_op jit(solution)/shard_map/concatenate | solution.py:188
  31.4 0.0 copy-start.6
  31.4 5.9 %shard_map.138 = bf16[2048,256]{1,0:T(8,128)(2,1)} custom-call(s32[320]{0:T(512)} %src_ref.3, s32[320]{0:T(512)} %dst_ref.3, s32[1]{0:T(128)S(6)} %copy.19.cnt_ref, bf16[320,128,128]{2,1,0:T(8,128)(2,1)} %val_ref.3, bf16[2816,256]{1,0:T(8,128)(2,1)} %pad_maximum_fusion.source_ref), custom_call_target="tpu_custom_call" | custom-call | tf_op jit(solution)/shard_map/pallas_call | solution.py:64
  37.3 0.0 copy-done
  37.3 0.0 copy-done.6
  37.3 4.1 %multiply_convert_fusion = (bf16[2048,256]{1,0:T(8,128)(2,1)S(1)}, bf16[2048,256]{1,0:T(8,128)(2,1)}) fusion(bf16[2048,256]{1,0:T(8,128)(2,1)S(1)} %copy-done.6, f32[2048,256]{1,0:T(8,128)} %fusion.23, bf16[2048,256]{1,0:T(8,128)(2,1)} %shard_map.138, bf16[256,256]{1,0:T(8,128)(2,1)S(1)} %copy-done), kind=kOutput, calls=%fused_computation.12 | convolution fusion | flops 275251200 | bytes 6422528 | tf_op jit(solution)/shard_map/dot_general | solution.py:193
  41.4 1.4 %fusion.3.daggT_ref = bf16[256,2048]{1,0:T(8,128)(2,1)} fusion(bf16[2048,256]{1,0:T(8,128)(2,1)S(1)} %get-tuple-element.14, bf16[256,256]{1,0:T(8,128)(2,1)S(1)} %copy-done), kind=kOutput, calls=%fused_computation.9 | convolution fusion | flops 268959744 | bytes 2228224 | tf_op jit(solution)/shard_map/dot_general | solution.py:205
  42.9 0.0 copy-start.2
  42.9 7.8 %shard_map.139 = (f32[2048,256]{1,0:T(8,128)}, bf16[512,256]{1,0:T(8,128)(2,1)}, bf16[256,256]{1,0:T(8,128)(2,1)}) custom-call(s32[320]{0:T(512)} %src_ref.3, s32[320]{0:T(512)} %dst_ref.3, s32[1]{0:T(128)S(6)} %copy.19.cnt_ref, bf16[320,128,128]{2,1,0:T(8,128)(2,1)} %val_ref.3, bf16[256,2048]{1,0:T(8,128)(2,1)} %fusion.3.daggT_ref), custom_call_target="tpu_custom_call" | custom-call | tf_op jit(solution)/shard_map/pallas_call | solution.py:132
  50.7 13.9 %all-to-all-start.2 = ((bf16[32,16,256]{2,1,0:T(8,128)(2,1)}), bf16[32,16,256]{2,1,0:T(8,128)(2,1)}, u32[]{:S(2)}, u32[]{:S(2)}) async-start(bf16[32,16,256]{2,1,0:T(8,128)(2,1)} %bitcast.34), calls=%async_computation.2 | async-start | bytes 524288 | tf_op jit(solution)/shard_map/all_to_all | solution.py:212
  64.5 0.0 copy-done.2
  64.6 0.5 fusion.24
  65.0 0.0 copy-start.5
  65.0 0.5 convolution_bitcast_fusion.1
  65.6 0.8 pad_maximum_fusion.1
  66.4 8.5 %all-to-all-done.2 = bf16[32,16,256]{2,1,0:T(8,128)(2,1)} async-done(((bf16[32,16,256]{2,1,0:T(8,128)(2,1)}), bf16[32,16,256]{2,1,0:T(8,128)(2,1)}, u32[]{:S(2)}, u32[]{:S(2)}) %all-to-all-start.2) | async-done | bytes 262176 | tf_op jit(solution)/shard_map/all_to_all | solution.py:212
  74.9 2.6 %all-to-all-start.4 = ((f32[32,16,256]{2,1,0:T(8,128)}), f32[32,16,256]{2,1,0:T(8,128)S(1)}, u32[]{:S(2)}, u32[]{:S(2)}) async-start(f32[32,16,256]{2,1,0:T(8,128)} %bitcast.10), calls=%async_computation.4 | async-start | bytes 1048576 | tf_op jit(solution)/shard_map/all_to_all | solution.py:218
  77.5 0.0 copy-done.5
  77.5 0.1 fusion.18
  77.6 16.2 %all-to-all-done.4 = f32[32,16,256]{2,1,0:T(8,128)S(1)} async-done(((f32[32,16,256]{2,1,0:T(8,128)}), f32[32,16,256]{2,1,0:T(8,128)S(1)}, u32[]{:S(2)}, u32[]{:S(2)}) %all-to-all-start.4) | async-done | bytes 524320 | tf_op jit(solution)/shard_map/all_to_all | solution.py:218
  93.9 3.4 %all-to-all-start.3 = ((bf16[8,32,256]{2,1,0:T(8,128)(2,1)}), bf16[8,32,256]{2,1,0:T(8,128)(2,1)S(1)}, u32[]{:S(2)}, u32[]{:S(2)}) async-start(bf16[8,32,256]{2,1,0:T(8,128)(2,1)} %bitcast.8), calls=%async_computation.3 | async-start | bytes 262144 | tf_op jit(solution)/shard_map/all_to_all | solution.py:226
  97.3 3.4 %convolution_add_fusion.1 = f32[2048,256]{1,0:T(8,128)} fusion(f32[2048,256]{1,0:T(8,128)} %get-tuple-element.9, bf16[2048,256]{1,0:T(8,128)(2,1)S(1)} %get-tuple-element.14, bf16[256,256]{1,0:T(8,128)(2,1)S(1)} %copy-done.4), kind=kOutput, calls=%fused_computation.5 | convolution fusion | flops 268959744 | bytes 5373952 | tf_op jit(solution)/shard_map/dot_general | solution.py:234
  100.7 3.3 %all-to-all-done.3 = bf16[8,32,256]{2,1,0:T(8,128)(2,1)S(1)} async-done(((bf16[8,32,256]{2,1,0:T(8,128)(2,1)}), bf16[8,32,256]{2,1,0:T(8,128)(2,1)S(1)}, u32[]{:S(2)}, u32[]{:S(2)}) %all-to-all-start.3) | async-done | bytes 131104 | tf_op jit(solution)/shard_map/all_to_all | solution.py:226
  104.0 0.7 broadcast_in_dim.35
  104.7 2.6 %all-to-all-start.5 = ((bf16[32,16,256]{2,1,0:T(8,128)(2,1)}), bf16[32,16,256]{2,1,0:T(8,128)(2,1)S(1)}, u32[]{:S(2)}, u32[]{:S(2)}) async-start(bf16[32,16,256]{2,1,0:T(8,128)(2,1)} %broadcast_in_dim.35), calls=%async_computation.5 | async-start | bytes 524288 | tf_op jit(solution)/shard_map/all_to_all | solution.py:222
  107.3 0.0 copy-start.3
  107.3 0.5 convolution_bitcast_fusion
  107.8 1.1 copy-done.3
  108.9 3.3 %fusion.2 = bf16[2048,256]{1,0:T(8,128)(2,1)} fusion(f32[2048,256]{1,0:T(8,128)S(1)} %convolution_bitcast_fusion, f32[2048,256]{1,0:T(8,128)S(1)} %copy-done.3, bf16[512,256]{1,0:T(8,128)(2,1)} %bitcast.7, s32[512]{0:T(512)S(1)} %eq.22, pred[512]{0:T(512)(128)(4,1)S(1)} %lt.20), kind=kOutput, calls=%fused_computation.7 | convolution fusion | flops 541589504 | bytes 5507584 | tf_op jit(solution)/shard_map/dot_general | solution.py:235
  112.1 5.5 %all-to-all-done.5 = bf16[32,16,256]{2,1,0:T(8,128)(2,1)S(1)} async-done(((bf16[32,16,256]{2,1,0:T(8,128)(2,1)}), bf16[32,16,256]{2,1,0:T(8,128)(2,1)S(1)}, u32[]{:S(2)}, u32[]{:S(2)}) %all-to-all-start.5) | async-done | bytes 262176 | tf_op jit(solution)/shard_map/all_to_all | solution.py:222
  117.7 0.8 fusion.22
  (2 shorter events, 0.1 us)
Async XLA Ops:
  0.6 36.7 %copy-start = (bf16[256,256]{1,0:T(8,128)(2,1)S(1)}, bf16[256,256]{1,0:T(8,128)(2,1)}, u32[]{:S(2)}) copy-start(bf16[256,256]{1,0:T(8,128)(2,1)} %param.13) | copy-start | bytes 393220
  2.9 13.1 %all-to-all-start.1 = ((bf16[8,32,256]{2,1,0:T(8,128)(2,1)}), bf16[8,32,256]{2,1,0:T(8,128)(2,1)S(1)}, u32[]{:S(2)}, u32[]{:S(2)}) async-start(bf16[8,32,256]{2,1,0:T(8,128)(2,1)} %broadcast_in_dim.20), calls=%async_computation.1 | async-start | bytes 262144 | tf_op jit(solution)/shard_map/all_to_all | solution.py:179
  10.9 9.5 %copy-start.1 = (bf16[2048,256]{1,0:T(8,128)(2,1)S(1)}, bf16[2048,256]{1,0:T(8,128)(2,1)}, u32[]{:S(2)}) copy-start(bf16[2048,256]{1,0:T(8,128)(2,1)} %param.11) | copy-start | bytes 3145732
  10.9 9.5 %copy-start.4 = (bf16[256,256]{1,0:T(8,128)(2,1)S(1)}, bf16[256,256]{1,0:T(8,128)(2,1)}, u32[]{:S(2)}) copy-start(bf16[256,256]{1,0:T(8,128)(2,1)} %param.12) | copy-start | bytes 393220
  16.0 14.2 %all-to-all-start = ((bf16[32,16,256]{2,1,0:T(8,128)(2,1)}), bf16[32,16,256]{2,1,0:T(8,128)(2,1)S(1)}, u32[]{:S(2)}, u32[]{:S(2)}) async-start(bf16[32,16,256]{2,1,0:T(8,128)(2,1)} %bitcast.1), calls=%async_computation | async-start | bytes 524288 | tf_op jit(solution)/shard_map/all_to_all | solution.py:187
  31.4 5.9 %copy-start.6 = (bf16[2048,256]{1,0:T(8,128)(2,1)S(1)}, bf16[2048,256]{1,0:T(8,128)(2,1)}, u32[]{:S(2)}) copy-start(bf16[2048,256]{1,0:T(8,128)(2,1)} %param.14) | copy-start | bytes 3145732
  42.9 21.7 %copy-start.2 = (bf16[2048,256]{1,0:T(8,128)(2,1)S(1)}, bf16[2048,256]{1,0:T(8,128)(2,1)}, u32[]{:S(2)}) copy-start(bf16[2048,256]{1,0:T(8,128)(2,1)} %shard_map.138) | copy-start | bytes 3145732
  50.7 24.2 %all-to-all-start.2 = ((bf16[32,16,256]{2,1,0:T(8,128)(2,1)}), bf16[32,16,256]{2,1,0:T(8,128)(2,1)}, u32[]{:S(2)}, u32[]{:S(2)}) async-start(bf16[32,16,256]{2,1,0:T(8,128)(2,1)} %bitcast.34), calls=%async_computation.2 | async-start | bytes 524288 | tf_op jit(solution)/shard_map/all_to_all | solution.py:212
  65.0 12.5 %copy-start.5 = (s32[32]{0:T(128)S(1)}, s32[32]{0:T(128)}, u32[]{:S(2)}) copy-start(s32[32]{0:T(128)} %param.15) | copy-start | bytes 388
  74.9 19.0 %all-to-all-start.4 = ((f32[32,16,256]{2,1,0:T(8,128)}), f32[32,16,256]{2,1,0:T(8,128)S(1)}, u32[]{:S(2)}, u32[]{:S(2)}) async-start(f32[32,16,256]{2,1,0:T(8,128)} %bitcast.10), calls=%async_computation.4 | async-start | bytes 1048576 | tf_op jit(solution)/shard_map/all_to_all | solution.py:218
  93.9 10.1 %all-to-all-start.3 = ((bf16[8,32,256]{2,1,0:T(8,128)(2,1)}), bf16[8,32,256]{2,1,0:T(8,128)(2,1)S(1)}, u32[]{:S(2)}, u32[]{:S(2)}) async-start(bf16[8,32,256]{2,1,0:T(8,128)(2,1)} %bitcast.8), calls=%async_computation.3 | async-start | bytes 262144 | tf_op jit(solution)/shard_map/all_to_all | solution.py:226
  104.7 13.0 %all-to-all-start.5 = ((bf16[32,16,256]{2,1,0:T(8,128)(2,1)}), bf16[32,16,256]{2,1,0:T(8,128)(2,1)S(1)}, u32[]{:S(2)}, u32[]{:S(2)}) async-start(bf16[32,16,256]{2,1,0:T(8,128)(2,1)} %broadcast_in_dim.35), calls=%async_computation.5 | async-start | bytes 524288 | tf_op jit(solution)/shard_map/all_to_all | solution.py:222
  107.3 1.6 %copy-start.3 = (f32[2048,256]{1,0:T(8,128)S(1)}, f32[2048,256]{1,0:T(8,128)}, u32[]{:S(2)}) copy-start(f32[2048,256]{1,0:T(8,128)} %convolution_add_fusion.1) | copy-start | bytes 6291460

commit v8 on v7

--- a/solution.py
+++ b/solution.py
@@ -213,7 +213,14 @@
         returning, ("dom", "dev"), split_axis=0, concat_axis=0, tiled=True
     )
     partial = jnp.concatenate([local_ws, local_wn], axis=0)
-    partial, returned = lax.optimization_barrier((partial, returned))
+    hub_back = lax.all_to_all(
+        hub_part.reshape(group, hubs_dev, width),
+        "dev",
+        split_axis=0,
+        concat_axis=0,
+        tiled=True,
+    )
+    partial, returned, hub_back = lax.optimization_barrier((partial, returned, hub_back))
     parts = partial.reshape(peers, -1, width)
     gathered = lax.all_to_all(parts, ("dom", "dev"), split_axis=0, concat_axis=0, tiled=True)
     scale = 1.0 / jnp.sqrt(jnp.float32(rows * peers))
@@ -223,13 +230,6 @@
     summed = summed.reshape(partial.shape).astype(jnp.float32)
     grad_ws = summed[: w_self.shape[0]]
     grad_wn = summed[w_self.shape[0] :]
-    hub_back = lax.all_to_all(
-        hub_part.reshape(group, hubs_dev, width),
-        "dev",
-        split_axis=0,
-        concat_axis=0,
-        tiled=True,
-    )
     hub_spread = jnp.broadcast_to(hub_pick[None], (group,) + hub_pick.shape)
     grad = lax.dot_general(dpre, w_self, contract_cols, preferred_element_type=jnp.float32) + own
     grad = grad + lax.dot_general(

time: 119 us -> 120 us (level)
  blocking collectives: 0 us -> 21.2 us
  starting transfers between devices: 32.5 us -> 18.6 us
  waiting for transfers between devices: 43.8 us -> 37.2 us
    all_to_all x0 -> x1, blocking collectives: none -> 21.2 us  [body(): lax.all_to_all(hub_part.reshape(group, hubs_dev, width), 'dev', split_axi...]
    all_to_all x1, starting transfers between devices: 13.9 us -> 3.31 us  [body(): lax.all_to_all(returning, ('dom', 'dev'), split_axis=0, concat_axis=0, ti...]
    all_to_all x1, waiting for transfers between devices: 16.2 us -> 12.9 us  [body(): lax.all_to_all(parts, ('dom', 'dev'), split_axis=0, concat_axis=0, tiled=...]
    all_to_all x1 -> x0, starting transfers between devices: 3.37 us -> none  [body(): lax.all_to_all(hub_part.reshape(group, hubs_dev, width), 'dev', split_axi...]
    all_to_all x1 -> x0, waiting for transfers between devices: 3.27 us -> none  [body(): lax.all_to_all(hub_part.reshape(group, hubs_dev, width), 'dev', split_axi...]
  transfers between devices with their start and end apart: 6 -> 5, of which waited for: 6 -> 5; matrix products, arithmetic and copies ran while one was open for 13% -> 13% of each run, Pallas kernels for 0% -> 0%
where the time goes in v8:
time: 120 us; the launch traced here: 119 us
  waiting for transfers between devices  37.2 us (31%)
  blocking collectives  21.2 us (18%)
  matrix products  19.8 us (16%)
  starting transfers between devices  18.6 us (16%)
  Pallas kernels  13.7 us (11%)
  local copies, waits for them, and re-layouts  4.31 us (4%)
  other arithmetic  2.91 us (2%)
  between operations  1.42 us (1%)
    all_to_all x1, blocking collectives, body(): lax.all_to_all(hub_part.reshape(group, hubs_dev, width), 'dev', split_axi...  21.2 us
    all_to_all x1, waiting for transfers between devices, body(): lax.all_to_all(parts, ('dom', 'dev'), split_axis=0, concat_axis=0, tiled=...  12.9 us
    all_to_all x1, waiting for transfers between devices, body(): lax.all_to_all(returning, ('dom', 'dev'), split_axis=0, concat_axis=0, ti...  8.5 us
    all_to_all x1, waiting for transfers between devices, body(): lax.all_to_all(outgoing, ('dom', 'dev'), split_axis=0, concat_axis=0, til...  7.94 us
    pallas_call x1, Pallas kernels, tile_backward_t(): pl.pallas_call(kernel, out_shape=(jax.ShapeDtypeStruct((rows, width), jnp...  7.74 us
    all_to_all x1, starting transfers between devices, body(): lax.all_to_all(hub_out, 'dev', split_axis=0, concat_axis=0, tiled=True)  6.32 us
    pallas_call x1, Pallas kernels, tile_aggregate(): pl.pallas_call(kernel, out_shape=jax.ShapeDtypeStruct((rows, width), jnp....  5.93 us
    all_to_all x1, waiting for transfers between devices, body(): lax.all_to_all(spread_piece, ('dom', 'dev'), split_axis=0, concat_axis=0,...  5.56 us
  transfers between devices with their start and end apart: 5, of which 5 were waited for; matrix products, arithmetic and copies ran while one was open for 13% of the time, Pallas kernels for 0%

profile of v8, /device:TPU:0, one launch (start us, length us, event | category | flops | bytes accessed | tf_op | source)
XLA Modules:
  0.0 119.0 jit_solution(9892069509938315961)
XLA Ops:
  0.6 0.0 copy-start
  0.6 1.6 %convolution_convert_fusion.1 = bf16[32,256]{1,0:T(8,128)(2,1)S(1)} fusion(bf16[2048,256]{1,0:T(8,128)(2,1)} %param.11, s32[32]{0:T(128)} %param.15), kind=kOutput, calls=%fused_computation.22 | convolution fusion | flops 33628160 | bytes 1065088 | tf_op jit(solution)/shard_map/dot_general | solution.py:177
  2.2 0.7 broadcast_in_dim.20
  2.9 6.3 %all-to-all-start.1 = ((bf16[8,32,256]{2,1,0:T(8,128)(2,1)}), bf16[8,32,256]{2,1,0:T(8,128)(2,1)S(1)}, u32[]{:S(2)}, u32[]{:S(2)}) async-start(bf16[8,32,256]{2,1,0:T(8,128)(2,1)} %broadcast_in_dim.20), calls=%async_computation.1 | async-start | bytes 262144 | tf_op jit(solution)/shard_map/all_to_all | solution.py:179
  9.2 0.7 iota_compare_fusion.3
  10.0 0.1 lt.20
  10.1 0.8 copy.16
  10.8 0.1 eq.22
  10.9 0.0 copy-start.1
  10.9 0.0 copy-start.4
  10.9 2.8 %fusion.12 = bf16[512,256]{1,0:T(8,128)(2,1)} fusion(bf16[2048,256]{1,0:T(8,128)(2,1)} %param.11, s32[512]{0:T(512)S(1)} %eq.22, pred[512]{0:T(512)(128)(4,1)S(1)} %lt.20), kind=kOutput, calls=%fused_computation.20 | convolution fusion | flops 540147712 | bytes 1313280 | tf_op jit(solution)/shard_map/dot_general | solution.py:185
  13.7 2.3 %all-to-all-done.1 = bf16[8,32,256]{2,1,0:T(8,128)(2,1)S(1)} async-done(((bf16[8,32,256]{2,1,0:T(8,128)(2,1)}), bf16[8,32,256]{2,1,0:T(8,128)(2,1)S(1)}, u32[]{:S(2)}, u32[]{:S(2)}) %all-to-all-start.1) | async-done | bytes 131104 | tf_op jit(solution)/shard_map/all_to_all | solution.py:179
  16.0 3.8 %all-to-all-start = ((bf16[32,16,256]{2,1,0:T(8,128)(2,1)}), bf16[32,16,256]{2,1,0:T(8,128)(2,1)S(1)}, u32[]{:S(2)}, u32[]{:S(2)}) async-start(bf16[32,16,256]{2,1,0:T(8,128)(2,1)} %bitcast.1), calls=%async_computation | async-start | bytes 524288 | tf_op jit(solution)/shard_map/all_to_all | solution.py:187
  20.4 0.0 copy-done.1
  20.4 0.0 copy-done.4
  20.5 1.8 %fusion.23 = f32[2048,256]{1,0:T(8,128)} fusion(bf16[2048,256]{1,0:T(8,128)(2,1)S(1)} %copy-done.1, bf16[256,256]{1,0:T(8,128)(2,1)S(1)} %copy-done.4), kind=kOutput, calls=%fused_computation.35 | convolution fusion | flops 268435456 | bytes 3276800 | tf_op jit(solution)/shard_map/dot_general | solution.py:193
  22.2 7.9 %all-to-all-done = bf16[32,16,256]{2,1,0:T(8,128)(2,1)S(1)} async-done(((bf16[32,16,256]{2,1,0:T(8,128)(2,1)}), bf16[32,16,256]{2,1,0:T(8,128)(2,1)S(1)}, u32[]{:S(2)}, u32[]{:S(2)}) %all-to-all-start) | async-done | bytes 262176 | tf_op jit(solution)/shard_map/all_to_all | solution.py:187
  30.2 1.2 %pad_maximum_fusion.source_ref = bf16[2816,256]{1,0:T(8,128)(2,1)} fusion(bf16[256,256]{1,0:T(8,128)(2,1)S(1)} %bitcast.33, bf16[512,256]{1,0:T(8,128)(2,1)S(1)} %bitcast.32, bf16[2048,256]{1,0:T(8,128)(2,1)S(1)} %copy-done.1), kind=kLoop, calls=%fused_computation.19 | loop fusion | flops 4325376 | bytes 2883584 | tf_op jit(solution)/shard_map/concatenate | solution.py:188
  31.4 0.0 copy-start.6
  31.4 5.9 %shard_map.138 = bf16[2048,256]{1,0:T(8,128)(2,1)} custom-call(s32[320]{0:T(512)} %src_ref.3, s32[320]{0:T(512)} %dst_ref.3, s32[1]{0:T(128)S(6)} %copy.19.cnt_ref, bf16[320,128,128]{2,1,0:T(8,128)(2,1)} %val_ref.3, bf16[2816,256]{1,0:T(8,128)(2,1)} %pad_maximum_fusion.source_ref), custom_call_target="tpu_custom_call" | custom-call | tf_op jit(solution)/shard_map/pallas_call | solution.py:64
  37.3 0.0 copy-done
  37.3 0.0 copy-done.6
  37.3 4.1 %multiply_convert_fusion = (bf16[2048,256]{1,0:T(8,128)(2,1)S(1)}, bf16[2048,256]{1,0:T(8,128)(2,1)}) fusion(bf16[2048,256]{1,0:T(8,128)(2,1)S(1)} %copy-done.6, f32[2048,256]{1,0:T(8,128)} %fusion.23, bf16[2048,256]{1,0:T(8,128)(2,1)} %shard_map.138, bf16[256,256]{1,0:T(8,128)(2,1)S(1)} %copy-done), kind=kOutput, calls=%fused_computation.12 | convolution fusion | flops 275251200 | bytes 6422528 | tf_op jit(solution)/shard_map/dot_general | solution.py:193
  41.4 1.4 %fusion.3.daggT_ref = bf16[256,2048]{1,0:T(8,128)(2,1)} fusion(bf16[2048,256]{1,0:T(8,128)(2,1)S(1)} %get-tuple-element.16, bf16[256,256]{1,0:T(8,128)(2,1)S(1)} %copy-done), kind=kOutput, calls=%fused_computation.9 | convolution fusion | flops 268959744 | bytes 2228224 | tf_op jit(solution)/shard_map/dot_general | solution.py:205
  42.9 0.0 copy-start.2
  42.9 7.7 %shard_map.139 = (f32[2048,256]{1,0:T(8,128)}, bf16[512,256]{1,0:T(8,128)(2,1)}, bf16[256,256]{1,0:T(8,128)(2,1)}) custom-call(s32[320]{0:T(512)} %src_ref.3, s32[320]{0:T(512)} %dst_ref.3, s32[1]{0:T(128)S(6)} %copy.19.cnt_ref, bf16[320,128,128]{2,1,0:T(8,128)(2,1)} %val_ref.3, bf16[256,2048]{1,0:T(8,128)(2,1)} %fusion.3.daggT_ref), custom_call_target="tpu_custom_call" | custom-call | tf_op jit(solution)/shard_map/pallas_call | solution.py:132
  50.6 21.2 %all_to_all.30 = bf16[8,32,256]{2,1,0:T(8,128)(2,1)S(1)} all-to-all(bf16[8,32,256]{2,1,0:T(8,128)(2,1)} %bitcast.37), channel_id=1, replica_groups=mesh['dom'=4,'dev'=8] {'dev'}, dimensions={0} | all-to-all | bytes 262144 | tf_op jit(solution)/shard_map/all_to_all | solution.py:216
  71.8 3.3 %all-to-all-start.2 = ((bf16[32,16,256]{2,1,0:T(8,128)(2,1)}), bf16[32,16,256]{2,1,0:T(8,128)(2,1)}, u32[]{:S(2)}, u32[]{:S(2)}) async-start(bf16[32,16,256]{2,1,0:T(8,128)(2,1)} %bitcast.34), calls=%async_computation.2 | async-start | bytes 524288 | tf_op jit(solution)/shard_map/all_to_all | solution.py:212
  75.1 0.0 copy-done.2
  75.1 0.5 fusion.24
  75.6 0.0 copy-start.5
  75.6 0.5 convolution_bitcast_fusion.1
  76.1 0.8 pad_maximum_fusion.1
  77.0 8.5 %all-to-all-done.2 = bf16[32,16,256]{2,1,0:T(8,128)(2,1)} async-done(((bf16[32,16,256]{2,1,0:T(8,128)(2,1)}), bf16[32,16,256]{2,1,0:T(8,128)(2,1)}, u32[]{:S(2)}, u32[]{:S(2)}) %all-to-all-start.2) | async-done | bytes 262176 | tf_op jit(solution)/shard_map/all_to_all | solution.py:212
  85.5 2.6 %all-to-all-start.4 = ((f32[32,16,256]{2,1,0:T(8,128)}), f32[32,16,256]{2,1,0:T(8,128)S(1)}, u32[]{:S(2)}, u32[]{:S(2)}) async-start(f32[32,16,256]{2,1,0:T(8,128)} %bitcast.10), calls=%async_computation.4 | async-start | bytes 1048576 | tf_op jit(solution)/shard_map/all_to_all | solution.py:225
  88.1 0.0 copy-done.5
  88.1 0.1 fusion.18
  88.2 3.4 %convolution_add_fusion.1 = f32[2048,256]{1,0:T(8,128)} fusion(f32[2048,256]{1,0:T(8,128)} %get-tuple-element.10, bf16[2048,256]{1,0:T(8,128)(2,1)S(1)} %get-tuple-element.16, bf16[256,256]{1,0:T(8,128)(2,1)S(1)} %copy-done.4), kind=kOutput, calls=%fused_computation.5 | convolution fusion | flops 268959744 | bytes 5373952 | tf_op jit(solution)/shard_map/dot_general | solution.py:234
  91.6 12.9 %all-to-all-done.4 = f32[32,16,256]{2,1,0:T(8,128)S(1)} async-done(((f32[32,16,256]{2,1,0:T(8,128)}), f32[32,16,256]{2,1,0:T(8,128)S(1)}, u32[]{:S(2)}, u32[]{:S(2)}) %all-to-all-start.4) | async-done | bytes 524320 | tf_op jit(solution)/shard_map/all_to_all | solution.py:225
  104.5 0.7 broadcast_in_dim.35
  105.2 2.6 %all-to-all-start.5 = ((bf16[32,16,256]{2,1,0:T(8,128)(2,1)}), bf16[32,16,256]{2,1,0:T(8,128)(2,1)S(1)}, u32[]{:S(2)}, u32[]{:S(2)}) async-start(bf16[32,16,256]{2,1,0:T(8,128)(2,1)} %broadcast_in_dim.35), calls=%async_computation.5 | async-start | bytes 524288 | tf_op jit(solution)/shard_map/all_to_all | solution.py:229
  107.8 0.0 copy-start.3
  107.8 0.5 convolution_bitcast_fusion
  108.3 1.1 copy-done.3
  109.4 3.2 %fusion.2 = bf16[2048,256]{1,0:T(8,128)(2,1)} fusion(f32[2048,256]{1,0:T(8,128)S(1)} %convolution_bitcast_fusion, f32[2048,256]{1,0:T(8,128)S(1)} %copy-done.3, bf16[512,256]{1,0:T(8,128)(2,1)} %bitcast.8, s32[512]{0:T(512)S(1)} %eq.22, pred[512]{0:T(512)(128)(4,1)S(1)} %lt.20), kind=kOutput, calls=%fused_computation.7 | convolution fusion | flops 541589504 | bytes 5507584 | tf_op jit(solution)/shard_map/dot_general | solution.py:235
  112.6 5.6 %all-to-all-done.5 = bf16[32,16,256]{2,1,0:T(8,128)(2,1)S(1)} async-done(((bf16[32,16,256]{2,1,0:T(8,128)(2,1)}), bf16[32,16,256]{2,1,0:T(8,128)(2,1)S(1)}, u32[]{:S(2)}, u32[]{:S(2)}) %all-to-all-start.5) | async-done | bytes 262176 | tf_op jit(solution)/shard_map/all_to_all | solution.py:229
  118.2 0.8 fusion.22
  (2 shorter events, 0.1 us)
Async XLA Ops:
  0.6 36.7 %copy-start = (bf16[256,256]{1,0:T(8,128)(2,1)S(1)}, bf16[256,256]{1,0:T(8,128)(2,1)}, u32[]{:S(2)}) copy-start(bf16[256,256]{1,0:T(8,128)(2,1)} %param.13) | copy-start | bytes 393220
  2.9 13.1 %all-to-all-start.1 = ((bf16[8,32,256]{2,1,0:T(8,128)(2,1)}), bf16[8,32,256]{2,1,0:T(8,128)(2,1)S(1)}, u32[]{:S(2)}, u32[]{:S(2)}) async-start(bf16[8,32,256]{2,1,0:T(8,128)(2,1)} %broadcast_in_dim.20), calls=%async_computation.1 | async-start | bytes 262144 | tf_op jit(solution)/shard_map/all_to_all | solution.py:179
  10.9 9.5 %copy-start.1 = (bf16[2048,256]{1,0:T(8,128)(2,1)S(1)}, bf16[2048,256]{1,0:T(8,128)(2,1)}, u32[]{:S(2)}) copy-start(bf16[2048,256]{1,0:T(8,128)(2,1)} %param.11) | copy-start | bytes 3145732
  10.9 9.5 %copy-start.4 = (bf16[256,256]{1,0:T(8,128)(2,1)S(1)}, bf16[256,256]{1,0:T(8,128)(2,1)}, u32[]{:S(2)}) copy-start(bf16[256,256]{1,0:T(8,128)(2,1)} %param.12) | copy-start | bytes 393220
  16.0 14.2 %all-to-all-start = ((bf16[32,16,256]{2,1,0:T(8,128)(2,1)}), bf16[32,16,256]{2,1,0:T(8,128)(2,1)S(1)}, u32[]{:S(2)}, u32[]{:S(2)}) async-start(bf16[32,16,256]{2,1,0:T(8,128)(2,1)} %bitcast.1), calls=%async_computation | async-start | bytes 524288 | tf_op jit(solution)/shard_map/all_to_all | solution.py:187
  31.4 5.9 %copy-start.6 = (bf16[2048,256]{1,0:T(8,128)(2,1)S(1)}, bf16[2048,256]{1,0:T(8,128)(2,1)}, u32[]{:S(2)}) copy-start(bf16[2048,256]{1,0:T(8,128)(2,1)} %param.14) | copy-start | bytes 3145732
  42.9 32.2 %copy-start.2 = (bf16[2048,256]{1,0:T(8,128)(2,1)S(1)}, bf16[2048,256]{1,0:T(8,128)(2,1)}, u32[]{:S(2)}) copy-start(bf16[2048,256]{1,0:T(8,128)(2,1)} %shard_map.138) | copy-start | bytes 3145732
  71.8 13.7 %all-to-all-start.2 = ((bf16[32,16,256]{2,1,0:T(8,128)(2,1)}), bf16[32,16,256]{2,1,0:T(8,128)(2,1)}, u32[]{:S(2)}, u32[]{:S(2)}) async-start(bf16[32,16,256]{2,1,0:T(8,128)(2,1)} %bitcast.34), calls=%async_computation.2 | async-start | bytes 524288 | tf_op jit(solution)/shard_map/all_to_all | solution.py:212
  75.6 12.5 %copy-start.5 = (s32[32]{0:T(128)S(1)}, s32[32]{0:T(128)}, u32[]{:S(2)}) copy-start(s32[32]{0:T(128)} %param.15) | copy-start | bytes 388
  85.5 19.0 %all-to-all-start.4 = ((f32[32,16,256]{2,1,0:T(8,128)}), f32[32,16,256]{2,1,0:T(8,128)S(1)}, u32[]{:S(2)}, u32[]{:S(2)}) async-start(f32[32,16,256]{2,1,0:T(8,128)} %bitcast.10), calls=%async_computation.4 | async-start | bytes 1048576 | tf_op jit(solution)/shard_map/all_to_all | solution.py:225
  105.2 13.0 %all-to-all-start.5 = ((bf16[32,16,256]{2,1,0:T(8,128)(2,1)}), bf16[32,16,256]{2,1,0:T(8,128)(2,1)S(1)}, u32[]{:S(2)}, u32[]{:S(2)}) async-start(bf16[32,16,256]{2,1,0:T(8,128)(2,1)} %broadcast_in_dim.35), calls=%async_computation.5 | async-start | bytes 524288 | tf_op jit(solution)/shard_map/all_to_all | solution.py:229
  107.8 1.6 %copy-start.3 = (f32[2048,256]{1,0:T(8,128)S(1)}, f32[2048,256]{1,0:T(8,128)}, u32[]{:S(2)}) copy-start(f32[2048,256]{1,0:T(8,128)} %convolution_add_fusion.1) | copy-start | bytes 6291460

commit v9 on v8

--- a/solution.py
+++ b/solution.py
@@ -73,10 +73,10 @@
         compiler_params=pltpu.CompilerParams(dimension_semantics=("arbitrary",)),
     )(tile_src, tile_dst, tile_count, tile_val, source)
 
-def _back_kernel(src_ref, dst_ref, cnt_ref, val_ref, daggT_ref, own_ref, ret_ref, hub_ref, acc_ref, *, tb, edge, batch):
+def _back_kernel(src_ref, dst_ref, cnt_ref, val_ref, dagg_ref, own_ref, ret_ref, hub_ref, acc_ref, *, tb, edge, batch):
     i = pl.program_id(0)
-    last_src = acc_ref.shape[1] // edge - 1
-    last_dst = daggT_ref.shape[1] // edge - 1
+    last_src = acc_ref.shape[0] // edge - 1
+    last_dst = dagg_ref.shape[0] // edge - 1
     rows = own_ref.shape[0]
 
     @pl.when(i == 0)
@@ -87,13 +87,13 @@
 
     def one(t, k):
         d = jnp.clip(dst_ref[t], 0, last_dst)
-        y = daggT_ref[:, pl.ds(pl.multiple_of(d * edge, edge), edge)]
-        return jnp.dot(y, val_ref[k], preferred_element_type=jnp.float32)
+        y = dagg_ref[pl.ds(pl.multiple_of(d * edge, edge), edge), :]
+        return lax.dot_general(val_ref[k], y, (((0,), (0,)), ((), ())), preferred_element_type=jnp.float32)
 
     def add(t, term):
         s = jnp.clip(src_ref[t], 0, last_src)
-        cols = pl.ds(pl.multiple_of(s * edge, edge), edge)
-        acc_ref[:, cols] += term
+        block = pl.ds(pl.multiple_of(s * edge, edge), edge)
+        acc_ref[block, :] += term
 
     full = (i + 1) * tb <= count
 
@@ -119,15 +119,15 @@
 
     @pl.when(i == pl.num_programs(0) - 1)
     def _():
-        own_ref[...] = acc_ref[:, :rows].T
         split = rows + ret_ref.shape[0]
-        ret_ref[...] = acc_ref[:, rows:split].T.astype(ret_ref.dtype)
-        hub_ref[...] = acc_ref[:, split:].T.astype(hub_ref.dtype)
-
-
-def tile_backward_t(tile_src, tile_dst, tile_count, tile_val, daggT, src_rows, ret_rows, tb=16, batch=1):
+        own_ref[...] = acc_ref[:rows, :]
+        ret_ref[...] = acc_ref[rows:split, :].astype(ret_ref.dtype)
+        hub_ref[...] = acc_ref[split:, :].astype(hub_ref.dtype)
+
+
+def tile_backward(tile_src, tile_dst, tile_count, tile_val, dagg, src_rows, ret_rows, tb=16, batch=1):
     tiles, edge, _ = tile_val.shape
-    width, rows = daggT.shape
+    rows, width = dagg.shape
     kernel = functools.partial(_back_kernel, tb=tb, edge=edge, batch=batch)
     return pl.pallas_call(
         kernel,
@@ -139,13 +139,13 @@
         grid_spec=pltpu.PrefetchScalarGridSpec(
             num_scalar_prefetch=3, grid=(tiles // tb,),
             in_specs=[pl.BlockSpec((tb, edge, edge), _val_map(tb)),
-                      pl.BlockSpec(daggT.shape, lambda i, s, d, c: (0, 0))],
+                      pl.BlockSpec(dagg.shape, lambda i, s, d, c: (0, 0))],
             out_specs=[pl.BlockSpec((rows, width), lambda i, s, d, c: (0, 0)),
                        pl.BlockSpec((ret_rows, width), lambda i, s, d, c: (0, 0)),
                        pl.BlockSpec((src_rows - rows - ret_rows, width), lambda i, s, d, c: (0, 0))],
-            scratch_shapes=[pltpu.VMEM((width, src_rows), jnp.float32)]),
+            scratch_shapes=[pltpu.VMEM((src_rows, width), jnp.float32)]),
         compiler_params=pltpu.CompilerParams(dimension_semantics=("arbitrary",)),
-    )(tile_src, tile_dst, tile_count, tile_val, daggT)
+    )(tile_src, tile_dst, tile_count, tile_val, dagg)
 
 
 def one_hot_rows(index, count):
@@ -202,11 +202,11 @@
     local_wn = lax.dot_general(agg, dpre, contract_rows, preferred_element_type=jnp.float32)
 
     contract_cols = (((1,), (1,)), ((), ()))
-    dagg_t = lax.dot_general(w_neigh, dpre, contract_cols, preferred_element_type=jnp.float32).astype(
+    dagg = lax.dot_general(dpre, w_neigh, contract_cols, preferred_element_type=jnp.float32).astype(
         jnp.bfloat16
     )
-    own, returning, hub_part = tile_backward_t(
-        tile_src, tile_dst, tile_count, tile_val, dagg_t, source.shape[0], peers * slots, tb=tb
+    own, returning, hub_part = tile_backward(
+        tile_src, tile_dst, tile_count, tile_val, dagg, source.shape[0], peers * slots, tb=tb
     )
     returning = returning.reshape(peers, slots, width)
     returned = lax.all_to_all(

time: 120 us -> 116 us (0.967)
  blocking collectives: 21.2 us -> 18.9 us
  Pallas kernels: 13.7 us -> 12.4 us
    all_to_all x1, blocking collectives: 21.2 us -> 18.9 us  [body(): lax.all_to_all(hub_part.reshape(group, hubs_dev, width), 'dev', split_axi...]
    pallas_call x1, Pallas kernels: 7.74 us -> 6.43 us  [tile_backward(): pl.pallas_call(kernel, out_shape=(jax.ShapeDtypeStruct((rows, width), jnp...]
where the time goes in v9:
time: 116 us; the launch traced here: 115 us
  waiting for transfers between devices  37.2 us (32%)
  matrix products  19.8 us (17%)
  blocking collectives  18.9 us (16%)
  starting transfers between devices  18.6 us (16%)
  Pallas kernels  12.4 us (11%)
  local copies, waits for them, and re-layouts  4.31 us (4%)
  other arithmetic  2.91 us (3%)
  between operations  1.42 us (1%)
    all_to_all x1, blocking collectives, body(): lax.all_to_all(hub_part.reshape(group, hubs_dev, width), 'dev', split_axi...  18.9 us
    all_to_all x1, waiting for transfers between devices, body(): lax.all_to_all(parts, ('dom', 'dev'), split_axis=0, concat_axis=0, tiled=...  12.9 us
    all_to_all x1, waiting for transfers between devices, body(): lax.all_to_all(returning, ('dom', 'dev'), split_axis=0, concat_axis=0, ti...  8.5 us
    all_to_all x1, waiting for transfers between devices, body(): lax.all_to_all(outgoing, ('dom', 'dev'), split_axis=0, concat_axis=0, til...  7.94 us
    pallas_call x1, Pallas kernels, tile_backward(): pl.pallas_call(kernel, out_shape=(jax.ShapeDtypeStruct((rows, width), jnp...  6.43 us
    all_to_all x1, starting transfers between devices, body(): lax.all_to_all(hub_out, 'dev', split_axis=0, concat_axis=0, tiled=True)  6.32 us
    pallas_call x1, Pallas kernels, tile_aggregate(): pl.pallas_call(kernel, out_shape=jax.ShapeDtypeStruct((rows, width), jnp....  5.93 us
    all_to_all x1, waiting for transfers between devices, body(): lax.all_to_all(spread_piece, ('dom', 'dev'), split_axis=0, concat_axis=0,...  5.55 us
  transfers between devices with their start and end apart: 5, of which 5 were waited for; matrix products, arithmetic and copies ran while one was open for 13% of the time, Pallas kernels for 0%

profile of v9, /device:TPU:0, one launch (start us, length us, event | category | flops | bytes accessed | tf_op | source)
XLA Modules:
  0.0 115.4 jit_solution(7303719653744146412)
XLA Ops:
  0.6 0.0 copy-start
  0.6 1.6 %convolution_convert_fusion.1 = bf16[32,256]{1,0:T(8,128)(2,1)S(1)} fusion(bf16[2048,256]{1,0:T(8,128)(2,1)} %param.11, s32[32]{0:T(128)} %param.15), kind=kOutput, calls=%fused_computation.21 | convolution fusion | flops 33628160 | bytes 1065088 | tf_op jit(solution)/shard_map/dot_general | solution.py:177
  2.2 0.7 broadcast_in_dim.20
  2.9 6.3 %all-to-all-start.1 = ((bf16[8,32,256]{2,1,0:T(8,128)(2,1)}), bf16[8,32,256]{2,1,0:T(8,128)(2,1)S(1)}, u32[]{:S(2)}, u32[]{:S(2)}) async-start(bf16[8,32,256]{2,1,0:T(8,128)(2,1)} %broadcast_in_dim.20), calls=%async_computation.1 | async-start | bytes 262144 | tf_op jit(solution)/shard_map/all_to_all | solution.py:179
  9.2 0.7 iota_compare_fusion.3
  10.0 0.1 lt.20
  10.1 0.8 copy.15
  10.8 0.1 eq.22
  10.9 0.0 copy-start.1
  10.9 0.0 copy-start.4
  10.9 2.8 %fusion.11 = bf16[512,256]{1,0:T(8,128)(2,1)} fusion(bf16[2048,256]{1,0:T(8,128)(2,1)} %param.11, s32[512]{0:T(512)S(1)} %eq.22, pred[512]{0:T(512)(128)(4,1)S(1)} %lt.20), kind=kOutput, calls=%fused_computation.19 | convolution fusion | flops 540147712 | bytes 1313280 | tf_op jit(solution)/shard_map/dot_general | solution.py:185
  13.7 2.3 %all-to-all-done.1 = bf16[8,32,256]{2,1,0:T(8,128)(2,1)S(1)} async-done(((bf16[8,32,256]{2,1,0:T(8,128)(2,1)}), bf16[8,32,256]{2,1,0:T(8,128)(2,1)S(1)}, u32[]{:S(2)}, u32[]{:S(2)}) %all-to-all-start.1) | async-done | bytes 131104 | tf_op jit(solution)/shard_map/all_to_all | solution.py:179
  16.0 3.8 %all-to-all-start = ((bf16[32,16,256]{2,1,0:T(8,128)(2,1)}), bf16[32,16,256]{2,1,0:T(8,128)(2,1)S(1)}, u32[]{:S(2)}, u32[]{:S(2)}) async-start(bf16[32,16,256]{2,1,0:T(8,128)(2,1)} %bitcast.1), calls=%async_computation | async-start | bytes 524288 | tf_op jit(solution)/shard_map/all_to_all | solution.py:187
  20.4 0.0 copy-done.1
  20.4 0.0 copy-done.4
  20.5 1.8 %fusion.22 = f32[2048,256]{1,0:T(8,128)} fusion(bf16[2048,256]{1,0:T(8,128)(2,1)S(1)} %copy-done.1, bf16[256,256]{1,0:T(8,128)(2,1)S(1)} %copy-done.4), kind=kOutput, calls=%fused_computation.34 | convolution fusion | flops 268435456 | bytes 3276800 | tf_op jit(solution)/shard_map/dot_general | solution.py:193
  22.2 7.9 %all-to-all-done = bf16[32,16,256]{2,1,0:T(8,128)(2,1)S(1)} async-done(((bf16[32,16,256]{2,1,0:T(8,128)(2,1)}), bf16[32,16,256]{2,1,0:T(8,128)(2,1)S(1)}, u32[]{:S(2)}, u32[]{:S(2)}) %all-to-all-start) | async-done | bytes 262176 | tf_op jit(solution)/shard_map/all_to_all | solution.py:187
  30.2 1.2 %pad_maximum_fusion.source_ref = bf16[2816,256]{1,0:T(8,128)(2,1)} fusion(bf16[256,256]{1,0:T(8,128)(2,1)S(1)} %bitcast.31, bf16[512,256]{1,0:T(8,128)(2,1)S(1)} %bitcast.30, bf16[2048,256]{1,0:T(8,128)(2,1)S(1)} %copy-done.1), kind=kLoop, calls=%fused_computation.18 | loop fusion | flops 4325376 | bytes 2883584 | tf_op jit(solution)/shard_map/concatenate | solution.py:188
  31.4 0.0 copy-start.6
  31.4 5.9 %shard_map.138 = bf16[2048,256]{1,0:T(8,128)(2,1)} custom-call(s32[320]{0:T(512)} %src_ref.3, s32[320]{0:T(512)} %dst_ref.3, s32[1]{0:T(128)S(6)} %copy.16.cnt_ref, bf16[320,128,128]{2,1,0:T(8,128)(2,1)} %val_ref.3, bf16[2816,256]{1,0:T(8,128)(2,1)} %pad_maximum_fusion.source_ref), custom_call_target="tpu_custom_call" | custom-call | tf_op jit(solution)/shard_map/pallas_call | solution.py:64
  37.3 0.0 copy-done
  37.3 0.0 copy-done.6
  37.3 4.1 %multiply_convert_fusion = (bf16[2048,256]{1,0:T(8,128)(2,1)S(1)}, bf16[2048,256]{1,0:T(8,128)(2,1)}) fusion(bf16[2048,256]{1,0:T(8,128)(2,1)S(1)} %copy-done.6, f32[2048,256]{1,0:T(8,128)} %fusion.22, bf16[2048,256]{1,0:T(8,128)(2,1)} %shard_map.138, bf16[256,256]{1,0:T(8,128)(2,1)S(1)} %copy-done), kind=kOutput, calls=%fused_computation.11 | convolution fusion | flops 275251200 | bytes 6422528 | tf_op jit(solution)/shard_map/dot_general | solution.py:193
  41.4 1.4 %convolution_convert_fusion.dagg_ref = bf16[2048,256]{1,0:T(8,128)(2,1)} fusion(bf16[2048,256]{1,0:T(8,128)(2,1)S(1)} %get-tuple-element.16, bf16[256,256]{1,0:T(8,128)(2,1)S(1)} %copy-done), kind=kOutput, calls=%fused_computation.8 | convolution fusion | flops 268959744 | bytes 2228224 | tf_op jit(solution)/shard_map/dot_general | solution.py:205
  42.9 0.0 copy-start.2
  42.9 6.4 %shard_map.139 = (f32[2048,256]{1,0:T(8,128)}, bf16[512,256]{1,0:T(8,128)(2,1)}, bf16[256,256]{1,0:T(8,128)(2,1)}) custom-call(s32[320]{0:T(512)} %src_ref.3, s32[320]{0:T(512)} %dst_ref.3, s32[1]{0:T(128)S(6)} %copy.16.cnt_ref, bf16[320,128,128]{2,1,0:T(8,128)(2,1)} %val_ref.3, bf16[2048,256]{1,0:T(8,128)(2,1)} %convolution_convert_fusion.dagg_ref), custom_call_target="tpu_custom_call" | custom-call | tf_op jit(solution)/shard_map/pallas_call | solution.py:132
  49.3 18.9 %all_to_all.30 = bf16[8,32,256]{2,1,0:T(8,128)(2,1)S(1)} all-to-all(bf16[8,32,256]{2,1,0:T(8,128)(2,1)} %bitcast.35), channel_id=1, replica_groups=mesh['dom'=4,'dev'=8] {'dev'}, dimensions={0} | all-to-all | bytes 262144 | tf_op jit(solution)/shard_map/all_to_all | solution.py:216
  68.2 3.3 %all-to-all-start.2 = ((bf16[32,16,256]{2,1,0:T(8,128)(2,1)}), bf16[32,16,256]{2,1,0:T(8,128)(2,1)}, u32[]{:S(2)}, u32[]{:S(2)}) async-start(bf16[32,16,256]{2,1,0:T(8,128)(2,1)} %bitcast.32), calls=%async_computation.2 | async-start | bytes 524288 | tf_op jit(solution)/shard_map/all_to_all | solution.py:212
  71.5 0.0 copy-done.2
  71.5 0.5 fusion.23
  72.0 0.0 copy-start.5
  72.0 0.5 convolution_bitcast_fusion.1
  72.5 0.8 pad_maximum_fusion.1
  73.3 8.5 %all-to-all-done.2 = bf16[32,16,256]{2,1,0:T(8,128)(2,1)} async-done(((bf16[32,16,256]{2,1,0:T(8,128)(2,1)}), bf16[32,16,256]{2,1,0:T(8,128)(2,1)}, u32[]{:S(2)}, u32[]{:S(2)}) %all-to-all-start.2) | async-done | bytes 262176 | tf_op jit(solution)/shard_map/all_to_all | solution.py:212
  81.8 2.6 %all-to-all-start.4 = ((f32[32,16,256]{2,1,0:T(8,128)}), f32[32,16,256]{2,1,0:T(8,128)S(1)}, u32[]{:S(2)}, u32[]{:S(2)}) async-start(f32[32,16,256]{2,1,0:T(8,128)} %bitcast.9), calls=%async_computation.4 | async-start | bytes 1048576 | tf_op jit(solution)/shard_map/all_to_all | solution.py:225
  84.4 0.0 copy-done.5
  84.5 0.1 fusion.17
  84.6 3.4 %convolution_add_fusion.1 = f32[2048,256]{1,0:T(8,128)} fusion(f32[2048,256]{1,0:T(8,128)} %get-tuple-element.10, bf16[2048,256]{1,0:T(8,128)(2,1)S(1)} %get-tuple-element.16, bf16[256,256]{1,0:T(8,128)(2,1)S(1)} %copy-done.4), kind=kOutput, calls=%fused_computation.5 | convolution fusion | flops 268959744 | bytes 5373952 | tf_op jit(solution)/shard_map/dot_general | solution.py:234
  87.9 12.9 %all-to-all-done.4 = f32[32,16,256]{2,1,0:T(8,128)S(1)} async-done(((f32[32,16,256]{2,1,0:T(8,128)}), f32[32,16,256]{2,1,0:T(8,128)S(1)}, u32[]{:S(2)}, u32[]{:S(2)}) %all-to-all-start.4) | async-done | bytes 524320 | tf_op jit(solution)/shard_map/all_to_all | solution.py:225
  100.9 0.7 broadcast_in_dim.35
  101.6 2.6 %all-to-all-start.5 = ((bf16[32,16,256]{2,1,0:T(8,128)(2,1)}), bf16[32,16,256]{2,1,0:T(8,128)(2,1)S(1)}, u32[]{:S(2)}, u32[]{:S(2)}) async-start(bf16[32,16,256]{2,1,0:T(8,128)(2,1)} %broadcast_in_dim.35), calls=%async_computation.5 | async-start | bytes 524288 | tf_op jit(solution)/shard_map/all_to_all | solution.py:229
  104.2 0.0 copy-start.3
  104.2 0.5 convolution_bitcast_fusion
  104.7 1.1 copy-done.3
  105.8 3.2 %fusion.2 = bf16[2048,256]{1,0:T(8,128)(2,1)} fusion(f32[2048,256]{1,0:T(8,128)S(1)} %convolution_bitcast_fusion, f32[2048,256]{1,0:T(8,128)S(1)} %copy-done.3, bf16[512,256]{1,0:T(8,128)(2,1)} %bitcast.7, s32[512]{0:T(512)S(1)} %eq.22, pred[512]{0:T(512)(128)(4,1)S(1)} %lt.20), kind=kOutput, calls=%fused_computation.7 | convolution fusion | flops 541589504 | bytes 5507584 | tf_op jit(solution)/shard_map/dot_general | solution.py:235
  109.0 5.6 %all-to-all-done.5 = bf16[32,16,256]{2,1,0:T(8,128)(2,1)S(1)} async-done(((bf16[32,16,256]{2,1,0:T(8,128)(2,1)}), bf16[32,16,256]{2,1,0:T(8,128)(2,1)S(1)}, u32[]{:S(2)}, u32[]{:S(2)}) %all-to-all-start.5) | async-done | bytes 262176 | tf_op jit(solution)/shard_map/all_to_all | solution.py:229
  114.6 0.8 fusion.21
  (2 shorter events, 0.1 us)
Async XLA Ops:
  0.6 36.7 %copy-start = (bf16[256,256]{1,0:T(8,128)(2,1)S(1)}, bf16[256,256]{1,0:T(8,128)(2,1)}, u32[]{:S(2)}) copy-start(bf16[256,256]{1,0:T(8,128)(2,1)} %param.13) | copy-start | bytes 393220
  2.9 13.1 %all-to-all-start.1 = ((bf16[8,32,256]{2,1,0:T(8,128)(2,1)}), bf16[8,32,256]{2,1,0:T(8,128)(2,1)S(1)}, u32[]{:S(2)}, u32[]{:S(2)}) async-start(bf16[8,32,256]{2,1,0:T(8,128)(2,1)} %broadcast_in_dim.20), calls=%async_computation.1 | async-start | bytes 262144 | tf_op jit(solution)/shard_map/all_to_all | solution.py:179
  10.9 9.5 %copy-start.1 = (bf16[2048,256]{1,0:T(8,128)(2,1)S(1)}, bf16[2048,256]{1,0:T(8,128)(2,1)}, u32[]{:S(2)}) copy-start(bf16[2048,256]{1,0:T(8,128)(2,1)} %param.11) | copy-start | bytes 3145732
  10.9 9.5 %copy-start.4 = (bf16[256,256]{1,0:T(8,128)(2,1)S(1)}, bf16[256,256]{1,0:T(8,128)(2,1)}, u32[]{:S(2)}) copy-start(bf16[256,256]{1,0:T(8,128)(2,1)} %param.12) | copy-start | bytes 393220
  16.0 14.2 %all-to-all-start = ((bf16[32,16,256]{2,1,0:T(8,128)(2,1)}), bf16[32,16,256]{2,1,0:T(8,128)(2,1)S(1)}, u32[]{:S(2)}, u32[]{:S(2)}) async-start(bf16[32,16,256]{2,1,0:T(8,128)(2,1)} %bitcast.1), calls=%async_computation | async-start | bytes 524288 | tf_op jit(solution)/shard_map/all_to_all | solution.py:187
  31.4 5.9 %copy-start.6 = (bf16[2048,256]{1,0:T(8,128)(2,1)S(1)}, bf16[2048,256]{1,0:T(8,128)(2,1)}, u32[]{:S(2)}) copy-start(bf16[2048,256]{1,0:T(8,128)(2,1)} %param.14) | copy-start | bytes 3145732
  42.9 28.6 %copy-start.2 = (bf16[2048,256]{1,0:T(8,128)(2,1)S(1)}, bf16[2048,256]{1,0:T(8,128)(2,1)}, u32[]{:S(2)}) copy-start(bf16[2048,256]{1,0:T(8,128)(2,1)} %shard_map.138) | copy-start | bytes 3145732
  68.2 13.7 %all-to-all-start.2 = ((bf16[32,16,256]{2,1,0:T(8,128)(2,1)}), bf16[32,16,256]{2,1,0:T(8,128)(2,1)}, u32[]{:S(2)}, u32[]{:S(2)}) async-start(bf16[32,16,256]{2,1,0:T(8,128)(2,1)} %bitcast.32), calls=%async_computation.2 | async-start | bytes 524288 | tf_op jit(solution)/shard_map/all_to_all | solution.py:212
  72.0 12.5 %copy-start.5 = (s32[32]{0:T(128)S(1)}, s32[32]{0:T(128)}, u32[]{:S(2)}) copy-start(s32[32]{0:T(128)} %param.15) | copy-start | bytes 388
  81.8 19.0 %all-to-all-start.4 = ((f32[32,16,256]{2,1,0:T(8,128)}), f32[32,16,256]{2,1,0:T(8,128)S(1)}, u32[]{:S(2)}, u32[]{:S(2)}) async-start(f32[32,16,256]{2,1,0:T(8,128)} %bitcast.9), calls=%async_computation.4 | async-start | bytes 1048576 | tf_op jit(solution)/shard_map/all_to_all | solution.py:225
  101.6 13.0 %all-to-all-start.5 = ((bf16[32,16,256]{2,1,0:T(8,128)(2,1)}), bf16[32,16,256]{2,1,0:T(8,128)(2,1)S(1)}, u32[]{:S(2)}, u32[]{:S(2)}) async-start(bf16[32,16,256]{2,1,0:T(8,128)(2,1)} %broadcast_in_dim.35), calls=%async_computation.5 | async-start | bytes 524288 | tf_op jit(solution)/shard_map/all_to_all | solution.py:229
  104.2 1.6 %copy-start.3 = (f32[2048,256]{1,0:T(8,128)S(1)}, f32[2048,256]{1,0:T(8,128)}, u32[]{:S(2)}) copy-start(f32[2048,256]{1,0:T(8,128)} %convolution_add_fusion.1) | copy-start | bytes 6291460

commit v10 on v9

--- a/solution.py
+++ b/solution.py
@@ -173,18 +173,19 @@
     group = lax.axis_size("dev")
     hubs_dev = hub_rows.shape[0]
 
-    hub_pick = one_hot_rows(hub_rows, rows)
-    own_hubs = jnp.dot(hub_pick, feats, preferred_element_type=jnp.float32).astype(jnp.bfloat16)
-    hub_out = jnp.broadcast_to(own_hubs[None], (group, hubs_dev, width))
-    hub_table = lax.all_to_all(hub_out, "dev", split_axis=0, concat_axis=0, tiled=True)
-    hub_table = hub_table.reshape(group * hubs_dev, width)
-
     live = lax.broadcasted_iota(jnp.int32, (peers, slots), 1) < send_count[0][:, None]
     send_pick = one_hot_rows(send_rows[0].reshape(-1), rows)
     send_pick = jnp.where(live.reshape(-1, 1), send_pick, jnp.zeros((), jnp.bfloat16))
     outgoing = jnp.dot(send_pick, feats, preferred_element_type=jnp.float32).astype(jnp.bfloat16)
     outgoing = outgoing.reshape(peers, slots, width)
     incoming = lax.all_to_all(outgoing, ("dom", "dev"), split_axis=0, concat_axis=0, tiled=True)
+
+    hub_pick = one_hot_rows(hub_rows, rows)
+    own_hubs = jnp.dot(hub_pick, feats, preferred_element_type=jnp.float32).astype(jnp.bfloat16)
+    hub_out = jnp.broadcast_to(own_hubs[None], (group, hubs_dev, width))
+    hub_out, incoming = lax.optimization_barrier((hub_out, incoming))
+    hub_table = lax.all_to_all(hub_out, "dev", split_axis=0, concat_axis=0, tiled=True)
+    hub_table = hub_table.reshape(group * hubs_dev, width)
     source = jnp.concatenate([feats, incoming.reshape(peers * slots, width), hub_table], axis=0)
 
     tb = _tile_block(tile_val.shape[0])

time: 116 us -> 120 us (1.034)
  Pallas kernels: 12.4 us -> 21.9 us
  blocking collectives: 18.9 us -> 10.1 us
  waiting for transfers between devices: 37.2 us -> 41.3 us
  matrix products: 19.8 us -> 18.5 us
    all_to_all x1, blocking collectives: 18.9 us -> 10.1 us  [body(): lax.all_to_all(hub_part.reshape(group, hubs_dev, width), 'dev', split_axi...]
    pallas_call x1, Pallas kernels: 6.43 us -> 11.2 us  [tile_backward(): pl.pallas_call(kernel, out_shape=(jax.ShapeDtypeStruct((rows, width), jnp...]
    pallas_call x1, Pallas kernels: 5.93 us -> 10.7 us  [tile_aggregate(): pl.pallas_call(kernel, out_shape=jax.ShapeDtypeStruct((rows, width), jnp....]
    all_to_all x1, starting transfers between devices: 3.76 us -> 7.29 us  [body(): lax.all_to_all(outgoing, ('dom', 'dev'), split_axis=0, concat_axis=0, til...]
    all_to_all x1, starting transfers between devices: 6.32 us -> 3.37 us  [body(): lax.all_to_all(hub_out, 'dev', split_axis=0, concat_axis=0, tiled=True)]
    all_to_all x1, waiting for transfers between devices: 2.31 us -> 4.93 us  [body(): lax.all_to_all(hub_out, 'dev', split_axis=0, concat_axis=0, tiled=True)]
    all_to_all x1, waiting for transfers between devices: 7.94 us -> 9.4 us  [body(): lax.all_to_all(outgoing, ('dom', 'dev'), split_axis=0, concat_axis=0, til...]
    dot_general x1, matrix products: 1.6 us -> 0.32 us  [body(): jnp.dot(hub_pick, feats, preferred_element_type=jnp.float32)]
  transfers between devices with their start and end apart: 5 -> 5, of which waited for: 5 -> 5; matrix products, arithmetic and copies ran while one was open for 13% -> 9% of each run, Pallas kernels for 0% -> 0%
where the time goes in v10:
time: 120 us
  waiting for transfers between devices  41.3 us (34%)
  Pallas kernels  21.9 us (18%)
  starting transfers between devices  19.2 us (16%)
  matrix products  18.5 us (15%)
  blocking collectives  10.1 us (8%)
  local copies, waits for them, and re-layouts  4.31 us (4%)
  other arithmetic  2.95 us (2%)
  between operations  1.43 us (1%)
    all_to_all x1, waiting for transfers between devices, body(): lax.all_to_all(parts, ('dom', 'dev'), split_axis=0, concat_axis=0, tiled=...  12.9 us
    pallas_call x1, Pallas kernels, tile_backward(): pl.pallas_call(kernel, out_shape=(jax.ShapeDtypeStruct((rows, width), jnp...  11.2 us
    pallas_call x1, Pallas kernels, tile_aggregate(): pl.pallas_call(kernel, out_shape=jax.ShapeDtypeStruct((rows, width), jnp....  10.7 us
    all_to_all x1, blocking collectives, body(): lax.all_to_all(hub_part.reshape(group, hubs_dev, width), 'dev', split_axi...  10.1 us
    all_to_all x1, waiting for transfers between devices, body(): lax.all_to_all(outgoing, ('dom', 'dev'), split_axis=0, concat_axis=0, til...  9.4 us
    all_to_all x1, waiting for transfers between devices, body(): lax.all_to_all(returning, ('dom', 'dev'), split_axis=0, concat_axis=0, ti...  8.51 us
    all_to_all x1, starting transfers between devices, body(): lax.all_to_all(outgoing, ('dom', 'dev'), split_axis=0, concat_axis=0, til...  7.29 us
    all_to_all x1, waiting for transfers between devices, body(): lax.all_to_all(spread_piece, ('dom', 'dev'), split_axis=0, concat_axis=0,...  5.55 us
  transfers between devices with their start and end apart: 5, of which 5 were waited for; matrix products, arithmetic and copies ran while one was open for 9% of the time, Pallas kernels for 0%

profile of v10, /device:TPU:0, one launch (start us, length us, event | category | flops | bytes accessed | tf_op | source)
XLA Modules:
  0.0 119.6 jit_solution(7704067471811384101)
XLA Ops:
  0.6 0.0 copy-start
  0.6 0.8 iota_compare_fusion.3
  1.4 0.1 lt.20
  1.5 0.8 copy.15
  2.3 0.1 eq.24
  2.4 0.0 copy-start.1
  2.4 0.0 copy-start.5
  2.4 0.0 copy-start.4
  2.4 2.8 %fusion.11 = bf16[512,256]{1,0:T(8,128)(2,1)} fusion(bf16[2048,256]{1,0:T(8,128)(2,1)} %param.11, s32[512]{0:T(512)S(1)} %eq.24, pred[512]{0:T(512)(128)(4,1)S(1)} %lt.20), kind=kOutput, calls=%fused_computation.19 | convolution fusion | flops 540147712 | bytes 1313280 | tf_op jit(solution)/shard_map/dot_general | solution.py:179
  5.2 7.3 %all-to-all-start = ((bf16[32,16,256]{2,1,0:T(8,128)(2,1)}), bf16[32,16,256]{2,1,0:T(8,128)(2,1)S(1)}, u32[]{:S(2)}, u32[]{:S(2)}) async-start(bf16[32,16,256]{2,1,0:T(8,128)(2,1)} %bitcast.1), calls=%async_computation | async-start | bytes 524288 | tf_op jit(solution)/shard_map/all_to_all | solution.py:181
  13.1 0.0 copy-done.1
  13.1 0.0 copy-done.5
  13.1 0.3 convolution_convert_fusion.1
  13.5 9.4 %all-to-all-done = bf16[32,16,256]{2,1,0:T(8,128)(2,1)S(1)} async-done(((bf16[32,16,256]{2,1,0:T(8,128)(2,1)}), bf16[32,16,256]{2,1,0:T(8,128)(2,1)S(1)}, u32[]{:S(2)}, u32[]{:S(2)}) %all-to-all-start) | async-done | bytes 262176 | tf_op jit(solution)/shard_map/all_to_all | solution.py:181
  22.8 0.7 broadcast_in_dim.18
  23.5 3.4 %all-to-all-start.1 = ((bf16[8,32,256]{2,1,0:T(8,128)(2,1)}), bf16[8,32,256]{2,1,0:T(8,128)(2,1)S(1)}, u32[]{:S(2)}, u32[]{:S(2)}) async-start(bf16[8,32,256]{2,1,0:T(8,128)(2,1)} %broadcast_in_dim.18), calls=%async_computation.1 | async-start | bytes 262144 | tf_op jit(solution)/shard_map/all_to_all | solution.py:187
  26.9 0.0 copy-done.4
  26.9 1.8 %fusion.22 = f32[2048,256]{1,0:T(8,128)} fusion(bf16[2048,256]{1,0:T(8,128)(2,1)S(1)} %copy-done.1, bf16[256,256]{1,0:T(8,128)(2,1)S(1)} %copy-done.4), kind=kOutput, calls=%fused_computation.34 | convolution fusion | flops 268435456 | bytes 3276800 | tf_op jit(solution)/shard_map/dot_general | solution.py:194
  28.7 4.9 %all-to-all-done.1 = bf16[8,32,256]{2,1,0:T(8,128)(2,1)S(1)} async-done(((bf16[8,32,256]{2,1,0:T(8,128)(2,1)}), bf16[8,32,256]{2,1,0:T(8,128)(2,1)S(1)}, u32[]{:S(2)}, u32[]{:S(2)}) %all-to-all-start.1) | async-done | bytes 131104 | tf_op jit(solution)/shard_map/all_to_all | solution.py:187
  33.6 1.2 %pad_maximum_fusion.source_ref = bf16[2816,256]{1,0:T(8,128)(2,1)} fusion(bf16[256,256]{1,0:T(8,128)(2,1)S(1)} %bitcast.31, bf16[512,256]{1,0:T(8,128)(2,1)S(1)} %bitcast.30, bf16[2048,256]{1,0:T(8,128)(2,1)S(1)} %copy-done.1), kind=kLoop, calls=%fused_computation.18 | loop fusion | flops 4325376 | bytes 2883584 | tf_op jit(solution)/shard_map/concatenate | solution.py:189
  34.8 0.0 copy-start.6
  34.8 10.7 %shard_map.138 = bf16[2048,256]{1,0:T(8,128)(2,1)} custom-call(s32[320]{0:T(512)} %src_ref.3, s32[320]{0:T(512)} %dst_ref.3, s32[1]{0:T(128)S(6)} %copy.16.cnt_ref, bf16[320,128,128]{2,1,0:T(8,128)(2,1)} %val_ref.3, bf16[2816,256]{1,0:T(8,128)(2,1)} %pad_maximum_fusion.source_ref), custom_call_target="tpu_custom_call" | custom-call | tf_op jit(solution)/shard_map/pallas_call | solution.py:64
  45.5 0.0 copy-done
  45.5 0.0 copy-done.6
  45.5 4.1 %multiply_convert_fusion = (bf16[2048,256]{1,0:T(8,128)(2,1)S(1)}, bf16[2048,256]{1,0:T(8,128)(2,1)}) fusion(bf16[2048,256]{1,0:T(8,128)(2,1)S(1)} %copy-done.6, f32[2048,256]{1,0:T(8,128)} %fusion.22, bf16[2048,256]{1,0:T(8,128)(2,1)} %shard_map.138, bf16[256,256]{1,0:T(8,128)(2,1)S(1)} %copy-done), kind=kOutput, calls=%fused_computation.11 | convolution fusion | flops 275251200 | bytes 6422528 | tf_op jit(solution)/shard_map/dot_general | solution.py:194
  49.6 1.4 %convolution_convert_fusion.dagg_ref = bf16[2048,256]{1,0:T(8,128)(2,1)} fusion(bf16[2048,256]{1,0:T(8,128)(2,1)S(1)} %get-tuple-element.20, bf16[256,256]{1,0:T(8,128)(2,1)S(1)} %copy-done), kind=kOutput, calls=%fused_computation.8 | convolution fusion | flops 268959744 | bytes 2228224 | tf_op jit(solution)/shard_map/dot_general | solution.py:206
  51.0 0.0 copy-start.2
  51.0 11.2 %shard_map.139 = (f32[2048,256]{1,0:T(8,128)}, bf16[512,256]{1,0:T(8,128)(2,1)}, bf16[256,256]{1,0:T(8,128)(2,1)}) custom-call(s32[320]{0:T(512)} %src_ref.3, s32[320]{0:T(512)} %dst_ref.3, s32[1]{0:T(128)S(6)} %copy.16.cnt_ref, bf16[320,128,128]{2,1,0:T(8,128)(2,1)} %val_ref.3, bf16[2048,256]{1,0:T(8,128)(2,1)} %convolution_convert_fusion.dagg_ref), custom_call_target="tpu_custom_call" | custom-call | tf_op jit(solution)/shard_map/pallas_call | solution.py:132
  62.3 10.1 %all_to_all.30 = bf16[8,32,256]{2,1,0:T(8,128)(2,1)S(1)} all-to-all(bf16[8,32,256]{2,1,0:T(8,128)(2,1)} %bitcast.35), channel_id=1, replica_groups=mesh['dom'=4,'dev'=8] {'dev'}, dimensions={0} | all-to-all | bytes 262144 | tf_op jit(solution)/shard_map/all_to_all | solution.py:217
  72.3 3.3 %all-to-all-start.2 = ((bf16[32,16,256]{2,1,0:T(8,128)(2,1)}), bf16[32,16,256]{2,1,0:T(8,128)(2,1)}, u32[]{:S(2)}, u32[]{:S(2)}) async-start(bf16[32,16,256]{2,1,0:T(8,128)(2,1)} %bitcast.32), calls=%async_computation.2 | async-start | bytes 524288 | tf_op jit(solution)/shard_map/all_to_all | solution.py:213
  75.6 0.0 copy-done.2
  75.7 0.5 fusion.23
  76.1 0.5 convolution_bitcast_fusion.1
  76.7 0.8 pad_maximum_fusion.1
  77.5 8.5 %all-to-all-done.2 = bf16[32,16,256]{2,1,0:T(8,128)(2,1)} async-done(((bf16[32,16,256]{2,1,0:T(8,128)(2,1)}), bf16[32,16,256]{2,1,0:T(8,128)(2,1)}, u32[]{:S(2)}, u32[]{:S(2)}) %all-to-all-start.2) | async-done | bytes 262176 | tf_op jit(solution)/shard_map/all_to_all | solution.py:213
  86.0 2.6 %all-to-all-start.4 = ((f32[32,16,256]{2,1,0:T(8,128)}), f32[32,16,256]{2,1,0:T(8,128)S(1)}, u32[]{:S(2)}, u32[]{:S(2)}) async-start(f32[32,16,256]{2,1,0:T(8,128)} %bitcast.9), calls=%async_computation.4 | async-start | bytes 1048576 | tf_op jit(solution)/shard_map/all_to_all | solution.py:226
  88.6 0.1 fusion.17
  88.7 3.4 %convolution_add_fusion.1 = f32[2048,256]{1,0:T(8,128)} fusion(f32[2048,256]{1,0:T(8,128)} %get-tuple-element.14, bf16[2048,256]{1,0:T(8,128)(2,1)S(1)} %get-tuple-element.20, bf16[256,256]{1,0:T(8,128)(2,1)S(1)} %copy-done.4), kind=kOutput, calls=%fused_computation.5 | convolution fusion | flops 268959744 | bytes 5373952 | tf_op jit(solution)/shard_map/dot_general | solution.py:235
  92.1 12.9 %all-to-all-done.4 = f32[32,16,256]{2,1,0:T(8,128)S(1)} async-done(((f32[32,16,256]{2,1,0:T(8,128)}), f32[32,16,256]{2,1,0:T(8,128)S(1)}, u32[]{:S(2)}, u32[]{:S(2)}) %all-to-all-start.4) | async-done | bytes 524320 | tf_op jit(solution)/shard_map/all_to_all | solution.py:226
  105.0 0.7 broadcast_in_dim.35
  105.8 2.6 %all-to-all-start.5 = ((bf16[32,16,256]{2,1,0:T(8,128)(2,1)}), bf16[32,16,256]{2,1,0:T(8,128)(2,1)S(1)}, u32[]{:S(2)}, u32[]{:S(2)}) async-start(bf16[32,16,256]{2,1,0:T(8,128)(2,1)} %broadcast_in_dim.35), calls=%async_computation.5 | async-start | bytes 524288 | tf_op jit(solution)/shard_map/all_to_all | solution.py:230
  108.4 0.0 copy-start.3
  108.4 0.5 convolution_bitcast_fusion
  108.8 1.1 copy-done.3
  109.9 3.2 %fusion.2 = bf16[2048,256]{1,0:T(8,128)(2,1)} fusion(f32[2048,256]{1,0:T(8,128)S(1)} %convolution_bitcast_fusion, f32[2048,256]{1,0:T(8,128)S(1)} %copy-done.3, bf16[512,256]{1,0:T(8,128)(2,1)} %bitcast.7, s32[512]{0:T(512)S(1)} %eq.24, pred[512]{0:T(512)(128)(4,1)S(1)} %lt.20), kind=kOutput, calls=%fused_computation.7 | convolution fusion | flops 541589504 | bytes 5507584 | tf_op jit(solution)/shard_map/dot_general | solution.py:236
  113.2 5.6 %all-to-all-done.5 = bf16[32,16,256]{2,1,0:T(8,128)(2,1)S(1)} async-done(((bf16[32,16,256]{2,1,0:T(8,128)(2,1)}), bf16[32,16,256]{2,1,0:T(8,128)(2,1)S(1)}, u32[]{:S(2)}, u32[]{:S(2)}) %all-to-all-start.5) | async-done | bytes 262176 | tf_op jit(solution)/shard_map/all_to_all | solution.py:230
  118.7 0.8 fusion.21
  (2 shorter events, 0.1 us)
Async XLA Ops:
  0.6 44.9 %copy-start = (bf16[256,256]{1,0:T(8,128)(2,1)S(1)}, bf16[256,256]{1,0:T(8,128)(2,1)}, u32[]{:S(2)}) copy-start(bf16[256,256]{1,0:T(8,128)(2,1)} %param.13) | copy-start | bytes 393220
  2.4 10.8 %copy-start.1 = (bf16[2048,256]{1,0:T(8,128)(2,1)S(1)}, bf16[2048,256]{1,0:T(8,128)(2,1)}, u32[]{:S(2)}) copy-start(bf16[2048,256]{1,0:T(8,128)(2,1)} %param.11) | copy-start | bytes 3145732
  2.4 10.8 %copy-start.5 = (s32[32]{0:T(128)S(1)}, s32[32]{0:T(128)}, u32[]{:S(2)}) copy-start(s32[32]{0:T(128)} %param.15) | copy-start | bytes 388
  2.4 24.5 %copy-start.4 = (bf16[256,256]{1,0:T(8,128)(2,1)S(1)}, bf16[256,256]{1,0:T(8,128)(2,1)}, u32[]{:S(2)}) copy-start(bf16[256,256]{1,0:T(8,128)(2,1)} %param.12) | copy-start | bytes 393220
  5.2 17.7 %all-to-all-start = ((bf16[32,16,256]{2,1,0:T(8,128)(2,1)}), bf16[32,16,256]{2,1,0:T(8,128)(2,1)S(1)}, u32[]{:S(2)}, u32[]{:S(2)}) async-start(bf16[32,16,256]{2,1,0:T(8,128)(2,1)} %bitcast.1), calls=%async_computation | async-start | bytes 524288 | tf_op jit(solution)/shard_map/all_to_all | solution.py:181
  23.5 10.1 %all-to-all-start.1 = ((bf16[8,32,256]{2,1,0:T(8,128)(2,1)}), bf16[8,32,256]{2,1,0:T(8,128)(2,1)S(1)}, u32[]{:S(2)}, u32[]{:S(2)}) async-start(bf16[8,32,256]{2,1,0:T(8,128)(2,1)} %broadcast_in_dim.18), calls=%async_computation.1 | async-start | bytes 262144 | tf_op jit(solution)/shard_map/all_to_all | solution.py:187
  34.8 10.7 %copy-start.6 = (bf16[2048,256]{1,0:T(8,128)(2,1)S(1)}, bf16[2048,256]{1,0:T(8,128)(2,1)}, u32[]{:S(2)}) copy-start(bf16[2048,256]{1,0:T(8,128)(2,1)} %param.14) | copy-start | bytes 3145732
  51.0 24.6 %copy-start.2 = (bf16[2048,256]{1,0:T(8,128)(2,1)S(1)}, bf16[2048,256]{1,0:T(8,128)(2,1)}, u32[]{:S(2)}) copy-start(bf16[2048,256]{1,0:T(8,128)(2,1)} %shard_map.138) | copy-start | bytes 3145732
  72.3 13.7 %all-to-all-start.2 = ((bf16[32,16,256]{2,1,0:T(8,128)(2,1)}), bf16[32,16,256]{2,1,0:T(8,128)(2,1)}, u32[]{:S(2)}, u32[]{:S(2)}) async-start(bf16[32,16,256]{2,1,0:T(8,128)(2,1)} %bitcast.32), calls=%async_computation.2 | async-start | bytes 524288 | tf_op jit(solution)/shard_map/all_to_all | solution.py:213
  86.0 19.0 %all-to-all-start.4 = ((f32[32,16,256]{2,1,0:T(8,128)}), f32[32,16,256]{2,1,0:T(8,128)S(1)}, u32[]{:S(2)}, u32[]{:S(2)}) async-start(f32[32,16,256]{2,1,0:T(8,128)} %bitcast.9), calls=%async_computation.4 | async-start | bytes 1048576 | tf_op jit(solution)/shard_map/all_to_all | solution.py:226
  105.8 13.0 %all-to-all-start.5 = ((bf16[32,16,256]{2,1,0:T(8,128)(2,1)}), bf16[32,16,256]{2,1,0:T(8,128)(2,1)S(1)}, u32[]{:S(2)}, u32[]{:S(2)}) async-start(bf16[32,16,256]{2,1,0:T(8,128)(2,1)} %broadcast_in_dim.35), calls=%async_computation.5 | async-start | bytes 524288 | tf_op jit(solution)/shard_map/all_to_all | solution.py:230
  108.4 1.6 %copy-start.3 = (f32[2048,256]{1,0:T(8,128)S(1)}, f32[2048,256]{1,0:T(8,128)}, u32[]{:S(2)}) copy-start(f32[2048,256]{1,0:T(8,128)} %convolution_add_fusion.1) | copy-start | bytes 6291460

commit v11 on v9

--- a/solution.py
+++ b/solution.py
@@ -21,7 +21,8 @@
         return (jnp.minimum(i, last), 0, 0)
     return index_map
 
-def _agg_kernel(src_ref, dst_ref, cnt_ref, val_ref, source_ref, out_ref, acc_ref, *, tb, edge, batch):
+def _agg_kernel(src_ref, dst_ref, cnt_ref, val_ref, source_ref, fws_ref, wn_ref, cot_ref,
+                agg_ref, out_ref, dpre_ref, dagg_ref, acc_ref, *, tb, edge, batch):
     i = pl.program_id(0)
     last_src = source_ref.shape[0] // edge - 1
     last_dst = acc_ref.shape[0] // edge - 1
@@ -55,23 +56,43 @@
         lax.fori_loop(0, tb, body, 0)
     @pl.when(i == pl.num_programs(0) - 1)
     def _():
-        out_ref[...] = acc_ref[...].astype(out_ref.dtype)
-
-def tile_aggregate(tile_src, tile_dst, tile_count, tile_val, source, rows, tb=16, batch=1):
+        def rows_block(r, carry):
+            blk = pl.ds(pl.multiple_of(r * edge, edge), edge)
+            agg = acc_ref[blk, :].astype(jnp.bfloat16)
+            agg_ref[blk, :] = agg
+            pre = fws_ref[blk, :] + jnp.dot(agg, wn_ref[...], preferred_element_type=jnp.float32)
+            sig = jax.nn.sigmoid(pre)
+            out_ref[blk, :] = (pre * sig).astype(out_ref.dtype)
+            cot = cot_ref[blk, :].astype(jnp.float32)
+            dpre = (cot * sig * (1.0 + pre * (1.0 - sig))).astype(jnp.bfloat16)
+            dpre_ref[blk, :] = dpre
+            dagg = lax.dot_general(dpre, wn_ref[...], (((1,), (1,)), ((), ())), preferred_element_type=jnp.float32)
+            dagg_ref[blk, :] = dagg.astype(dagg_ref.dtype)
+            return carry
+
+        lax.fori_loop(0, acc_ref.shape[0] // edge, rows_block, 0)
+
+def tile_aggregate(tile_src, tile_dst, tile_count, tile_val, source, fws, w_neigh, cotangent, tb=16, batch=1):
     tiles, edge, _ = tile_val.shape
-    width = source.shape[1]
+    rows, width = fws.shape
     kernel = functools.partial(_agg_kernel, tb=tb, edge=edge, batch=batch)
+    whole = lambda i, s, d, c: (0, 0)
+    row_out = jax.ShapeDtypeStruct((rows, width), jnp.bfloat16)
     return pl.pallas_call(
         kernel,
-        out_shape=jax.ShapeDtypeStruct((rows, width), jnp.bfloat16),
+        out_shape=(row_out, row_out, row_out, row_out),
         grid_spec=pltpu.PrefetchScalarGridSpec(
             num_scalar_prefetch=3, grid=(tiles // tb,),
             in_specs=[pl.BlockSpec((tb, edge, edge), _val_map(tb)),
-                      pl.BlockSpec(source.shape, lambda i, s, d, c: (0, 0))],
-            out_specs=pl.BlockSpec((rows, width), lambda i, s, d, c: (0, 0)),
+                      pl.BlockSpec(source.shape, whole),
+                      pl.BlockSpec(fws.shape, whole),
+                      pl.BlockSpec(w_neigh.shape, whole),
+                      pl.BlockSpec(cotangent.shape, whole)],
+            out_specs=[pl.BlockSpec((rows, width), whole) for _ in range(4)],
             scratch_shapes=[pltpu.VMEM((rows, width), jnp.float32)]),
         compiler_params=pltpu.CompilerParams(dimension_semantics=("arbitrary",)),
-    )(tile_src, tile_dst, tile_count, tile_val, source)
+    )(tile_src, tile_dst, tile_count, tile_val, source, fws, w_neigh, cotangent)
+
 
 def _back_kernel(src_ref, dst_ref, cnt_ref, val_ref, dagg_ref, own_ref, ret_ref, hub_ref, acc_ref, *, tb, edge, batch):
     i = pl.program_id(0)
@@ -188,23 +209,16 @@
     source = jnp.concatenate([feats, incoming.reshape(peers * slots, width), hub_table], axis=0)
 
     tb = _tile_block(tile_val.shape[0])
-    agg = tile_aggregate(tile_src, tile_dst, tile_count, tile_val, source, rows, tb=tb)
-
-    pre = jnp.dot(feats, w_self, preferred_element_type=jnp.float32) + jnp.dot(
-        agg, w_neigh, preferred_element_type=jnp.float32
-    )
-    sig = jax.nn.sigmoid(pre)
-    out = (pre * sig).astype(jnp.bfloat16)
-    dpre = (cotangent.astype(jnp.float32) * sig * (1.0 + pre * (1.0 - sig))).astype(jnp.bfloat16)
+    fws = jnp.dot(feats, w_self, preferred_element_type=jnp.float32)
+    agg, out, dpre, dagg = tile_aggregate(
+        tile_src, tile_dst, tile_count, tile_val, source, fws, w_neigh, cotangent, tb=tb
+    )
 
     contract_rows = (((0,), (0,)), ((), ()))
     local_ws = lax.dot_general(feats, dpre, contract_rows, preferred_element_type=jnp.float32)
     local_wn = lax.dot_general(agg, dpre, contract_rows, preferred_element_type=jnp.float32)
 
     contract_cols = (((1,), (1,)), ((), ()))
-    dagg = lax.dot_general(dpre, w_neigh, contract_cols, preferred_element_type=jnp.float32).astype(
-        jnp.bfloat16
-    )
     own, returning, hub_part = tile_backward(
         tile_src, tile_dst, tile_count, tile_val, dagg, source.shape[0], peers * slots, tb=tb
     )

time: 116 us -> 118 us (1.017)
  Pallas kernels: 12.4 us -> 19.5 us
  matrix products: 19.8 us -> 13.3 us
    pallas_call x1, Pallas kernels: 5.93 us -> 13.1 us  [tile_aggregate(): pl.pallas_call(kernel, out_shape=(row_out, row_out, row_out, row_out), gr...]
    dot_general x3 -> x1, matrix products: 7.31 us -> 1.78 us  [body(): fws = jnp.dot(feats, w_self, preferred_element_type=jnp.float32)]
  transfers between devices with their start and end apart: 5 -> 5, of which waited for: 5 -> 5; matrix products, arithmetic and copies ran while one was open for 13% -> 12% of each run, Pallas kernels for 0% -> 0%
where the time goes in v11:
time: 118 us; the launch traced here: 117 us
  waiting for transfers between devices  38.1 us (32%)
  Pallas kernels  19.5 us (17%)
  blocking collectives  19.1 us (16%)
  starting transfers between devices  18.3 us (16%)
  matrix products  13.3 us (11%)
  local copies, waits for them, and re-layouts  4.31 us (4%)
  other arithmetic  2.91 us (2%)
  between operations  1.44 us (1%)
    all_to_all x1, blocking collectives, body(): lax.all_to_all(hub_part.reshape(group, hubs_dev, width), 'dev', split_axi...  19.1 us
    pallas_call x1, Pallas kernels, tile_aggregate(): pl.pallas_call(kernel, out_shape=(row_out, row_out, row_out, row_out), gr...  13.1 us
    all_to_all x1, waiting for transfers between devices, body(): lax.all_to_all(parts, ('dom', 'dev'), split_axis=0, concat_axis=0, tiled=...  12.8 us
    all_to_all x1, waiting for transfers between devices, body(): lax.all_to_all(returning, ('dom', 'dev'), split_axis=0, concat_axis=0, ti...  8.52 us
    all_to_all x1, waiting for transfers between devices, body(): lax.all_to_all(outgoing, ('dom', 'dev'), split_axis=0, concat_axis=0, til...  7.94 us
    all_to_all x1, waiting for transfers between devices, body(): lax.all_to_all(spread_piece, ('dom', 'dev'), split_axis=0, concat_axis=0,...  6.51 us
    pallas_call x1, Pallas kernels, tile_backward(): pl.pallas_call(kernel, out_shape=(jax.ShapeDtypeStruct((rows, width), jnp...  6.43 us
    all_to_all x1, starting transfers between devices, body(): lax.all_to_all(hub_out, 'dev', split_axis=0, concat_axis=0, tiled=True)  6.32 us
  transfers between devices with their start and end apart: 5, of which 5 were waited for; matrix products, arithmetic and copies ran while one was open for 12% of the time, Pallas kernels for 0%

profile of v11, /device:TPU:0, one launch (start us, length us, event | category | flops | bytes accessed | tf_op | source)
XLA Modules:
  0.0 117.0 jit_solution(1998953205303056876)
XLA Ops:
  0.6 0.0 copy-start
  0.6 1.6 %convolution_convert_fusion = bf16[32,256]{1,0:T(8,128)(2,1)S(1)} fusion(bf16[2048,256]{1,0:T(8,128)(2,1)} %param.11, s32[32]{0:T(128)} %param.15), kind=kOutput, calls=%fused_computation.16 | convolution fusion | flops 33628160 | bytes 1065088 | tf_op jit(solution)/shard_map/dot_general | solution.py:198
  2.2 0.7 broadcast_in_dim.20
  2.9 6.3 %all-to-all-start.1 = ((bf16[8,32,256]{2,1,0:T(8,128)(2,1)}), bf16[8,32,256]{2,1,0:T(8,128)(2,1)S(1)}, u32[]{:S(2)}, u32[]{:S(2)}) async-start(bf16[8,32,256]{2,1,0:T(8,128)(2,1)} %broadcast_in_dim.20), calls=%async_computation.1 | async-start | bytes 262144 | tf_op jit(solution)/shard_map/all_to_all | solution.py:200
  9.2 0.7 iota_compare_fusion.3
  10.0 0.1 lt.20
  10.1 0.8 copy.15
  10.8 0.1 eq.22
  10.9 0.0 copy-start.1
  10.9 2.8 %fusion.11 = bf16[512,256]{1,0:T(8,128)(2,1)} fusion(bf16[2048,256]{1,0:T(8,128)(2,1)} %param.11, s32[512]{0:T(512)S(1)} %eq.22, pred[512]{0:T(512)(128)(4,1)S(1)} %lt.20), kind=kOutput, calls=%fused_computation.14 | convolution fusion | flops 540147712 | bytes 1313280 | tf_op jit(solution)/shard_map/dot_general | solution.py:206
  13.7 2.3 %all-to-all-done.1 = bf16[8,32,256]{2,1,0:T(8,128)(2,1)S(1)} async-done(((bf16[8,32,256]{2,1,0:T(8,128)(2,1)}), bf16[8,32,256]{2,1,0:T(8,128)(2,1)S(1)}, u32[]{:S(2)}, u32[]{:S(2)}) %all-to-all-start.1) | async-done | bytes 131104 | tf_op jit(solution)/shard_map/all_to_all | solution.py:200
  16.0 3.7 %all-to-all-start = ((bf16[32,16,256]{2,1,0:T(8,128)(2,1)}), bf16[32,16,256]{2,1,0:T(8,128)(2,1)S(1)}, u32[]{:S(2)}, u32[]{:S(2)}) async-start(bf16[32,16,256]{2,1,0:T(8,128)(2,1)} %bitcast.1), calls=%async_computation | async-start | bytes 524288 | tf_op jit(solution)/shard_map/all_to_all | solution.py:208
  20.4 0.0 copy-done
  20.4 0.0 copy-done.1
  20.4 1.8 %fusion.22.fws_ref = f32[2048,256]{1,0:T(8,128)} fusion(bf16[2048,256]{1,0:T(8,128)(2,1)S(1)} %copy-done.1, bf16[256,256]{1,0:T(8,128)(2,1)S(1)} %copy-done), kind=kOutput, calls=%fused_computation.29 | convolution fusion | flops 268435456 | bytes 3276800 | tf_op jit(solution)/shard_map/dot_general | solution.py:212
  22.2 7.9 %all-to-all-done = bf16[32,16,256]{2,1,0:T(8,128)(2,1)S(1)} async-done(((bf16[32,16,256]{2,1,0:T(8,128)(2,1)}), bf16[32,16,256]{2,1,0:T(8,128)(2,1)S(1)}, u32[]{:S(2)}, u32[]{:S(2)}) %all-to-all-start) | async-done | bytes 262176 | tf_op jit(solution)/shard_map/all_to_all | solution.py:208
  30.2 1.2 %pad_maximum_fusion.source_ref = bf16[2816,256]{1,0:T(8,128)(2,1)} fusion(bf16[256,256]{1,0:T(8,128)(2,1)S(1)} %bitcast.27, bf16[512,256]{1,0:T(8,128)(2,1)S(1)} %bitcast.26, bf16[2048,256]{1,0:T(8,128)(2,1)S(1)} %copy-done.1), kind=kLoop, calls=%fused_computation.13 | loop fusion | flops 4325376 | bytes 2883584 | tf_op jit(solution)/shard_map/concatenate | solution.py:209
  31.4 13.1 %shard_map.138 = (bf16[2048,256]{1,0:T(8,128)(2,1)}, bf16[2048,256]{1,0:T(8,128)(2,1)}, bf16[2048,256]{1,0:T(8,128)(2,1)}, bf16[2048,256]{1,0:T(8,128)(2,1)}) custom-call(s32[320]{0:T(512)} %src_ref.3, s32[320]{0:T(512)} %dst_ref.3, s32[1]{0:T(128)S(6)} %copy.16.cnt_ref, bf16[320,128,128]{2,1,0:T(8,128)(2,1)} %val_ref.3, ...), custom_call_target="tpu_custom_call" | custom-call | tf_op jit(solution)/shard_map/pallas_call | solution.py:81
  44.4 0.0 copy-start.2
  44.4 6.4 %shard_map.139 = (f32[2048,256]{1,0:T(8,128)}, bf16[512,256]{1,0:T(8,128)(2,1)}, bf16[256,256]{1,0:T(8,128)(2,1)}) custom-call(s32[320]{0:T(512)} %src_ref.3, s32[320]{0:T(512)} %dst_ref.3, s32[1]{0:T(128)S(6)} %copy.16.cnt_ref, bf16[320,128,128]{2,1,0:T(8,128)(2,1)} %val_ref.3, bf16[2048,256]{1,0:T(8,128)(2,1)} %get-tuple-element.16.dagg_ref), custom_call_target="tpu_custom_call" | custom-call | tf_op jit(solution)/shard_map/pallas_call | solution.py:153
  50.9 0.0 copy-start.4
  50.9 19.1 %all_to_all.30 = bf16[8,32,256]{2,1,0:T(8,128)(2,1)} all-to-all(bf16[8,32,256]{2,1,0:T(8,128)(2,1)} %bitcast.32), channel_id=1, replica_groups=mesh['dom'=4,'dev'=8] {'dev'}, dimensions={0} | all-to-all | bytes 262144 | tf_op jit(solution)/shard_map/all_to_all | solution.py:230
  69.9 3.1 %all-to-all-start.2 = ((bf16[32,16,256]{2,1,0:T(8,128)(2,1)}), bf16[32,16,256]{2,1,0:T(8,128)(2,1)S(1)}, u32[]{:S(2)}, u32[]{:S(2)}) async-start(bf16[32,16,256]{2,1,0:T(8,128)(2,1)} %bitcast.29), calls=%async_computation.2 | async-start | bytes 524288 | tf_op jit(solution)/shard_map/all_to_all | solution.py:226
  73.0 0.0 copy-done.2
  73.0 0.5 convolution_bitcast_fusion.1
  73.5 0.0 copy-done.4
  73.6 0.0 copy-start.6
  73.6 0.5 fusion.23
  74.0 0.8 pad_maximum_fusion.1
  74.9 8.5 %all-to-all-done.2 = bf16[32,16,256]{2,1,0:T(8,128)(2,1)S(1)} async-done(((bf16[32,16,256]{2,1,0:T(8,128)(2,1)}), bf16[32,16,256]{2,1,0:T(8,128)(2,1)S(1)}, u32[]{:S(2)}, u32[]{:S(2)}) %all-to-all-start.2) | async-done | bytes 262176 | tf_op jit(solution)/shard_map/all_to_all | solution.py:226
  83.4 2.6 %all-to-all-start.4 = ((f32[32,16,256]{2,1,0:T(8,128)}), f32[32,16,256]{2,1,0:T(8,128)S(1)}, u32[]{:S(2)}, u32[]{:S(2)}) async-start(f32[32,16,256]{2,1,0:T(8,128)} %bitcast.9), calls=%async_computation.4 | async-start | bytes 1048576 | tf_op jit(solution)/shard_map/all_to_all | solution.py:239
  86.0 0.0 copy-done.6
  86.0 0.1 fusion.17
  86.1 0.0 copy-start.5
  86.1 3.4 %convolution_add_fusion.1 = f32[2048,256]{1,0:T(8,128)} fusion(f32[2048,256]{1,0:T(8,128)} %get-tuple-element.17, bf16[2048,256]{1,0:T(8,128)(2,1)S(1)} %copy-done.2, bf16[256,256]{1,0:T(8,128)(2,1)S(1)} %copy-done), kind=kOutput, calls=%fused_computation.5 | convolution fusion | flops 268959744 | bytes 5373952 | tf_op jit(solution)/shard_map/dot_general | solution.py:248
  89.5 12.8 %all-to-all-done.4 = f32[32,16,256]{2,1,0:T(8,128)S(1)} async-done(((f32[32,16,256]{2,1,0:T(8,128)}), f32[32,16,256]{2,1,0:T(8,128)S(1)}, u32[]{:S(2)}, u32[]{:S(2)}) %all-to-all-start.4) | async-done | bytes 524320 | tf_op jit(solution)/shard_map/all_to_all | solution.py:239
  102.4 0.7 broadcast_in_dim.35
  103.1 2.6 %all-to-all-start.5 = ((bf16[32,16,256]{2,1,0:T(8,128)(2,1)}), bf16[32,16,256]{2,1,0:T(8,128)(2,1)S(1)}, u32[]{:S(2)}, u32[]{:S(2)}) async-start(bf16[32,16,256]{2,1,0:T(8,128)(2,1)} %broadcast_in_dim.35), calls=%async_computation.5 | async-start | bytes 524288 | tf_op jit(solution)/shard_map/all_to_all | solution.py:243
  105.7 0.0 copy-done.5
  105.7 0.0 copy-start.3
  105.8 0.5 convolution_bitcast_fusion
  106.2 1.1 copy-done.3
  107.3 2.3 %fusion.2 = bf16[2048,256]{1,0:T(8,128)(2,1)} fusion(f32[2048,256]{1,0:T(8,128)S(1)} %convolution_bitcast_fusion, f32[2048,256]{1,0:T(8,128)S(1)} %copy-done.3, bf16[512,256]{1,0:T(8,128)(2,1)S(1)} %bitcast.28, s32[512]{0:T(512)S(1)} %eq.22, pred[512]{0:T(512)(128)(4,1)S(1)} %lt.20), kind=kOutput, calls=%fused_computation.6 | convolution fusion | flops 541589504 | bytes 5507584 | tf_op jit(solution)/shard_map/dot_general | solution.py:249
  109.6 6.5 %all-to-all-done.5 = bf16[32,16,256]{2,1,0:T(8,128)(2,1)S(1)} async-done(((bf16[32,16,256]{2,1,0:T(8,128)(2,1)}), bf16[32,16,256]{2,1,0:T(8,128)(2,1)S(1)}, u32[]{:S(2)}, u32[]{:S(2)}) %all-to-all-start.5) | async-done | bytes 262176 | tf_op jit(solution)/shard_map/all_to_all | solution.py:243
  116.1 0.8 fusion.21
  (2 shorter events, 0.1 us)
Async XLA Ops:
  0.6 19.8 %copy-start = (bf16[256,256]{1,0:T(8,128)(2,1)S(1)}, bf16[256,256]{1,0:T(8,128)(2,1)}, u32[]{:S(2)}) copy-start(bf16[256,256]{1,0:T(8,128)(2,1)} %param.12) | copy-start | bytes 393220
  2.9 13.1 %all-to-all-start.1 = ((bf16[8,32,256]{2,1,0:T(8,128)(2,1)}), bf16[8,32,256]{2,1,0:T(8,128)(2,1)S(1)}, u32[]{:S(2)}, u32[]{:S(2)}) async-start(bf16[8,32,256]{2,1,0:T(8,128)(2,1)} %broadcast_in_dim.20), calls=%async_computation.1 | async-start | bytes 262144 | tf_op jit(solution)/shard_map/all_to_all | solution.py:200
  10.9 9.5 %copy-start.1 = (bf16[2048,256]{1,0:T(8,128)(2,1)S(1)}, bf16[2048,256]{1,0:T(8,128)(2,1)}, u32[]{:S(2)}) copy-start(bf16[2048,256]{1,0:T(8,128)(2,1)} %param.11) | copy-start | bytes 3145732
  16.0 14.1 %all-to-all-start = ((bf16[32,16,256]{2,1,0:T(8,128)(2,1)}), bf16[32,16,256]{2,1,0:T(8,128)(2,1)S(1)}, u32[]{:S(2)}, u32[]{:S(2)}) async-start(bf16[32,16,256]{2,1,0:T(8,128)(2,1)} %bitcast.1), calls=%async_computation | async-start | bytes 524288 | tf_op jit(solution)/shard_map/all_to_all | solution.py:208
  44.4 28.6 %copy-start.2 = (bf16[2048,256]{1,0:T(8,128)(2,1)S(1)}, bf16[2048,256]{1,0:T(8,128)(2,1)}, u32[]{:S(2)}) copy-start(bf16[2048,256]{1,0:T(8,128)(2,1)} %get-tuple-element.15) | copy-start | bytes 3145732
  50.9 22.7 %copy-start.4 = (bf16[2048,256]{1,0:T(8,128)(2,1)S(1)}, bf16[2048,256]{1,0:T(8,128)(2,1)}, u32[]{:S(2)}) copy-start(bf16[2048,256]{1,0:T(8,128)(2,1)} %get-tuple-element.18) | copy-start | bytes 3145732
  69.9 13.5 %all-to-all-start.2 = ((bf16[32,16,256]{2,1,0:T(8,128)(2,1)}), bf16[32,16,256]{2,1,0:T(8,128)(2,1)S(1)}, u32[]{:S(2)}, u32[]{:S(2)}) async-start(bf16[32,16,256]{2,1,0:T(8,128)(2,1)} %bitcast.29), calls=%async_computation.2 | async-start | bytes 524288 | tf_op jit(solution)/shard_map/all_to_all | solution.py:226
  73.6 12.4 %copy-start.6 = (s32[32]{0:T(128)S(1)}, s32[32]{0:T(128)}, u32[]{:S(2)}) copy-start(s32[32]{0:T(128)} %param.15) | copy-start | bytes 388
  83.4 19.0 %all-to-all-start.4 = ((f32[32,16,256]{2,1,0:T(8,128)}), f32[32,16,256]{2,1,0:T(8,128)S(1)}, u32[]{:S(2)}, u32[]{:S(2)}) async-start(f32[32,16,256]{2,1,0:T(8,128)} %bitcast.9), calls=%async_computation.4 | async-start | bytes 1048576 | tf_op jit(solution)/shard_map/all_to_all | solution.py:239
  86.1 19.6 %copy-start.5 = (bf16[8,32,256]{2,1,0:T(8,128)(2,1)S(1)}, bf16[8,32,256]{2,1,0:T(8,128)(2,1)}, u32[]{:S(2)}) copy-start(bf16[8,32,256]{2,1,0:T(8,128)(2,1)} %all_to_all.30) | copy-start | bytes 393220
  103.1 13.0 %all-to-all-start.5 = ((bf16[32,16,256]{2,1,0:T(8,128)(2,1)}), bf16[32,16,256]{2,1,0:T(8,128)(2,1)S(1)}, u32[]{:S(2)}, u32[]{:S(2)}) async-start(bf16[32,16,256]{2,1,0:T(8,128)(2,1)} %broadcast_in_dim.35), calls=%async_computation.5 | async-start | bytes 524288 | tf_op jit(solution)/shard_map/all_to_all | solution.py:243
  105.7 1.6 %copy-start.3 = (f32[2048,256]{1,0:T(8,128)S(1)}, f32[2048,256]{1,0:T(8,128)}, u32[]{:S(2)}) copy-start(f32[2048,256]{1,0:T(8,128)} %convolution_add_fusion.1) | copy-start | bytes 6291460

commit v12 on v11

--- a/solution.py
+++ b/solution.py
@@ -70,7 +70,7 @@
             dagg_ref[blk, :] = dagg.astype(dagg_ref.dtype)
             return carry
 
-        lax.fori_loop(0, acc_ref.shape[0] // edge, rows_block, 0)
+        lax.fori_loop(0, acc_ref.shape[0] // edge, rows_block, 0, unroll=True)
 
 def tile_aggregate(tile_src, tile_dst, tile_count, tile_val, source, fws, w_neigh, cotangent, tb=16, batch=1):
     tiles, edge, _ = tile_val.shape

time: 118 us -> 115 us (0.975)
  blocking collectives: 19.1 us -> 16 us
    all_to_all x1, blocking collectives: 19.1 us -> 16 us  [body(): lax.all_to_all(hub_part.reshape(group, hubs_dev, width), 'dev', split_axi...]
    pallas_call x1, Pallas kernels: 13.1 us -> 11.4 us  [tile_aggregate(): pl.pallas_call(kernel, out_shape=(row_out, row_out, row_out, row_out), gr...]
    pallas_call x1, Pallas kernels: 6.43 us -> 7.98 us  [tile_backward(): pl.pallas_call(kernel, out_shape=(jax.ShapeDtypeStruct((rows, width), jnp...]
  transfers between devices with their start and end apart: 5 -> 5, of which waited for: 5 -> 5; matrix products, arithmetic and copies ran while one was open for 12% -> 13% of each run, Pallas kernels for 0% -> 0%
where the time goes in v12:
time: 115 us; the launch traced here: 114 us
  waiting for transfers between devices  38.1 us (33%)
  Pallas kernels  19.3 us (17%)
  starting transfers between devices  18.4 us (16%)
  blocking collectives  16 us (14%)
  matrix products  13.3 us (12%)
  local copies, waits for them, and re-layouts  4.31 us (4%)
  other arithmetic  2.91 us (3%)
  between operations  1.44 us (1%)
    all_to_all x1, blocking collectives, body(): lax.all_to_all(hub_part.reshape(group, hubs_dev, width), 'dev', split_axi...  16 us
    all_to_all x1, waiting for transfers between devices, body(): lax.all_to_all(parts, ('dom', 'dev'), split_axis=0, concat_axis=0, tiled=...  12.8 us
    pallas_call x1, Pallas kernels, tile_aggregate(): pl.pallas_call(kernel, out_shape=(row_out, row_out, row_out, row_out), gr...  11.4 us
    all_to_all x1, waiting for transfers between devices, body(): lax.all_to_all(returning, ('dom', 'dev'), split_axis=0, concat_axis=0, ti...  8.52 us
    pallas_call x1, Pallas kernels, tile_backward(): pl.pallas_call(kernel, out_shape=(jax.ShapeDtypeStruct((rows, width), jnp...  7.98 us
    all_to_all x1, waiting for transfers between devices, body(): lax.all_to_all(outgoing, ('dom', 'dev'), split_axis=0, concat_axis=0, til...  7.94 us
    all_to_all x1, waiting for transfers between devices, body(): lax.all_to_all(spread_piece, ('dom', 'dev'), split_axis=0, concat_axis=0,...  6.51 us
    all_to_all x1, starting transfers between devices, body(): lax.all_to_all(hub_out, 'dev', split_axis=0, concat_axis=0, tiled=True)  6.32 us
  transfers between devices with their start and end apart: 5, of which 5 were waited for; matrix products, arithmetic and copies ran while one was open for 13% of the time, Pallas kernels for 0%

profile of v12, /device:TPU:0, one launch (start us, length us, event | category | flops | bytes accessed | tf_op | source)
XLA Modules:
  0.0 113.8 jit_solution(3011507322941848263)
XLA Ops:
  0.6 0.0 copy-start
  0.6 1.6 %convolution_convert_fusion = bf16[32,256]{1,0:T(8,128)(2,1)S(1)} fusion(bf16[2048,256]{1,0:T(8,128)(2,1)} %param.11, s32[32]{0:T(128)} %param.15), kind=kOutput, calls=%fused_computation.16 | convolution fusion | flops 33628160 | bytes 1065088 | tf_op jit(solution)/shard_map/dot_general | solution.py:198
  2.2 0.7 broadcast_in_dim.20
  2.9 6.3 %all-to-all-start.1 = ((bf16[8,32,256]{2,1,0:T(8,128)(2,1)}), bf16[8,32,256]{2,1,0:T(8,128)(2,1)S(1)}, u32[]{:S(2)}, u32[]{:S(2)}) async-start(bf16[8,32,256]{2,1,0:T(8,128)(2,1)} %broadcast_in_dim.20), calls=%async_computation.1 | async-start | bytes 262144 | tf_op jit(solution)/shard_map/all_to_all | solution.py:200
  9.2 0.7 iota_compare_fusion.3
  10.0 0.1 lt.20
  10.1 0.8 copy.15
  10.8 0.1 eq.22
  10.9 0.0 copy-start.1
  10.9 2.8 %fusion.11 = bf16[512,256]{1,0:T(8,128)(2,1)} fusion(bf16[2048,256]{1,0:T(8,128)(2,1)} %param.11, s32[512]{0:T(512)S(1)} %eq.22, pred[512]{0:T(512)(128)(4,1)S(1)} %lt.20), kind=kOutput, calls=%fused_computation.14 | convolution fusion | flops 540147712 | bytes 1313280 | tf_op jit(solution)/shard_map/dot_general | solution.py:206
  13.7 2.3 %all-to-all-done.1 = bf16[8,32,256]{2,1,0:T(8,128)(2,1)S(1)} async-done(((bf16[8,32,256]{2,1,0:T(8,128)(2,1)}), bf16[8,32,256]{2,1,0:T(8,128)(2,1)S(1)}, u32[]{:S(2)}, u32[]{:S(2)}) %all-to-all-start.1) | async-done | bytes 131104 | tf_op jit(solution)/shard_map/all_to_all | solution.py:200
  16.0 3.7 %all-to-all-start = ((bf16[32,16,256]{2,1,0:T(8,128)(2,1)}), bf16[32,16,256]{2,1,0:T(8,128)(2,1)S(1)}, u32[]{:S(2)}, u32[]{:S(2)}) async-start(bf16[32,16,256]{2,1,0:T(8,128)(2,1)} %bitcast.1), calls=%async_computation | async-start | bytes 524288 | tf_op jit(solution)/shard_map/all_to_all | solution.py:208
  20.4 0.0 copy-done
  20.4 0.0 copy-done.1
  20.4 1.8 %fusion.22.fws_ref = f32[2048,256]{1,0:T(8,128)} fusion(bf16[2048,256]{1,0:T(8,128)(2,1)S(1)} %copy-done.1, bf16[256,256]{1,0:T(8,128)(2,1)S(1)} %copy-done), kind=kOutput, calls=%fused_computation.29 | convolution fusion | flops 268435456 | bytes 3276800 | tf_op jit(solution)/shard_map/dot_general | solution.py:212
  22.2 7.9 %all-to-all-done = bf16[32,16,256]{2,1,0:T(8,128)(2,1)S(1)} async-done(((bf16[32,16,256]{2,1,0:T(8,128)(2,1)}), bf16[32,16,256]{2,1,0:T(8,128)(2,1)S(1)}, u32[]{:S(2)}, u32[]{:S(2)}) %all-to-all-start) | async-done | bytes 262176 | tf_op jit(solution)/shard_map/all_to_all | solution.py:208
  30.2 1.2 %pad_maximum_fusion.source_ref = bf16[2816,256]{1,0:T(8,128)(2,1)} fusion(bf16[256,256]{1,0:T(8,128)(2,1)S(1)} %bitcast.27, bf16[512,256]{1,0:T(8,128)(2,1)S(1)} %bitcast.26, bf16[2048,256]{1,0:T(8,128)(2,1)S(1)} %copy-done.1), kind=kLoop, calls=%fused_computation.13 | loop fusion | flops 4325376 | bytes 2883584 | tf_op jit(solution)/shard_map/concatenate | solution.py:209
  31.4 11.4 %shard_map.138 = (bf16[2048,256]{1,0:T(8,128)(2,1)}, bf16[2048,256]{1,0:T(8,128)(2,1)}, bf16[2048,256]{1,0:T(8,128)(2,1)}, bf16[2048,256]{1,0:T(8,128)(2,1)}) custom-call(s32[320]{0:T(512)} %src_ref.3, s32[320]{0:T(512)} %dst_ref.3, s32[1]{0:T(128)S(6)} %copy.16.cnt_ref, bf16[320,128,128]{2,1,0:T(8,128)(2,1)} %val_ref.3, ...), custom_call_target="tpu_custom_call" | custom-call | tf_op jit(solution)/shard_map/pallas_call | solution.py:81
  42.7 0.0 copy-start.2
  42.7 8.0 %shard_map.139 = (f32[2048,256]{1,0:T(8,128)}, bf16[512,256]{1,0:T(8,128)(2,1)}, bf16[256,256]{1,0:T(8,128)(2,1)}) custom-call(s32[320]{0:T(512)} %src_ref.3, s32[320]{0:T(512)} %dst_ref.3, s32[1]{0:T(128)S(6)} %copy.16.cnt_ref, bf16[320,128,128]{2,1,0:T(8,128)(2,1)} %val_ref.3, bf16[2048,256]{1,0:T(8,128)(2,1)} %get-tuple-element.16.dagg_ref), custom_call_target="tpu_custom_call" | custom-call | tf_op jit(solution)/shard_map/pallas_call | solution.py:153
  50.7 0.0 copy-start.4
  50.7 16.0 %all_to_all.30 = bf16[8,32,256]{2,1,0:T(8,128)(2,1)} all-to-all(bf16[8,32,256]{2,1,0:T(8,128)(2,1)} %bitcast.32), channel_id=1, replica_groups=mesh['dom'=4,'dev'=8] {'dev'}, dimensions={0} | all-to-all | bytes 262144 | tf_op jit(solution)/shard_map/all_to_all | solution.py:230
  66.7 3.1 %all-to-all-start.2 = ((bf16[32,16,256]{2,1,0:T(8,128)(2,1)}), bf16[32,16,256]{2,1,0:T(8,128)(2,1)S(1)}, u32[]{:S(2)}, u32[]{:S(2)}) async-start(bf16[32,16,256]{2,1,0:T(8,128)(2,1)} %bitcast.29), calls=%async_computation.2 | async-start | bytes 524288 | tf_op jit(solution)/shard_map/all_to_all | solution.py:226
  69.8 0.0 copy-done.2
  69.8 0.5 convolution_bitcast_fusion.1
  70.4 0.0 copy-done.4
  70.4 0.0 copy-start.6
  70.4 0.5 fusion.23
  70.9 0.8 pad_maximum_fusion.1
  71.7 8.5 %all-to-all-done.2 = bf16[32,16,256]{2,1,0:T(8,128)(2,1)S(1)} async-done(((bf16[32,16,256]{2,1,0:T(8,128)(2,1)}), bf16[32,16,256]{2,1,0:T(8,128)(2,1)S(1)}, u32[]{:S(2)}, u32[]{:S(2)}) %all-to-all-start.2) | async-done | bytes 262176 | tf_op jit(solution)/shard_map/all_to_all | solution.py:226
  80.2 2.6 %all-to-all-start.4 = ((f32[32,16,256]{2,1,0:T(8,128)}), f32[32,16,256]{2,1,0:T(8,128)S(1)}, u32[]{:S(2)}, u32[]{:S(2)}) async-start(f32[32,16,256]{2,1,0:T(8,128)} %bitcast.9), calls=%async_computation.4 | async-start | bytes 1048576 | tf_op jit(solution)/shard_map/all_to_all | solution.py:239
  82.8 0.0 copy-done.6
  82.8 0.1 fusion.17
  82.9 0.0 copy-start.5
  82.9 3.4 %convolution_add_fusion.1 = f32[2048,256]{1,0:T(8,128)} fusion(f32[2048,256]{1,0:T(8,128)} %get-tuple-element.17, bf16[2048,256]{1,0:T(8,128)(2,1)S(1)} %copy-done.2, bf16[256,256]{1,0:T(8,128)(2,1)S(1)} %copy-done), kind=kOutput, calls=%fused_computation.5 | convolution fusion | flops 268959744 | bytes 5373952 | tf_op jit(solution)/shard_map/dot_general | solution.py:248
  86.3 12.8 %all-to-all-done.4 = f32[32,16,256]{2,1,0:T(8,128)S(1)} async-done(((f32[32,16,256]{2,1,0:T(8,128)}), f32[32,16,256]{2,1,0:T(8,128)S(1)}, u32[]{:S(2)}, u32[]{:S(2)}) %all-to-all-start.4) | async-done | bytes 524320 | tf_op jit(solution)/shard_map/all_to_all | solution.py:239
  99.2 0.7 broadcast_in_dim.35
  99.9 2.6 %all-to-all-start.5 = ((bf16[32,16,256]{2,1,0:T(8,128)(2,1)}), bf16[32,16,256]{2,1,0:T(8,128)(2,1)S(1)}, u32[]{:S(2)}, u32[]{:S(2)}) async-start(bf16[32,16,256]{2,1,0:T(8,128)(2,1)} %broadcast_in_dim.35), calls=%async_computation.5 | async-start | bytes 524288 | tf_op jit(solution)/shard_map/all_to_all | solution.py:243
  102.5 0.0 copy-done.5
  102.5 0.0 copy-start.3
  102.6 0.5 convolution_bitcast_fusion
  103.0 1.1 copy-done.3
  104.1 2.3 %fusion.2 = bf16[2048,256]{1,0:T(8,128)(2,1)} fusion(f32[2048,256]{1,0:T(8,128)S(1)} %convolution_bitcast_fusion, f32[2048,256]{1,0:T(8,128)S(1)} %copy-done.3, bf16[512,256]{1,0:T(8,128)(2,1)S(1)} %bitcast.28, s32[512]{0:T(512)S(1)} %eq.22, pred[512]{0:T(512)(128)(4,1)S(1)} %lt.20), kind=kOutput, calls=%fused_computation.6 | convolution fusion | flops 541589504 | bytes 5507584 | tf_op jit(solution)/shard_map/dot_general | solution.py:249
  106.4 6.5 %all-to-all-done.5 = bf16[32,16,256]{2,1,0:T(8,128)(2,1)S(1)} async-done(((bf16[32,16,256]{2,1,0:T(8,128)(2,1)}), bf16[32,16,256]{2,1,0:T(8,128)(2,1)S(1)}, u32[]{:S(2)}, u32[]{:S(2)}) %all-to-all-start.5) | async-done | bytes 262176 | tf_op jit(solution)/shard_map/all_to_all | solution.py:243
  112.9 0.8 fusion.21
  (2 shorter events, 0.1 us)
Async XLA Ops:
  0.6 19.8 %copy-start = (bf16[256,256]{1,0:T(8,128)(2,1)S(1)}, bf16[256,256]{1,0:T(8,128)(2,1)}, u32[]{:S(2)}) copy-start(bf16[256,256]{1,0:T(8,128)(2,1)} %param.12) | copy-start | bytes 393220
  2.9 13.1 %all-to-all-start.1 = ((bf16[8,32,256]{2,1,0:T(8,128)(2,1)}), bf16[8,32,256]{2,1,0:T(8,128)(2,1)S(1)}, u32[]{:S(2)}, u32[]{:S(2)}) async-start(bf16[8,32,256]{2,1,0:T(8,128)(2,1)} %broadcast_in_dim.20), calls=%async_computation.1 | async-start | bytes 262144 | tf_op jit(solution)/shard_map/all_to_all | solution.py:200
  10.9 9.5 %copy-start.1 = (bf16[2048,256]{1,0:T(8,128)(2,1)S(1)}, bf16[2048,256]{1,0:T(8,128)(2,1)}, u32[]{:S(2)}) copy-start(bf16[2048,256]{1,0:T(8,128)(2,1)} %param.11) | copy-start | bytes 3145732
  16.0 14.1 %all-to-all-start = ((bf16[32,16,256]{2,1,0:T(8,128)(2,1)}), bf16[32,16,256]{2,1,0:T(8,128)(2,1)S(1)}, u32[]{:S(2)}, u32[]{:S(2)}) async-start(bf16[32,16,256]{2,1,0:T(8,128)(2,1)} %bitcast.1), calls=%async_computation | async-start | bytes 524288 | tf_op jit(solution)/shard_map/all_to_all | solution.py:208
  42.7 27.1 %copy-start.2 = (bf16[2048,256]{1,0:T(8,128)(2,1)S(1)}, bf16[2048,256]{1,0:T(8,128)(2,1)}, u32[]{:S(2)}) copy-start(bf16[2048,256]{1,0:T(8,128)(2,1)} %get-tuple-element.15) | copy-start | bytes 3145732
  50.7 19.6 %copy-start.4 = (bf16[2048,256]{1,0:T(8,128)(2,1)S(1)}, bf16[2048,256]{1,0:T(8,128)(2,1)}, u32[]{:S(2)}) copy-start(bf16[2048,256]{1,0:T(8,128)(2,1)} %get-tuple-element.18) | copy-start | bytes 3145732
  66.7 13.5 %all-to-all-start.2 = ((bf16[32,16,256]{2,1,0:T(8,128)(2,1)}), bf16[32,16,256]{2,1,0:T(8,128)(2,1)S(1)}, u32[]{:S(2)}, u32[]{:S(2)}) async-start(bf16[32,16,256]{2,1,0:T(8,128)(2,1)} %bitcast.29), calls=%async_computation.2 | async-start | bytes 524288 | tf_op jit(solution)/shard_map/all_to_all | solution.py:226
  70.4 12.4 %copy-start.6 = (s32[32]{0:T(128)S(1)}, s32[32]{0:T(128)}, u32[]{:S(2)}) copy-start(s32[32]{0:T(128)} %param.15) | copy-start | bytes 388
  80.2 19.0 %all-to-all-start.4 = ((f32[32,16,256]{2,1,0:T(8,128)}), f32[32,16,256]{2,1,0:T(8,128)S(1)}, u32[]{:S(2)}, u32[]{:S(2)}) async-start(f32[32,16,256]{2,1,0:T(8,128)} %bitcast.9), calls=%async_computation.4 | async-start | bytes 1048576 | tf_op jit(solution)/shard_map/all_to_all | solution.py:239
  82.9 19.6 %copy-start.5 = (bf16[8,32,256]{2,1,0:T(8,128)(2,1)S(1)}, bf16[8,32,256]{2,1,0:T(8,128)(2,1)}, u32[]{:S(2)}) copy-start(bf16[8,32,256]{2,1,0:T(8,128)(2,1)} %all_to_all.30) | copy-start | bytes 393220
  99.9 13.0 %all-to-all-start.5 = ((bf16[32,16,256]{2,1,0:T(8,128)(2,1)}), bf16[32,16,256]{2,1,0:T(8,128)(2,1)S(1)}, u32[]{:S(2)}, u32[]{:S(2)}) async-start(bf16[32,16,256]{2,1,0:T(8,128)(2,1)} %broadcast_in_dim.35), calls=%async_computation.5 | async-start | bytes 524288 | tf_op jit(solution)/shard_map/all_to_all | solution.py:243
  102.5 1.6 %copy-start.3 = (f32[2048,256]{1,0:T(8,128)S(1)}, f32[2048,256]{1,0:T(8,128)}, u32[]{:S(2)}) copy-start(f32[2048,256]{1,0:T(8,128)} %convolution_add_fusion.1) | copy-start | bytes 6291460

commit v13 on v9

--- a/solution.py
+++ b/solution.py
@@ -21,13 +21,18 @@
         return (jnp.minimum(i, last), 0, 0)
     return index_map
 
-def _agg_kernel(src_ref, dst_ref, cnt_ref, val_ref, source_ref, out_ref, acc_ref, *, tb, edge, batch):
+def _agg_kernel(src_ref, dst_ref, cnt_ref, val_ref, feats_ref, inc_ref, hub_ref, out_ref, acc_ref, source_ref, *, tb, edge, batch):
     i = pl.program_id(0)
     last_src = source_ref.shape[0] // edge - 1
     last_dst = acc_ref.shape[0] // edge - 1
     @pl.when(i == 0)
     def _():
         acc_ref[...] = jnp.zeros_like(acc_ref)
+        own = feats_ref.shape[0]
+        mid = own + inc_ref.shape[0]
+        source_ref[:own, :] = feats_ref[...]
+        source_ref[own:mid, :] = inc_ref[...]
+        source_ref[mid:, :] = hub_ref[...]
     count = cnt_ref[0]
     def one(t, k):
         s = jnp.clip(src_ref[t], 0, last_src)
@@ -57,21 +62,27 @@
     def _():
         out_ref[...] = acc_ref[...].astype(out_ref.dtype)
 
-def tile_aggregate(tile_src, tile_dst, tile_count, tile_val, source, rows, tb=16, batch=1):
+def tile_aggregate(tile_src, tile_dst, tile_count, tile_val, feats, incoming, hub_table, tb=16, batch=1):
     tiles, edge, _ = tile_val.shape
-    width = source.shape[1]
+    rows, width = feats.shape
+    src_rows = rows + incoming.shape[0] + hub_table.shape[0]
     kernel = functools.partial(_agg_kernel, tb=tb, edge=edge, batch=batch)
+    whole = lambda i, s, d, c: (0, 0)
     return pl.pallas_call(
         kernel,
         out_shape=jax.ShapeDtypeStruct((rows, width), jnp.bfloat16),
         grid_spec=pltpu.PrefetchScalarGridSpec(
             num_scalar_prefetch=3, grid=(tiles // tb,),
             in_specs=[pl.BlockSpec((tb, edge, edge), _val_map(tb)),
-                      pl.BlockSpec(source.shape, lambda i, s, d, c: (0, 0))],
-            out_specs=pl.BlockSpec((rows, width), lambda i, s, d, c: (0, 0)),
-            scratch_shapes=[pltpu.VMEM((rows, width), jnp.float32)]),
+                      pl.BlockSpec(feats.shape, whole),
+                      pl.BlockSpec(incoming.shape, whole),
+                      pl.BlockSpec(hub_table.shape, whole)],
+            out_specs=pl.BlockSpec((rows, width), whole),
+            scratch_shapes=[pltpu.VMEM((rows, width), jnp.float32),
+                            pltpu.VMEM((src_rows, width), feats.dtype)]),
         compiler_params=pltpu.CompilerParams(dimension_semantics=("arbitrary",)),
-    )(tile_src, tile_dst, tile_count, tile_val, source)
+    )(tile_src, tile_dst, tile_count, tile_val, feats, incoming, hub_table)
+
 
 def _back_kernel(src_ref, dst_ref, cnt_ref, val_ref, dagg_ref, own_ref, ret_ref, hub_ref, acc_ref, *, tb, edge, batch):
     i = pl.program_id(0)
@@ -185,10 +196,11 @@
     outgoing = jnp.dot(send_pick, feats, preferred_element_type=jnp.float32).astype(jnp.bfloat16)
     outgoing = outgoing.reshape(peers, slots, width)
     incoming = lax.all_to_all(outgoing, ("dom", "dev"), split_axis=0, concat_axis=0, tiled=True)
-    source = jnp.concatenate([feats, incoming.reshape(peers * slots, width), hub_table], axis=0)
+    incoming = incoming.reshape(peers * slots, width)
+    src_rows = rows + incoming.shape[0] + hub_table.shape[0]
 
     tb = _tile_block(tile_val.shape[0])
-    agg = tile_aggregate(tile_src, tile_dst, tile_count, tile_val, source, rows, tb=tb)
+    agg = tile_aggregate(tile_src, tile_dst, tile_count, tile_val, feats, incoming, hub_table, tb=tb)
 
     pre = jnp.dot(feats, w_self, preferred_element_type=jnp.float32) + jnp.dot(
         agg, w_neigh, preferred_element_type=jnp.float32
@@ -206,7 +218,7 @@
         jnp.bfloat16
     )
     own, returning, hub_part = tile_backward(
-        tile_src, tile_dst, tile_count, tile_val, dagg, source.shape[0], peers * slots, tb=tb
+        tile_src, tile_dst, tile_count, tile_val, dagg, src_rows, peers * slots, tb=tb
     )
     returning = returning.reshape(peers, slots, width)
     returned = lax.all_to_all(

time: 116 us -> 116 us (level)
  blocking collectives: 18.9 us -> 15.2 us
  Pallas kernels: 12.4 us -> 15.4 us
  matrix products: 19.8 us -> 18 us
  waiting for transfers between devices: 37.2 us -> 38.5 us
  other arithmetic: 2.91 us -> 1.7 us
    all_to_all x1, blocking collectives: 18.9 us -> 15.2 us  [body(): lax.all_to_all(hub_part.reshape(group, hubs_dev, width), 'dev', split_axi...]
    pallas_call x1, Pallas kernels: 6.43 us -> 7.98 us  [tile_backward(): pl.pallas_call(kernel, out_shape=(jax.ShapeDtypeStruct((rows, width), jnp...]
    pallas_call x1, Pallas kernels: 5.93 us -> 7.38 us  [tile_aggregate(): pl.pallas_call(kernel, out_shape=jax.ShapeDtypeStruct((rows, width), jnp....]
    concatenate x1 -> x0, other arithmetic: 1.21 us -> none  [body(): jnp.concatenate([feats, incoming.reshape(peers * slots, width), hub_table...]
    unnamed x15 -> x21, local copies, waits for them, and re-layouts: 1.9 us -> 2.62 us
  transfers between devices with their start and end apart: 5 -> 5, of which waited for: 5 -> 5; matrix products, arithmetic and copies ran while one was open for 13% -> 12% of each run, Pallas kernels for 0% -> 0%
where the time goes in v13:
time: 116 us; the launch traced here: 115 us
  waiting for transfers between devices  38.5 us (33%)
  starting transfers between devices  19.5 us (17%)
  matrix products  18 us (16%)
  Pallas kernels  15.4 us (13%)
  blocking collectives  15.2 us (13%)
  local copies, waits for them, and re-layouts  5.02 us (4%)
  other arithmetic  1.7 us (1%)
  between operations  1.46 us (1%)
    all_to_all x1, blocking collectives, body(): lax.all_to_all(hub_part.reshape(group, hubs_dev, width), 'dev', split_axi...  15.2 us
    all_to_all x1, waiting for transfers between devices, body(): lax.all_to_all(parts, ('dom', 'dev'), split_axis=0, concat_axis=0, tiled=...  12.8 us
    all_to_all x1, waiting for transfers between devices, body(): lax.all_to_all(returning, ('dom', 'dev'), split_axis=0, concat_axis=0, ti...  8.5 us
    all_to_all x1, waiting for transfers between devices, body(): lax.all_to_all(outgoing, ('dom', 'dev'), split_axis=0, concat_axis=0, til...  8.38 us
    pallas_call x1, Pallas kernels, tile_backward(): pl.pallas_call(kernel, out_shape=(jax.ShapeDtypeStruct((rows, width), jnp...  7.98 us
    pallas_call x1, Pallas kernels, tile_aggregate(): pl.pallas_call(kernel, out_shape=jax.ShapeDtypeStruct((rows, width), jnp....  7.38 us
    all_to_all x1, waiting for transfers between devices, body(): lax.all_to_all(spread_piece, ('dom', 'dev'), split_axis=0, concat_axis=0,...  6.47 us
    all_to_all x1, starting transfers between devices, body(): lax.all_to_all(hub_out, 'dev', split_axis=0, concat_axis=0, tiled=True)  6.32 us
  transfers between devices with their start and end apart: 5, of which 5 were waited for; matrix products, arithmetic and copies ran while one was open for 12% of the time, Pallas kernels for 0%

profile of v13, /device:TPU:0, one launch (start us, length us, event | category | flops | bytes accessed | tf_op | source)
XLA Modules:
  0.0 114.7 jit_solution(5317081912414506269)
XLA Ops:
  0.6 0.0 copy-start
  0.6 1.6 %convolution_convert_fusion.1 = bf16[32,256]{1,0:T(8,128)(2,1)S(1)} fusion(bf16[2048,256]{1,0:T(8,128)(2,1)} %feats_ref.1, s32[32]{0:T(128)} %param.15), kind=kOutput, calls=%fused_computation.20 | convolution fusion | flops 33628160 | bytes 1065088 | tf_op jit(solution)/shard_map/dot_general | solution.py:188
  2.2 0.7 broadcast_in_dim.20
  2.9 6.3 %all-to-all-start.1 = ((bf16[8,32,256]{2,1,0:T(8,128)(2,1)}), bf16[8,32,256]{2,1,0:T(8,128)(2,1)S(1)}, u32[]{:S(2)}, u32[]{:S(2)}) async-start(bf16[8,32,256]{2,1,0:T(8,128)(2,1)} %broadcast_in_dim.20), calls=%async_computation.1 | async-start | bytes 262144 | tf_op jit(solution)/shard_map/all_to_all | solution.py:190
  9.2 0.7 iota_compare_fusion.3
  10.0 0.1 lt.20
  10.1 0.8 copy.15
  10.8 0.1 eq.22
  10.9 0.0 copy-start.1
  10.9 2.8 %fusion.11 = bf16[512,256]{1,0:T(8,128)(2,1)} fusion(bf16[2048,256]{1,0:T(8,128)(2,1)} %feats_ref.1, s32[512]{0:T(512)S(1)} %eq.22, pred[512]{0:T(512)(128)(4,1)S(1)} %lt.20), kind=kOutput, calls=%fused_computation.18 | convolution fusion | flops 540147712 | bytes 1313280 | tf_op jit(solution)/shard_map/dot_general | solution.py:196
  13.7 2.3 %all-to-all-done.1 = bf16[8,32,256]{2,1,0:T(8,128)(2,1)S(1)} async-done(((bf16[8,32,256]{2,1,0:T(8,128)(2,1)}), bf16[8,32,256]{2,1,0:T(8,128)(2,1)S(1)}, u32[]{:S(2)}, u32[]{:S(2)}) %all-to-all-start.1) | async-done | bytes 131104 | tf_op jit(solution)/shard_map/all_to_all | solution.py:190
  16.0 3.7 %all-to-all-start = ((bf16[32,16,256]{2,1,0:T(8,128)(2,1)}), bf16[32,16,256]{2,1,0:T(8,128)(2,1)S(1)}, u32[]{:S(2)}, u32[]{:S(2)}) async-start(bf16[32,16,256]{2,1,0:T(8,128)(2,1)} %bitcast.1), calls=%async_computation | async-start | bytes 524288 | tf_op jit(solution)/shard_map/all_to_all | solution.py:198
  19.8 0.0 copy-done.6
  20.4 0.0 copy-done.1
  20.4 1.3 %fusion.22 = f32[2048,256]{1,0:T(8,128)S(1)} fusion(bf16[2048,256]{1,0:T(8,128)(2,1)S(1)} %copy-done.1, bf16[256,256]{1,0:T(8,128)(2,1)} %param.12), kind=kOutput, calls=%fused_computation.33 | convolution fusion | flops 268435456 | bytes 3276800 | tf_op jit(solution)/shard_map/dot_general | solution.py:205
  21.8 8.4 %all-to-all-done = bf16[32,16,256]{2,1,0:T(8,128)(2,1)S(1)} async-done(((bf16[32,16,256]{2,1,0:T(8,128)(2,1)}), bf16[32,16,256]{2,1,0:T(8,128)(2,1)S(1)}, u32[]{:S(2)}, u32[]{:S(2)}) %all-to-all-start) | async-done | bytes 262176 | tf_op jit(solution)/shard_map/all_to_all | solution.py:198
  30.2 0.7 copy-done.5
  30.9 7.4 %shard_map.138 = bf16[2048,256]{1,0:T(8,128)(2,1)} custom-call(s32[320]{0:T(512)} %src_ref.3, s32[320]{0:T(512)} %dst_ref.3, s32[1]{0:T(128)S(6)} %copy.16.cnt_ref, bf16[320,128,128]{2,1,0:T(8,128)(2,1)} %val_ref.3, bf16[2048,256]{1,0:T(8,128)(2,1)} %feats_ref.1, bf16[512,256]{1,0:T(8,128)(2,1)} %bitcast.30, bf16[256,256]{1,0:T(8,128)(2,1)} %bitcast.31), custom_call_target="tpu_custom_call" | custom-call | tf_op jit(solution)/shard_map/pallas_call | solution.py:71
  38.2 0.0 copy-done
  38.2 3.7 %multiply_convert_fusion = (bf16[2048,256]{1,0:T(8,128)(2,1)S(1)}, bf16[2048,256]{1,0:T(8,128)(2,1)}) fusion(bf16[2048,256]{1,0:T(8,128)(2,1)} %param.14, f32[2048,256]{1,0:T(8,128)S(1)} %fusion.22, bf16[2048,256]{1,0:T(8,128)(2,1)} %shard_map.138, bf16[256,256]{1,0:T(8,128)(2,1)S(1)} %copy-done), kind=kOutput, calls=%fused_computation.11 | convolution fusion | flops 275251200 | bytes 6422528 | tf_op jit(solution)/shard_map/dot_general | solution.py:205
  42.0 1.4 %convolution_convert_fusion.dagg_ref = bf16[2048,256]{1,0:T(8,128)(2,1)} fusion(bf16[2048,256]{1,0:T(8,128)(2,1)S(1)} %get-tuple-element.16, bf16[256,256]{1,0:T(8,128)(2,1)S(1)} %copy-done), kind=kOutput, calls=%fused_computation.8 | convolution fusion | flops 268959744 | bytes 2228224 | tf_op jit(solution)/shard_map/dot_general | solution.py:217
  43.4 8.0 %shard_map.139 = (f32[2048,256]{1,0:T(8,128)}, bf16[512,256]{1,0:T(8,128)(2,1)}, bf16[256,256]{1,0:T(8,128)(2,1)}) custom-call(s32[320]{0:T(512)} %src_ref.3, s32[320]{0:T(512)} %dst_ref.3, s32[1]{0:T(128)S(6)} %copy.16.cnt_ref, bf16[320,128,128]{2,1,0:T(8,128)(2,1)} %val_ref.3, bf16[2048,256]{1,0:T(8,128)(2,1)} %convolution_convert_fusion.dagg_ref), custom_call_target="tpu_custom_call" | custom-call | tf_op jit(solution)/shard_map/pallas_call | solution.py:143
  51.4 15.2 %all_to_all.30 = bf16[8,32,256]{2,1,0:T(8,128)(2,1)} all-to-all(bf16[8,32,256]{2,1,0:T(8,128)(2,1)} %bitcast.36), channel_id=1, replica_groups=mesh['dom'=4,'dev'=8] {'dev'}, dimensions={0} | all-to-all | bytes 262144 | tf_op jit(solution)/shard_map/all_to_all | solution.py:228
  66.5 4.2 %all-to-all-start.2 = ((bf16[32,16,256]{2,1,0:T(8,128)(2,1)}), bf16[32,16,256]{2,1,0:T(8,128)(2,1)S(1)}, u32[]{:S(2)}, u32[]{:S(2)}) async-start(bf16[32,16,256]{2,1,0:T(8,128)(2,1)} %bitcast.33), calls=%async_computation.2 | async-start | bytes 524288 | tf_op jit(solution)/shard_map/all_to_all | solution.py:224
  70.8 0.0 copy-done.3
  70.8 0.5 fusion.23
  71.2 0.0 copy-done.2
  71.3 0.0 copy-start.9
  71.3 0.0 copy-start.7
  71.3 0.5 convolution_bitcast_fusion.1
  71.8 0.8 pad_maximum_fusion
  72.6 8.5 %all-to-all-done.2 = bf16[32,16,256]{2,1,0:T(8,128)(2,1)S(1)} async-done(((bf16[32,16,256]{2,1,0:T(8,128)(2,1)}), bf16[32,16,256]{2,1,0:T(8,128)(2,1)S(1)}, u32[]{:S(2)}, u32[]{:S(2)}) %all-to-all-start.2) | async-done | bytes 262176 | tf_op jit(solution)/shard_map/all_to_all | solution.py:224
  81.1 2.6 %all-to-all-start.4 = ((f32[32,16,256]{2,1,0:T(8,128)}), f32[32,16,256]{2,1,0:T(8,128)S(1)}, u32[]{:S(2)}, u32[]{:S(2)}) async-start(f32[32,16,256]{2,1,0:T(8,128)} %bitcast.9), calls=%async_computation.4 | async-start | bytes 1048576 | tf_op jit(solution)/shard_map/all_to_all | solution.py:237
  83.8 0.0 copy-done.9
  83.8 0.1 fusion.17
  83.9 0.0 copy-done.7
  83.9 0.0 copy-start.8
  83.9 3.4 %convolution_add_fusion.1 = f32[2048,256]{1,0:T(8,128)} fusion(f32[2048,256]{1,0:T(8,128)} %get-tuple-element.10, bf16[2048,256]{1,0:T(8,128)(2,1)S(1)} %get-tuple-element.16, bf16[256,256]{1,0:T(8,128)(2,1)S(1)} %copy-done.7), kind=kOutput, calls=%fused_computation.5 | convolution fusion | flops 268959744 | bytes 5373952 | tf_op jit(solution)/shard_map/dot_general | solution.py:246
  87.3 12.8 %all-to-all-done.4 = f32[32,16,256]{2,1,0:T(8,128)S(1)} async-done(((f32[32,16,256]{2,1,0:T(8,128)}), f32[32,16,256]{2,1,0:T(8,128)S(1)}, u32[]{:S(2)}, u32[]{:S(2)}) %all-to-all-start.4) | async-done | bytes 524320 | tf_op jit(solution)/shard_map/all_to_all | solution.py:237
  100.2 0.7 broadcast_in_dim.35
  100.9 2.6 %all-to-all-start.5 = ((bf16[32,16,256]{2,1,0:T(8,128)(2,1)}), bf16[32,16,256]{2,1,0:T(8,128)(2,1)S(1)}, u32[]{:S(2)}, u32[]{:S(2)}) async-start(bf16[32,16,256]{2,1,0:T(8,128)(2,1)} %broadcast_in_dim.35), calls=%async_computation.5 | async-start | bytes 524288 | tf_op jit(solution)/shard_map/all_to_all | solution.py:241
  103.5 0.0 copy-done.8
  103.5 0.0 copy-start.4
  103.5 0.5 convolution_bitcast_fusion
  104.0 1.1 copy-done.4
  105.1 2.3 %fusion.2 = bf16[2048,256]{1,0:T(8,128)(2,1)} fusion(f32[2048,256]{1,0:T(8,128)S(1)} %convolution_bitcast_fusion, f32[2048,256]{1,0:T(8,128)S(1)} %copy-done.4, bf16[512,256]{1,0:T(8,128)(2,1)S(1)} %bitcast.32, s32[512]{0:T(512)S(1)} %eq.22, pred[512]{0:T(512)(128)(4,1)S(1)} %lt.20), kind=kOutput, calls=%fused_computation.7 | convolution fusion | flops 541589504 | bytes 5507584 | tf_op jit(solution)/shard_map/dot_general | solution.py:247
  107.4 6.5 %all-to-all-done.5 = bf16[32,16,256]{2,1,0:T(8,128)(2,1)S(1)} async-done(((bf16[32,16,256]{2,1,0:T(8,128)(2,1)}), bf16[32,16,256]{2,1,0:T(8,128)(2,1)S(1)}, u32[]{:S(2)}, u32[]{:S(2)}) %all-to-all-start.5) | async-done | bytes 262176 | tf_op jit(solution)/shard_map/all_to_all | solution.py:241
  113.9 0.8 fusion.21
  (6 shorter events, 0.1 us)
Async XLA Ops:
  0.6 37.6 %copy-start = (bf16[256,256]{1,0:T(8,128)(2,1)S(1)}, bf16[256,256]{1,0:T(8,128)(2,1)}, u32[]{:S(2)}) copy-start(bf16[256,256]{1,0:T(8,128)(2,1)} %param.13) | copy-start | bytes 393220
  2.9 13.1 %all-to-all-start.1 = ((bf16[8,32,256]{2,1,0:T(8,128)(2,1)}), bf16[8,32,256]{2,1,0:T(8,128)(2,1)S(1)}, u32[]{:S(2)}, u32[]{:S(2)}) async-start(bf16[8,32,256]{2,1,0:T(8,128)(2,1)} %broadcast_in_dim.20), calls=%async_computation.1 | async-start | bytes 262144 | tf_op jit(solution)/shard_map/all_to_all | solution.py:190
  10.9 9.5 %copy-start.1 = (bf16[2048,256]{1,0:T(8,128)(2,1)S(1)}, bf16[2048,256]{1,0:T(8,128)(2,1)}, u32[]{:S(2)}) copy-start(bf16[2048,256]{1,0:T(8,128)(2,1)} %feats_ref.1) | copy-start | bytes 3145732
  16.0 3.8 %copy-start.6 = (bf16[8,32,256]{2,1,0:T(8,128)(2,1)}, bf16[8,32,256]{2,1,0:T(8,128)(2,1)S(1)}, u32[]{:S(2)}) copy-start(bf16[8,32,256]{2,1,0:T(8,128)(2,1)S(1)} %all-to-all-done.1) | copy-start | bytes 393220
  16.0 14.1 %all-to-all-start = ((bf16[32,16,256]{2,1,0:T(8,128)(2,1)}), bf16[32,16,256]{2,1,0:T(8,128)(2,1)S(1)}, u32[]{:S(2)}, u32[]{:S(2)}) async-start(bf16[32,16,256]{2,1,0:T(8,128)(2,1)} %bitcast.1), calls=%async_computation | async-start | bytes 524288 | tf_op jit(solution)/shard_map/all_to_all | solution.py:198
  30.2 0.7 copy-start.5
  43.4 27.4 %copy-start.3 = (bf16[2048,256]{1,0:T(8,128)(2,1)S(1)}, bf16[2048,256]{1,0:T(8,128)(2,1)}, u32[]{:S(2)}) copy-start(bf16[2048,256]{1,0:T(8,128)(2,1)} %shard_map.138) | copy-start | bytes 3145732
  51.4 19.9 %copy-start.2 = (bf16[2048,256]{1,0:T(8,128)(2,1)S(1)}, bf16[2048,256]{1,0:T(8,128)(2,1)}, u32[]{:S(2)}) copy-start(bf16[2048,256]{1,0:T(8,128)(2,1)} %feats_ref.1) | copy-start | bytes 3145732
  66.5 14.6 %all-to-all-start.2 = ((bf16[32,16,256]{2,1,0:T(8,128)(2,1)}), bf16[32,16,256]{2,1,0:T(8,128)(2,1)S(1)}, u32[]{:S(2)}, u32[]{:S(2)}) async-start(bf16[32,16,256]{2,1,0:T(8,128)(2,1)} %bitcast.33), calls=%async_computation.2 | async-start | bytes 524288 | tf_op jit(solution)/shard_map/all_to_all | solution.py:224
  71.3 12.5 %copy-start.9 = (s32[32]{0:T(128)S(1)}, s32[32]{0:T(128)}, u32[]{:S(2)}) copy-start(s32[32]{0:T(128)} %param.15) | copy-start | bytes 388
  71.3 12.6 %copy-start.7 = (bf16[256,256]{1,0:T(8,128)(2,1)S(1)}, bf16[256,256]{1,0:T(8,128)(2,1)}, u32[]{:S(2)}) copy-start(bf16[256,256]{1,0:T(8,128)(2,1)} %param.12) | copy-start | bytes 393220
  81.1 19.0 %all-to-all-start.4 = ((f32[32,16,256]{2,1,0:T(8,128)}), f32[32,16,256]{2,1,0:T(8,128)S(1)}, u32[]{:S(2)}, u32[]{:S(2)}) async-start(f32[32,16,256]{2,1,0:T(8,128)} %bitcast.9), calls=%async_computation.4 | async-start | bytes 1048576 | tf_op jit(solution)/shard_map/all_to_all | solution.py:237
  83.9 19.6 %copy-start.8 = (bf16[8,32,256]{2,1,0:T(8,128)(2,1)S(1)}, bf16[8,32,256]{2,1,0:T(8,128)(2,1)}, u32[]{:S(2)}) copy-start(bf16[8,32,256]{2,1,0:T(8,128)(2,1)} %all_to_all.30) | copy-start | bytes 393220
  100.9 13.0 %all-to-all-start.5 = ((bf16[32,16,256]{2,1,0:T(8,128)(2,1)}), bf16[32,16,256]{2,1,0:T(8,128)(2,1)S(1)}, u32[]{:S(2)}, u32[]{:S(2)}) async-start(bf16[32,16,256]{2,1,0:T(8,128)(2,1)} %broadcast_in_dim.35), calls=%async_computation.5 | async-start | bytes 524288 | tf_op jit(solution)/shard_map/all_to_all | solution.py:241
  103.5 1.6 %copy-start.4 = (f32[2048,256]{1,0:T(8,128)S(1)}, f32[2048,256]{1,0:T(8,128)}, u32[]{:S(2)}) copy-start(f32[2048,256]{1,0:T(8,128)} %convolution_add_fusion.1) | copy-start | bytes 6291460

commit v14 on v13

--- a/solution.py
+++ b/solution.py
@@ -60,7 +60,9 @@
         lax.fori_loop(0, tb, body, 0)
     @pl.when(i == pl.num_programs(0) - 1)
     def _():
-        out_ref[...] = acc_ref[...].astype(out_ref.dtype)
+        width = acc_ref.shape[1]
+        out_ref[:, :width] = source_ref[: acc_ref.shape[0], :]
+        out_ref[:, width:] = acc_ref[...].astype(out_ref.dtype)
 
 def tile_aggregate(tile_src, tile_dst, tile_count, tile_val, feats, incoming, hub_table, tb=16, batch=1):
     tiles, edge, _ = tile_val.shape
@@ -70,14 +72,14 @@
     whole = lambda i, s, d, c: (0, 0)
     return pl.pallas_call(
         kernel,
-        out_shape=jax.ShapeDtypeStruct((rows, width), jnp.bfloat16),
+        out_shape=jax.ShapeDtypeStruct((rows, 2 * width), jnp.bfloat16),
         grid_spec=pltpu.PrefetchScalarGridSpec(
             num_scalar_prefetch=3, grid=(tiles // tb,),
             in_specs=[pl.BlockSpec((tb, edge, edge), _val_map(tb)),
                       pl.BlockSpec(feats.shape, whole),
                       pl.BlockSpec(incoming.shape, whole),
                       pl.BlockSpec(hub_table.shape, whole)],
-            out_specs=pl.BlockSpec((rows, width), whole),
+            out_specs=pl.BlockSpec((rows, 2 * width), whole),
             scratch_shapes=[pltpu.VMEM((rows, width), jnp.float32),
                             pltpu.VMEM((src_rows, width), feats.dtype)]),
         compiler_params=pltpu.CompilerParams(dimension_semantics=("arbitrary",)),
@@ -200,18 +202,16 @@
     src_rows = rows + incoming.shape[0] + hub_table.shape[0]
 
     tb = _tile_block(tile_val.shape[0])
-    agg = tile_aggregate(tile_src, tile_dst, tile_count, tile_val, feats, incoming, hub_table, tb=tb)
-
-    pre = jnp.dot(feats, w_self, preferred_element_type=jnp.float32) + jnp.dot(
-        agg, w_neigh, preferred_element_type=jnp.float32
-    )
+    feats_agg = tile_aggregate(tile_src, tile_dst, tile_count, tile_val, feats, incoming, hub_table, tb=tb)
+
+    w_both = jnp.concatenate([w_self, w_neigh], axis=0)
+    pre = jnp.dot(feats_agg, w_both, preferred_element_type=jnp.float32)
     sig = jax.nn.sigmoid(pre)
     out = (pre * sig).astype(jnp.bfloat16)
     dpre = (cotangent.astype(jnp.float32) * sig * (1.0 + pre * (1.0 - sig))).astype(jnp.bfloat16)
 
     contract_rows = (((0,), (0,)), ((), ()))
-    local_ws = lax.dot_general(feats, dpre, contract_rows, preferred_element_type=jnp.float32)
-    local_wn = lax.dot_general(agg, dpre, contract_rows, preferred_element_type=jnp.float32)
+    partial = lax.dot_general(feats_agg, dpre, contract_rows, preferred_element_type=jnp.float32)
 
     contract_cols = (((1,), (1,)), ((), ()))
     dagg = lax.dot_general(dpre, w_neigh, contract_cols, preferred_element_type=jnp.float32).astype(
@@ -224,7 +224,6 @@
     returned = lax.all_to_all(
         returning, ("dom", "dev"), split_axis=0, concat_axis=0, tiled=True
     )
-    partial = jnp.concatenate([local_ws, local_wn], axis=0)
     hub_back = lax.all_to_all(
         hub_part.reshape(group, hubs_dev, width),
         "dev",

time: 116 us -> 116 us (level)
  Pallas kernels: 15.4 us -> 22.4 us
  blocking collectives: 15.2 us -> 10.1 us
  waiting for transfers between devices: 38.5 us -> 40.2 us
  starting transfers between devices: 19.5 us -> 17.8 us
    all_to_all x1, blocking collectives: 15.2 us -> 10.1 us  [body(): lax.all_to_all(hub_part.reshape(group, hubs_dev, width), 'dev', split_axi...]
    pallas_call x1, Pallas kernels: 7.38 us -> 11.2 us  [tile_aggregate(): pl.pallas_call(kernel, out_shape=jax.ShapeDtypeStruct((rows, 2 * width),...]
    pallas_call x1, Pallas kernels: 7.98 us -> 11.2 us  [tile_backward(): pl.pallas_call(kernel, out_shape=(jax.ShapeDtypeStruct((rows, width), jnp...]
    all_to_all x1, starting transfers between devices: 4.2 us -> 2.59 us  [body(): lax.all_to_all(returning, ('dom', 'dev'), split_axis=0, concat_axis=0, ti...]
    all_to_all x1, waiting for transfers between devices: 8.38 us -> 9.74 us  [body(): lax.all_to_all(outgoing, ('dom', 'dev'), split_axis=0, concat_axis=0, til...]
    dot_general x4 -> x2, matrix products: 6.03 us -> 5.37 us  [the longest x1 3.83 us: body(): pre = jnp.dot(feats_agg, w_both, preferred_element_type=jnp.float32)]
    unnamed x21 -> x17, local copies, waits for them, and re-layouts: 2.62 us -> 2.6 us
  transfers between devices with their start and end apart: 5 -> 5, of which waited for: 5 -> 5; matrix products, arithmetic and copies ran while one was open for 12% -> 11% of each run, Pallas kernels for 0% -> 0%
where the time goes in v14:
time: 116 us; the launch traced here: 115 us
  waiting for transfers between devices  40.2 us (35%)
  Pallas kernels  22.4 us (19%)
  starting transfers between devices  17.8 us (15%)
  matrix products  17.3 us (15%)
  blocking collectives  10.1 us (9%)
  local copies, waits for them, and re-layouts  5 us (4%)
  between operations  1.38 us (1%)
    all_to_all x1, waiting for transfers between devices, body(): lax.all_to_all(parts, ('dom', 'dev'), split_axis=0, concat_axis=0, tiled=...  12.8 us
    pallas_call x1, Pallas kernels, tile_backward(): pl.pallas_call(kernel, out_shape=(jax.ShapeDtypeStruct((rows, width), jnp...  11.2 us
    pallas_call x1, Pallas kernels, tile_aggregate(): pl.pallas_call(kernel, out_shape=jax.ShapeDtypeStruct((rows, 2 * width),...  11.2 us
    all_to_all x1, blocking collectives, body(): lax.all_to_all(hub_part.reshape(group, hubs_dev, width), 'dev', split_axi...  10.1 us
    all_to_all x1, waiting for transfers between devices, body(): lax.all_to_all(outgoing, ('dom', 'dev'), split_axis=0, concat_axis=0, til...  9.74 us
    all_to_all x1, waiting for transfers between devices, body(): lax.all_to_all(returning, ('dom', 'dev'), split_axis=0, concat_axis=0, ti...  8.82 us
    all_to_all x1, waiting for transfers between devices, body(): lax.all_to_all(spread_piece, ('dom', 'dev'), split_axis=0, concat_axis=0,...  6.48 us
    all_to_all x1, starting transfers between devices, body(): lax.all_to_all(hub_out, 'dev', split_axis=0, concat_axis=0, tiled=True)  6.32 us
  transfers between devices with their start and end apart: 5, of which 5 were waited for; matrix products, arithmetic and copies ran while one was open for 11% of the time, Pallas kernels for 0%

profile of v14, /device:TPU:0, one launch (start us, length us, event | category | flops | bytes accessed | tf_op | source)
XLA Modules:
  0.0 115.0 jit_solution(13311535123949626965)
XLA Ops:
  0.6 1.6 %convolution_convert_fusion.1 = bf16[32,256]{1,0:T(8,128)(2,1)S(1)} fusion(bf16[2048,256]{1,0:T(8,128)(2,1)} %feats_ref.1, s32[32]{0:T(128)} %param.15), kind=kOutput, calls=%fused_computation.18 | convolution fusion | flops 33628160 | bytes 1065088 | tf_op jit(solution)/shard_map/dot_general | solution.py:190
  2.2 0.7 broadcast_in_dim.20
  2.9 6.3 %all-to-all-start.1 = ((bf16[8,32,256]{2,1,0:T(8,128)(2,1)}), bf16[8,32,256]{2,1,0:T(8,128)(2,1)S(1)}, u32[]{:S(2)}, u32[]{:S(2)}) async-start(bf16[8,32,256]{2,1,0:T(8,128)(2,1)} %broadcast_in_dim.20), calls=%async_computation.1 | async-start | bytes 262144 | tf_op jit(solution)/shard_map/all_to_all | solution.py:192
  9.2 0.7 iota_compare_fusion.3
  9.9 0.1 lt.20
  10.0 0.8 copy.15
  10.8 0.1 eq.22
  10.9 2.7 %fusion.11 = bf16[512,256]{1,0:T(8,128)(2,1)} fusion(bf16[2048,256]{1,0:T(8,128)(2,1)} %feats_ref.1, s32[512]{0:T(512)S(1)} %eq.22, pred[512]{0:T(512)(128)(4,1)S(1)} %lt.20), kind=kOutput, calls=%fused_computation.17 | convolution fusion | flops 540147712 | bytes 1313280 | tf_op jit(solution)/shard_map/dot_general | solution.py:198
  13.6 2.4 %all-to-all-done.1 = bf16[8,32,256]{2,1,0:T(8,128)(2,1)S(1)} async-done(((bf16[8,32,256]{2,1,0:T(8,128)(2,1)}), bf16[8,32,256]{2,1,0:T(8,128)(2,1)S(1)}, u32[]{:S(2)}, u32[]{:S(2)}) %all-to-all-start.1) | async-done | bytes 131104 | tf_op jit(solution)/shard_map/all_to_all | solution.py:192
  16.0 0.0 copy-start.3
  16.0 3.7 %all-to-all-start = ((bf16[32,16,256]{2,1,0:T(8,128)(2,1)}), bf16[32,16,256]{2,1,0:T(8,128)(2,1)S(1)}, u32[]{:S(2)}, u32[]{:S(2)}) async-start(bf16[32,16,256]{2,1,0:T(8,128)(2,1)} %bitcast.1), calls=%async_computation | async-start | bytes 524288 | tf_op jit(solution)/shard_map/all_to_all | solution.py:200
  20.3 9.7 %all-to-all-done = bf16[32,16,256]{2,1,0:T(8,128)(2,1)S(1)} async-done(((bf16[32,16,256]{2,1,0:T(8,128)(2,1)}), bf16[32,16,256]{2,1,0:T(8,128)(2,1)S(1)}, u32[]{:S(2)}, u32[]{:S(2)}) %all-to-all-start) | async-done | bytes 262176 | tf_op jit(solution)/shard_map/all_to_all | solution.py:200
  30.0 0.0 copy-start.2
  30.0 0.0 copy-done.3
  30.0 0.7 copy-done.2
  30.7 0.0 copy-start.4
  30.7 0.0 copy-start.5
  30.7 0.0 copy-start.7
  30.7 11.2 %shard_map.138 = bf16[2048,512]{1,0:T(8,128)(2,1)} custom-call(s32[320]{0:T(512)} %src_ref.3, s32[320]{0:T(512)} %dst_ref.3, s32[1]{0:T(128)S(6)} %copy.16.cnt_ref, bf16[320,128,128]{2,1,0:T(8,128)(2,1)} %val_ref.3, bf16[2048,256]{1,0:T(8,128)(2,1)} %feats_ref.1, bf16[512,256]{1,0:T(8,128)(2,1)} %bitcast.24, bf16[256,256]{1,0:T(8,128)(2,1)} %bitcast.25), custom_call_target="tpu_custom_call" | custom-call | tf_op jit(solution)/shard_map/pallas_call | solution.py:73
  41.9 0.0 copy-done.4
  41.9 0.0 copy-done.5
  41.9 0.0 copy-done.7
  41.9 3.8 %multiply_convert_fusion = (bf16[2048,256]{1,0:T(8,128)(2,1)S(1)}, bf16[2048,256]{1,0:T(8,128)(2,1)}) fusion(bf16[2048,256]{1,0:T(8,128)(2,1)S(1)} %copy-done.7, bf16[2048,512]{1,0:T(8,128)(2,1)} %shard_map.138, bf16[256,256]{1,0:T(8,128)(2,1)S(1)} %copy-done.4, bf16[256,256]{1,0:T(8,128)(2,1)S(1)} %copy-done.5), kind=kOutput, calls=%fused_computation.10 | convolution fusion | flops 543686656 | bytes 5505024 | tf_op jit(solution)/shard_map/dot_general | solution.py:208
  45.7 1.4 %convolution_convert_fusion.dagg_ref = bf16[2048,256]{1,0:T(8,128)(2,1)} fusion(bf16[2048,256]{1,0:T(8,128)(2,1)S(1)} %get-tuple-element.16, bf16[256,256]{1,0:T(8,128)(2,1)S(1)} %copy-done.4), kind=kOutput, calls=%fused_computation.7 | convolution fusion | flops 268959744 | bytes 2228224 | tf_op jit(solution)/shard_map/dot_general | solution.py:217
  47.2 0.0 copy-start
  47.2 11.2 %shard_map.139 = (f32[2048,256]{1,0:T(8,128)}, bf16[512,256]{1,0:T(8,128)(2,1)}, bf16[256,256]{1,0:T(8,128)(2,1)}) custom-call(s32[320]{0:T(512)} %src_ref.3, s32[320]{0:T(512)} %dst_ref.3, s32[1]{0:T(128)S(6)} %copy.16.cnt_ref, bf16[320,128,128]{2,1,0:T(8,128)(2,1)} %val_ref.3, bf16[2048,256]{1,0:T(8,128)(2,1)} %convolution_convert_fusion.dagg_ref), custom_call_target="tpu_custom_call" | custom-call | tf_op jit(solution)/shard_map/pallas_call | solution.py:145
  58.4 10.1 %all_to_all.30 = bf16[8,32,256]{2,1,0:T(8,128)(2,1)S(1)} all-to-all(bf16[8,32,256]{2,1,0:T(8,128)(2,1)} %bitcast.30), channel_id=1, replica_groups=mesh['dom'=4,'dev'=8] {'dev'}, dimensions={0} | all-to-all | bytes 262144 | tf_op jit(solution)/shard_map/all_to_all | solution.py:227
  68.5 2.6 %all-to-all-start.2 = ((bf16[32,16,256]{2,1,0:T(8,128)(2,1)}), bf16[32,16,256]{2,1,0:T(8,128)(2,1)S(1)}, u32[]{:S(2)}, u32[]{:S(2)}) async-start(bf16[32,16,256]{2,1,0:T(8,128)(2,1)} %bitcast.27), calls=%async_computation.2 | async-start | bytes 524288 | tf_op jit(solution)/shard_map/all_to_all | solution.py:224
  71.1 0.0 copy-done
  71.1 0.0 copy-start.6
  71.1 1.5 %fusion.27 = f32[512,256]{1,0:T(8,128)} fusion(bf16[2048,512]{1,0:T(8,128)(2,1)S(1)} %copy-done, bf16[2048,256]{1,0:T(8,128)(2,1)S(1)} %get-tuple-element.16), kind=kOutput, calls=%fused_computation.35 | convolution fusion | flops 536870912 | bytes 3670016 | tf_op jit(solution)/shard_map/dot_general | solution.py:214
  72.6 8.8 %all-to-all-done.2 = bf16[32,16,256]{2,1,0:T(8,128)(2,1)S(1)} async-done(((bf16[32,16,256]{2,1,0:T(8,128)(2,1)}), bf16[32,16,256]{2,1,0:T(8,128)(2,1)S(1)}, u32[]{:S(2)}, u32[]{:S(2)}) %all-to-all-start.2) | async-done | bytes 262176 | tf_op jit(solution)/shard_map/all_to_all | solution.py:224
  81.4 2.6 %all-to-all-start.4 = ((f32[32,16,256]{2,1,0:T(8,128)}), f32[32,16,256]{2,1,0:T(8,128)S(1)}, u32[]{:S(2)}, u32[]{:S(2)}) async-start(f32[32,16,256]{2,1,0:T(8,128)} %bitcast.23), calls=%async_computation.4 | async-start | bytes 1048576 | tf_op jit(solution)/shard_map/all_to_all | solution.py:236
  84.1 0.0 copy-done.6
  84.1 0.1 fusion.21
  84.2 3.5 %convolution_add_fusion.1 = f32[2048,256]{1,0:T(8,128)} fusion(f32[2048,256]{1,0:T(8,128)} %get-tuple-element.10, bf16[2048,256]{1,0:T(8,128)(2,1)S(1)} %get-tuple-element.16, bf16[256,256]{1,0:T(8,128)(2,1)} %param.12), kind=kOutput, calls=%fused_computation.5 | convolution fusion | flops 268959744 | bytes 5373952 | tf_op jit(solution)/shard_map/dot_general | solution.py:245
  87.6 12.8 %all-to-all-done.4 = f32[32,16,256]{2,1,0:T(8,128)S(1)} async-done(((f32[32,16,256]{2,1,0:T(8,128)}), f32[32,16,256]{2,1,0:T(8,128)S(1)}, u32[]{:S(2)}, u32[]{:S(2)}) %all-to-all-start.4) | async-done | bytes 524320 | tf_op jit(solution)/shard_map/all_to_all | solution.py:236
  100.5 0.7 broadcast_in_dim.35
  101.2 2.6 %all-to-all-start.5 = ((bf16[32,16,256]{2,1,0:T(8,128)(2,1)}), bf16[32,16,256]{2,1,0:T(8,128)(2,1)S(1)}, u32[]{:S(2)}, u32[]{:S(2)}) async-start(bf16[32,16,256]{2,1,0:T(8,128)(2,1)} %broadcast_in_dim.35), calls=%async_computation.5 | async-start | bytes 524288 | tf_op jit(solution)/shard_map/all_to_all | solution.py:240
  103.8 0.0 copy-start.1
  103.8 0.5 convolution_bitcast_fusion
  104.3 1.1 copy-done.1
  105.4 2.3 %fusion.2 = bf16[2048,256]{1,0:T(8,128)(2,1)} fusion(f32[2048,256]{1,0:T(8,128)S(1)} %convolution_bitcast_fusion, f32[2048,256]{1,0:T(8,128)S(1)} %copy-done.1, bf16[512,256]{1,0:T(8,128)(2,1)S(1)} %bitcast.26, s32[512]{0:T(512)S(1)} %eq.22, pred[512]{0:T(512)(128)(4,1)S(1)} %lt.20), kind=kOutput, calls=%fused_computation.6 | convolution fusion | flops 541589504 | bytes 5507584 | tf_op jit(solution)/shard_map/dot_general | solution.py:246
  107.7 6.5 %all-to-all-done.5 = bf16[32,16,256]{2,1,0:T(8,128)(2,1)S(1)} async-done(((bf16[32,16,256]{2,1,0:T(8,128)(2,1)}), bf16[32,16,256]{2,1,0:T(8,128)(2,1)S(1)}, u32[]{:S(2)}, u32[]{:S(2)}) %all-to-all-start.5) | async-done | bytes 262176 | tf_op jit(solution)/shard_map/all_to_all | solution.py:240
  114.2 0.8 fusion.26
  (2 shorter events, 0.1 us)
Async XLA Ops:
  2.9 13.1 %all-to-all-start.1 = ((bf16[8,32,256]{2,1,0:T(8,128)(2,1)}), bf16[8,32,256]{2,1,0:T(8,128)(2,1)S(1)}, u32[]{:S(2)}, u32[]{:S(2)}) async-start(bf16[8,32,256]{2,1,0:T(8,128)(2,1)} %broadcast_in_dim.20), calls=%async_computation.1 | async-start | bytes 262144 | tf_op jit(solution)/shard_map/all_to_all | solution.py:192
  16.0 14.1 %copy-start.3 = (bf16[8,32,256]{2,1,0:T(8,128)(2,1)}, bf16[8,32,256]{2,1,0:T(8,128)(2,1)S(1)}, u32[]{:S(2)}) copy-start(bf16[8,32,256]{2,1,0:T(8,128)(2,1)S(1)} %all-to-all-done.1) | copy-start | bytes 393220
  16.0 14.1 %all-to-all-start = ((bf16[32,16,256]{2,1,0:T(8,128)(2,1)}), bf16[32,16,256]{2,1,0:T(8,128)(2,1)S(1)}, u32[]{:S(2)}, u32[]{:S(2)}) async-start(bf16[32,16,256]{2,1,0:T(8,128)(2,1)} %bitcast.1), calls=%async_computation | async-start | bytes 524288 | tf_op jit(solution)/shard_map/all_to_all | solution.py:200
  30.0 0.7 copy-start.2
  30.7 11.2 %copy-start.4 = (bf16[256,256]{1,0:T(8,128)(2,1)S(1)}, bf16[256,256]{1,0:T(8,128)(2,1)}, u32[]{:S(2)}) copy-start(bf16[256,256]{1,0:T(8,128)(2,1)} %param.13) | copy-start | bytes 393220
  30.7 11.2 %copy-start.5 = (bf16[256,256]{1,0:T(8,128)(2,1)S(1)}, bf16[256,256]{1,0:T(8,128)(2,1)}, u32[]{:S(2)}) copy-start(bf16[256,256]{1,0:T(8,128)(2,1)} %param.12) | copy-start | bytes 393220
  30.7 11.2 %copy-start.7 = (bf16[2048,256]{1,0:T(8,128)(2,1)S(1)}, bf16[2048,256]{1,0:T(8,128)(2,1)}, u32[]{:S(2)}) copy-start(bf16[2048,256]{1,0:T(8,128)(2,1)} %param.14) | copy-start | bytes 3145732
  47.2 23.9 %copy-start = (bf16[2048,512]{1,0:T(8,128)(2,1)S(1)}, bf16[2048,512]{1,0:T(8,128)(2,1)}, u32[]{:S(2)}) copy-start(bf16[2048,512]{1,0:T(8,128)(2,1)} %shard_map.138) | copy-start | bytes 6291460
  68.5 13.0 %all-to-all-start.2 = ((bf16[32,16,256]{2,1,0:T(8,128)(2,1)}), bf16[32,16,256]{2,1,0:T(8,128)(2,1)S(1)}, u32[]{:S(2)}, u32[]{:S(2)}) async-start(bf16[32,16,256]{2,1,0:T(8,128)(2,1)} %bitcast.27), calls=%async_computation.2 | async-start | bytes 524288 | tf_op jit(solution)/shard_map/all_to_all | solution.py:224
  71.1 13.0 %copy-start.6 = (s32[32]{0:T(128)S(1)}, s32[32]{0:T(128)}, u32[]{:S(2)}) copy-start(s32[32]{0:T(128)} %param.15) | copy-start | bytes 388
  81.4 19.0 %all-to-all-start.4 = ((f32[32,16,256]{2,1,0:T(8,128)}), f32[32,16,256]{2,1,0:T(8,128)S(1)}, u32[]{:S(2)}, u32[]{:S(2)}) async-start(f32[32,16,256]{2,1,0:T(8,128)} %bitcast.23), calls=%async_computation.4 | async-start | bytes 1048576 | tf_op jit(solution)/shard_map/all_to_all | solution.py:236
  101.2 13.0 %all-to-all-start.5 = ((bf16[32,16,256]{2,1,0:T(8,128)(2,1)}), bf16[32,16,256]{2,1,0:T(8,128)(2,1)S(1)}, u32[]{:S(2)}, u32[]{:S(2)}) async-start(bf16[32,16,256]{2,1,0:T(8,128)(2,1)} %broadcast_in_dim.35), calls=%async_computation.5 | async-start | bytes 524288 | tf_op jit(solution)/shard_map/all_to_all | solution.py:240
  103.8 1.6 %copy-start.1 = (f32[2048,256]{1,0:T(8,128)S(1)}, f32[2048,256]{1,0:T(8,128)}, u32[]{:S(2)}) copy-start(f32[2048,256]{1,0:T(8,128)} %convolution_add_fusion.1) | copy-start | bytes 6291460

commit v15 on v14

--- a/solution.py
+++ b/solution.py
@@ -193,8 +193,8 @@
     hub_table = hub_table.reshape(group * hubs_dev, width)
 
     live = lax.broadcasted_iota(jnp.int32, (peers, slots), 1) < send_count[0][:, None]
-    send_pick = one_hot_rows(send_rows[0].reshape(-1), rows)
-    send_pick = jnp.where(live.reshape(-1, 1), send_pick, jnp.zeros((), jnp.bfloat16))
+    send_index = jnp.where(live, send_rows[0], jnp.int32(-1))
+    send_pick = one_hot_rows(send_index.reshape(-1), rows)
     outgoing = jnp.dot(send_pick, feats, preferred_element_type=jnp.float32).astype(jnp.bfloat16)
     outgoing = outgoing.reshape(peers, slots, width)
     incoming = lax.all_to_all(outgoing, ("dom", "dev"), split_axis=0, concat_axis=0, tiled=True)

time: 116 us -> 117 us (level)
  other arithmetic: 0.87 us -> 2.58 us
    dot_general x1, matrix products: 3.46 us -> 2.13 us  [body(): lax.dot_general(dpre, w_self, contract_cols, preferred_element_type=jnp.f...]
    unnamed x17 -> x15, local copies, waits for them, and re-layouts: 2.6 us -> 1.5 us
where the time goes in v15:
time: 117 us
  waiting for transfers between devices  40.8 us (35%)
  Pallas kernels  22.4 us (19%)
  starting transfers between devices  18.6 us (16%)
  matrix products  17.1 us (15%)
  blocking collectives  10.1 us (9%)
  local copies, waits for them, and re-layouts  3.9 us (3%)
  other arithmetic  2.58 us (2%)
  between operations  1.37 us (1%)
    all_to_all x1, waiting for transfers between devices, body(): lax.all_to_all(parts, ('dom', 'dev'), split_axis=0, concat_axis=0, tiled=...  13.4 us
    pallas_call x1, Pallas kernels, tile_backward(): pl.pallas_call(kernel, out_shape=(jax.ShapeDtypeStruct((rows, width), jnp...  11.2 us
    pallas_call x1, Pallas kernels, tile_aggregate(): pl.pallas_call(kernel, out_shape=jax.ShapeDtypeStruct((rows, 2 * width),...  11.2 us
    all_to_all x1, blocking collectives, body(): lax.all_to_all(hub_part.reshape(group, hubs_dev, width), 'dev', split_axi...  10.1 us
    all_to_all x1, waiting for transfers between devices, body(): lax.all_to_all(outgoing, ('dom', 'dev'), split_axis=0, concat_axis=0, til...  9.74 us
    all_to_all x1, waiting for transfers between devices, body(): lax.all_to_all(returning, ('dom', 'dev'), split_axis=0, concat_axis=0, ti...  8.82 us
    all_to_all x1, waiting for transfers between devices, body(): lax.all_to_all(spread_piece, ('dom', 'dev'), split_axis=0, concat_axis=0,...  6.55 us
    all_to_all x1, starting transfers between devices, body(): lax.all_to_all(hub_out, 'dev', split_axis=0, concat_axis=0, tiled=True)  6.32 us
  transfers between devices with their start and end apart: 5, of which 5 were waited for; matrix products, arithmetic and copies ran while one was open for 11% of the time, Pallas kernels for 0%

profile of v15, /device:TPU:0, one launch (start us, length us, event | category | flops | bytes accessed | tf_op | source)
XLA Modules:
  0.0 116.9 jit_solution(8300482255019570191)
XLA Ops:
  0.6 1.6 %convolution_convert_fusion.1 = bf16[32,256]{1,0:T(8,128)(2,1)S(1)} fusion(bf16[2048,256]{1,0:T(8,128)(2,1)} %feats_ref.1, s32[32]{0:T(128)} %param.15), kind=kOutput, calls=%fused_computation.15 | convolution fusion | flops 33628160 | bytes 1065088 | tf_op jit(solution)/shard_map/dot_general | solution.py:190
  2.2 0.7 broadcast_in_dim.11
  2.9 6.3 %all-to-all-start.1 = ((bf16[8,32,256]{2,1,0:T(8,128)(2,1)}), bf16[8,32,256]{2,1,0:T(8,128)(2,1)S(1)}, u32[]{:S(2)}, u32[]{:S(2)}) async-start(bf16[8,32,256]{2,1,0:T(8,128)(2,1)} %broadcast_in_dim.11), calls=%async_computation.1 | async-start | bytes 262144 | tf_op jit(solution)/shard_map/all_to_all | solution.py:192
  9.2 0.7 iota_compare_fusion.13
  9.9 0.1 lt.20
  10.0 0.8 copy.15
  10.8 0.1 squeeze.3
  10.9 2.8 %fusion.7 = bf16[512,256]{1,0:T(8,128)(2,1)} fusion(bf16[2048,256]{1,0:T(8,128)(2,1)} %feats_ref.1, s32[512]{0:T(512)S(1)} %broadcast_select_fusion), kind=kOutput, calls=%fused_computation.14 | convolution fusion | flops 538050560 | bytes 1312768 | tf_op jit(solution)/shard_map/dot_general | solution.py:198
  13.7 2.3 %all-to-all-done.1 = bf16[8,32,256]{2,1,0:T(8,128)(2,1)S(1)} async-done(((bf16[8,32,256]{2,1,0:T(8,128)(2,1)}), bf16[8,32,256]{2,1,0:T(8,128)(2,1)S(1)}, u32[]{:S(2)}, u32[]{:S(2)}) %all-to-all-start.1) | async-done | bytes 131104 | tf_op jit(solution)/shard_map/all_to_all | solution.py:192
  16.0 0.0 copy-start.2
  16.0 3.8 %all-to-all-start = ((bf16[32,16,256]{2,1,0:T(8,128)(2,1)}), bf16[32,16,256]{2,1,0:T(8,128)(2,1)S(1)}, u32[]{:S(2)}, u32[]{:S(2)}) async-start(bf16[32,16,256]{2,1,0:T(8,128)(2,1)} %bitcast.1), calls=%async_computation | async-start | bytes 524288 | tf_op jit(solution)/shard_map/all_to_all | solution.py:200
  20.4 9.7 %all-to-all-done = bf16[32,16,256]{2,1,0:T(8,128)(2,1)S(1)} async-done(((bf16[32,16,256]{2,1,0:T(8,128)(2,1)}), bf16[32,16,256]{2,1,0:T(8,128)(2,1)S(1)}, u32[]{:S(2)}, u32[]{:S(2)}) %all-to-all-start) | async-done | bytes 262176 | tf_op jit(solution)/shard_map/all_to_all | solution.py:200
  30.1 0.0 copy-start.1
  30.1 0.0 copy-done.2
  30.1 0.7 copy-done.1
  30.8 0.0 copy-start.3
  30.8 0.0 copy-start.4
  30.8 0.0 copy-start.6
  30.8 11.2 %shard_map.138 = bf16[2048,512]{1,0:T(8,128)(2,1)} custom-call(s32[320]{0:T(512)} %src_ref.3, s32[320]{0:T(512)} %dst_ref.3, s32[1]{0:T(128)S(6)} %copy.16.cnt_ref, bf16[320,128,128]{2,1,0:T(8,128)(2,1)} %val_ref.3, bf16[2048,256]{1,0:T(8,128)(2,1)} %feats_ref.1, bf16[512,256]{1,0:T(8,128)(2,1)} %bitcast.25, bf16[256,256]{1,0:T(8,128)(2,1)} %bitcast.26), custom_call_target="tpu_custom_call" | custom-call | tf_op jit(solution)/shard_map/pallas_call | solution.py:73
  42.0 0.0 copy-done.3
  42.0 0.0 copy-done.4
  42.0 0.0 copy-done.6
  42.0 3.8 %multiply_convert_fusion = (bf16[2048,256]{1,0:T(8,128)(2,1)S(1)}, bf16[2048,256]{1,0:T(8,128)(2,1)}) fusion(bf16[2048,256]{1,0:T(8,128)(2,1)S(1)} %copy-done.6, bf16[2048,512]{1,0:T(8,128)(2,1)} %shard_map.138, bf16[256,256]{1,0:T(8,128)(2,1)S(1)} %copy-done.3, bf16[256,256]{1,0:T(8,128)(2,1)S(1)} %copy-done.4), kind=kOutput, calls=%fused_computation.9 | convolution fusion | flops 543686656 | bytes 5505024 | tf_op jit(solution)/shard_map/dot_general | solution.py:208
  45.9 1.4 %convolution_convert_fusion.dagg_ref = bf16[2048,256]{1,0:T(8,128)(2,1)} fusion(bf16[2048,256]{1,0:T(8,128)(2,1)S(1)} %get-tuple-element.16, bf16[256,256]{1,0:T(8,128)(2,1)S(1)} %copy-done.3), kind=kOutput, calls=%fused_computation.8 | convolution fusion | flops 268959744 | bytes 2228224 | tf_op jit(solution)/shard_map/dot_general | solution.py:217
  47.3 0.0 copy-start
  47.3 11.2 %shard_map.139 = (f32[2048,256]{1,0:T(8,128)}, bf16[512,256]{1,0:T(8,128)(2,1)}, bf16[256,256]{1,0:T(8,128)(2,1)}) custom-call(s32[320]{0:T(512)} %src_ref.3, s32[320]{0:T(512)} %dst_ref.3, s32[1]{0:T(128)S(6)} %copy.16.cnt_ref, bf16[320,128,128]{2,1,0:T(8,128)(2,1)} %val_ref.3, bf16[2048,256]{1,0:T(8,128)(2,1)} %convolution_convert_fusion.dagg_ref), custom_call_target="tpu_custom_call" | custom-call | tf_op jit(solution)/shard_map/pallas_call | solution.py:145
  58.5 10.1 %all_to_all.30 = bf16[8,32,256]{2,1,0:T(8,128)(2,1)S(1)} all-to-all(bf16[8,32,256]{2,1,0:T(8,128)(2,1)} %bitcast.30), channel_id=1, replica_groups=mesh['dom'=4,'dev'=8] {'dev'}, dimensions={0} | all-to-all | bytes 262144 | tf_op jit(solution)/shard_map/all_to_all | solution.py:227
  68.6 2.6 %all-to-all-start.2 = ((bf16[32,16,256]{2,1,0:T(8,128)(2,1)}), bf16[32,16,256]{2,1,0:T(8,128)(2,1)S(1)}, u32[]{:S(2)}, u32[]{:S(2)}) async-start(bf16[32,16,256]{2,1,0:T(8,128)(2,1)} %bitcast.27), calls=%async_computation.2 | async-start | bytes 524288 | tf_op jit(solution)/shard_map/all_to_all | solution.py:224
  71.2 0.0 copy-done
  71.2 0.0 copy-start.5
  71.2 1.5 %fusion.17 = f32[512,256]{1,0:T(8,128)} fusion(bf16[2048,512]{1,0:T(8,128)(2,1)S(1)} %copy-done, bf16[2048,256]{1,0:T(8,128)(2,1)S(1)} %get-tuple-element.16), kind=kOutput, calls=%fused_computation.29 | convolution fusion | flops 536870912 | bytes 3670016 | tf_op jit(solution)/shard_map/dot_general | solution.py:214
  72.7 8.8 %all-to-all-done.2 = bf16[32,16,256]{2,1,0:T(8,128)(2,1)S(1)} async-done(((bf16[32,16,256]{2,1,0:T(8,128)(2,1)}), bf16[32,16,256]{2,1,0:T(8,128)(2,1)S(1)}, u32[]{:S(2)}, u32[]{:S(2)}) %all-to-all-start.2) | async-done | bytes 262176 | tf_op jit(solution)/shard_map/all_to_all | solution.py:224
  81.6 3.3 %all-to-all-start.4 = ((f32[32,16,256]{2,1,0:T(8,128)}), f32[32,16,256]{2,1,0:T(8,128)}, u32[]{:S(2)}, u32[]{:S(2)}) async-start(f32[32,16,256]{2,1,0:T(8,128)} %bitcast.23), calls=%async_computation.4 | async-start | bytes 1048576 | tf_op jit(solution)/shard_map/all_to_all | solution.py:236
  84.9 0.0 copy-done.5
  84.9 0.7 fusion.13
  85.7 2.1 %convolution_add_fusion = f32[2048,256]{1,0:T(8,128)S(1)} fusion(f32[2048,256]{1,0:T(8,128)} %get-tuple-element.10, bf16[2048,256]{1,0:T(8,128)(2,1)S(1)} %get-tuple-element.16, bf16[256,256]{1,0:T(8,128)(2,1)} %param.12), kind=kOutput, calls=%fused_computation.6 | convolution fusion | flops 268959744 | bytes 5373952 | tf_op jit(solution)/shard_map/dot_general | solution.py:245
  87.8 13.4 %all-to-all-done.4 = f32[32,16,256]{2,1,0:T(8,128)} async-done(((f32[32,16,256]{2,1,0:T(8,128)}), f32[32,16,256]{2,1,0:T(8,128)}, u32[]{:S(2)}, u32[]{:S(2)}) %all-to-all-start.4) | async-done | bytes 524320 | tf_op jit(solution)/shard_map/all_to_all | solution.py:236
  101.2 1.1 reduce_sum.9
  102.3 0.7 broadcast_in_dim.13
  103.0 2.6 %all-to-all-start.5 = ((bf16[32,16,256]{2,1,0:T(8,128)(2,1)}), bf16[32,16,256]{2,1,0:T(8,128)(2,1)S(1)}, u32[]{:S(2)}, u32[]{:S(2)}) async-start(bf16[32,16,256]{2,1,0:T(8,128)(2,1)} %broadcast_in_dim.13), calls=%async_computation.5 | async-start | bytes 524288 | tf_op jit(solution)/shard_map/all_to_all | solution.py:240
  105.6 1.4 %convolution_bitcast_fusion = f32[2048,256]{1,0:T(8,128)S(1)} fusion(bf16[8,32,256]{2,1,0:T(8,128)(2,1)S(1)} %all_to_all.30, bf16[32,2048]{1,0:T(8,128)(2,1)} %fusion.13), kind=kOutput, calls=%fused_computation.5 | convolution fusion | flops 268435456 | bytes 2359296 | tf_op jit(solution)/shard_map/dot_general | solution.py:249
  107.0 2.4 %fusion.4 = bf16[2048,256]{1,0:T(8,128)(2,1)} fusion(f32[2048,256]{1,0:T(8,128)S(1)} %convolution_bitcast_fusion, f32[2048,256]{1,0:T(8,128)S(1)} %convolution_add_fusion, bf16[512,256]{1,0:T(8,128)(2,1)S(1)} %bitcast.24, s32[512]{0:T(512)S(1)} %broadcast_select_fusion), kind=kOutput, calls=%fused_computation.7 | convolution fusion | flops 539492352 | bytes 5507072 | tf_op jit(solution)/shard_map/dot_general | solution.py:246
  109.5 6.5 %all-to-all-done.5 = bf16[32,16,256]{2,1,0:T(8,128)(2,1)S(1)} async-done(((bf16[32,16,256]{2,1,0:T(8,128)(2,1)}), bf16[32,16,256]{2,1,0:T(8,128)(2,1)S(1)}, u32[]{:S(2)}, u32[]{:S(2)}) %all-to-all-start.5) | async-done | bytes 262176 | tf_op jit(solution)/shard_map/all_to_all | solution.py:240
  116.0 0.8 fusion.16
  (2 shorter events, 0.0 us)
Async XLA Ops:
  2.9 13.1 %all-to-all-start.1 = ((bf16[8,32,256]{2,1,0:T(8,128)(2,1)}), bf16[8,32,256]{2,1,0:T(8,128)(2,1)S(1)}, u32[]{:S(2)}, u32[]{:S(2)}) async-start(bf16[8,32,256]{2,1,0:T(8,128)(2,1)} %broadcast_in_dim.11), calls=%async_computation.1 | async-start | bytes 262144 | tf_op jit(solution)/shard_map/all_to_all | solution.py:192
  16.0 14.2 %copy-start.2 = (bf16[8,32,256]{2,1,0:T(8,128)(2,1)}, bf16[8,32,256]{2,1,0:T(8,128)(2,1)S(1)}, u32[]{:S(2)}) copy-start(bf16[8,32,256]{2,1,0:T(8,128)(2,1)S(1)} %all-to-all-done.1) | copy-start | bytes 393220
  16.0 14.2 %all-to-all-start = ((bf16[32,16,256]{2,1,0:T(8,128)(2,1)}), bf16[32,16,256]{2,1,0:T(8,128)(2,1)S(1)}, u32[]{:S(2)}, u32[]{:S(2)}) async-start(bf16[32,16,256]{2,1,0:T(8,128)(2,1)} %bitcast.1), calls=%async_computation | async-start | bytes 524288 | tf_op jit(solution)/shard_map/all_to_all | solution.py:200
  30.1 0.7 copy-start.1
  30.8 11.2 %copy-start.3 = (bf16[256,256]{1,0:T(8,128)(2,1)S(1)}, bf16[256,256]{1,0:T(8,128)(2,1)}, u32[]{:S(2)}) copy-start(bf16[256,256]{1,0:T(8,128)(2,1)} %param.13) | copy-start | bytes 393220
  30.8 11.2 %copy-start.4 = (bf16[256,256]{1,0:T(8,128)(2,1)S(1)}, bf16[256,256]{1,0:T(8,128)(2,1)}, u32[]{:S(2)}) copy-start(bf16[256,256]{1,0:T(8,128)(2,1)} %param.12) | copy-start | bytes 393220
  30.8 11.2 %copy-start.6 = (bf16[2048,256]{1,0:T(8,128)(2,1)S(1)}, bf16[2048,256]{1,0:T(8,128)(2,1)}, u32[]{:S(2)}) copy-start(bf16[2048,256]{1,0:T(8,128)(2,1)} %param.14) | copy-start | bytes 3145732
  47.3 23.9 %copy-start = (bf16[2048,512]{1,0:T(8,128)(2,1)S(1)}, bf16[2048,512]{1,0:T(8,128)(2,1)}, u32[]{:S(2)}) copy-start(bf16[2048,512]{1,0:T(8,128)(2,1)} %shard_map.138) | copy-start | bytes 6291460
  68.6 13.0 %all-to-all-start.2 = ((bf16[32,16,256]{2,1,0:T(8,128)(2,1)}), bf16[32,16,256]{2,1,0:T(8,128)(2,1)S(1)}, u32[]{:S(2)}, u32[]{:S(2)}) async-start(bf16[32,16,256]{2,1,0:T(8,128)(2,1)} %bitcast.27), calls=%async_computation.2 | async-start | bytes 524288 | tf_op jit(solution)/shard_map/all_to_all | solution.py:224
  71.2 13.7 %copy-start.5 = (s32[32]{0:T(128)S(1)}, s32[32]{0:T(128)}, u32[]{:S(2)}) copy-start(s32[32]{0:T(128)} %param.15) | copy-start | bytes 388
  81.6 19.7 %all-to-all-start.4 = ((f32[32,16,256]{2,1,0:T(8,128)}), f32[32,16,256]{2,1,0:T(8,128)}, u32[]{:S(2)}, u32[]{:S(2)}) async-start(f32[32,16,256]{2,1,0:T(8,128)} %bitcast.23), calls=%async_computation.4 | async-start | bytes 1048576 | tf_op jit(solution)/shard_map/all_to_all | solution.py:236
  103.0 13.0 %all-to-all-start.5 = ((bf16[32,16,256]{2,1,0:T(8,128)(2,1)}), bf16[32,16,256]{2,1,0:T(8,128)(2,1)S(1)}, u32[]{:S(2)}, u32[]{:S(2)}) async-start(bf16[32,16,256]{2,1,0:T(8,128)(2,1)} %broadcast_in_dim.13), calls=%async_computation.5 | async-start | bytes 524288 | tf_op jit(solution)/shard_map/all_to_all | solution.py:240
